TPU v7x, 32 devices: a whole 2x2x4 slice. The times are simulated.
32 devices in a mesh: well: 4 (over y, x), tile: 8 (over z, core).
Axes of the slice: x: 2, y: 2, z: 4, core: 2. Of those that a mesh axis runs over, the one named last changes fastest.
Arguments:
- prior_state: float32 [3, 200, 8192], P(None, None, 'tile'), may hold values from -6 to 6
- pred_data: float32 [4096, 200], P(('well', 'tile')), may hold values from -6 to 6
- obs_pert: float32 [4096, 200], P(('well', 'tile')), may hold values from -12 to 12
- obs_std: float32 [4096], P(('well', 'tile')), may hold values from 0.5 to 2
- loc_mask: int32 [8, 32], P('tile', 'well'), may hold values from 0 to 1, as said below
- taper_level: int32 [8, 32], P('tile', 'well'), may hold values from 1 to 4
Outputs:
- analysis: float32 [3, 200, 8192], P(None, 'well', 'tile')
Inputs may be any that keep to these rules, and one draw needn't show every extreme that they name: `loc_mask`: each tile is localized to a set of data blocks whose size varies strongly from tile to tile; some tile is localized to most blocks.
All inputs are finite; a program needn't handle non-finite values.
Results may differ from a plain program's by a relative error of at most 0.0003.
Values sent between devices are 32-bit elements; how exact they have to be, the bound alone decides.
No kernel may reach another device: no remote copies, remote signals or barrier semaphores. Data moves between devices by JAX's collectives and lax.ppermute only.
A program may use at most 64 MiB of HBM per device.

v0:
```python
import jax
import jax.numpy as jnp
from jax import lax
from jax.sharding import PartitionSpec as P

BLOCK = 128


def chol_apply(system, right):
    factor = jnp.linalg.cholesky(system)
    middle = lax.linalg.triangular_solve(
        factor, right, left_side=True, lower=True, transpose_a=False
    )
    return lax.linalg.triangular_solve(factor, middle, left_side=True, lower=True, transpose_a=True)


def prepare(pred_rows, obs_rows, std_rows, norm_factor):
    data_anom = (pred_rows - jnp.mean(pred_rows, axis=1, keepdims=True)) * norm_factor
    innov = obs_rows - pred_rows
    row_weight = 1.0 / (4.0 * std_rows * std_rows)
    scaled = row_weight[:, None] * data_anom
    return (data_anom, innov, row_weight, scaled)


def shards(prior_state, pred_data, obs_pert, obs_std, loc_mask, taper_level):
    highest = lax.Precision.HIGHEST
    members = pred_data.shape[1]
    norm_factor = 1.0 / jnp.sqrt(jnp.float32(members - 1))
    data_anom, innov, row_weight, scaled = prepare(pred_data, obs_pert, obs_std, norm_factor)
    gram_matrix, cross_matrix = lax.psum(
        (
            jnp.dot(data_anom.T, scaled, precision=highest),
            jnp.dot(scaled.T, innov, precision=highest),
        ),
        ("well", "tile"),
    )
    system = jnp.eye(members, dtype=jnp.float32) + gram_matrix
    solved = chol_apply(system, cross_matrix)
    gain_rows = row_weight[:, None] * innov - jnp.dot(scaled, solved, precision=highest)
    group_anom, group_gain = (
        lax.all_gather(data_anom, "tile", axis=0, tiled=True),
        lax.all_gather(gain_rows, "tile", axis=0, tiled=True),
    )
    taper_row = loc_mask[0].astype(jnp.float32) * taper_level[0].astype(jnp.float32) / 4.0
    state_anom = (prior_state - jnp.mean(prior_state, axis=1, keepdims=True)) * norm_factor
    own_count = members // lax.axis_size("well")
    own_start = lax.axis_index("well") * own_count
    row_taper = jnp.repeat(taper_row, BLOCK)
    space = jnp.dot((group_anom * row_taper[:, None]).T, group_gain, precision=highest)
    space_mine = lax.psum_scatter(space, "well", scatter_dimension=1, tiled=True)
    increment = jnp.einsum("vnc,nm->vmc", state_anom, space_mine, precision=highest)
    prior_mine = lax.dynamic_slice_in_dim(prior_state, own_start, own_count, 1)
    return prior_mine + increment


def solution(mesh):
    return jax.shard_map(
        shards,
        mesh=mesh,
        in_specs=(
            P(None, None, "tile"),
            P(("well", "tile"), None),
            P(("well", "tile"), None),
            P(("well", "tile")),
            P("tile", "well"),
            P("tile", "well"),
        ),
        out_specs=P(None, "well", "tile"),
        check_vma=False,
    )
```

profile of v0, /device:TPU:0, one launch (start us, length us, event | category | flops | bytes accessed | tf_op | source)
XLA Modules:
  0.0 277.9 jit_solution(14750965140446197229)
XLA Ops:
  6.5 1.1 reduce_sum.18
  7.6 1.2 broadcast_multiply_fusion.1
  8.8 2.0 fusion.22
  10.8 2.0 fusion.21
  12.9 0.9 subtract_multiply_fusion.1
  13.8 17.5 %all_gather.6 = f32[1024,200]{0,1:T(8,128)S(1)} all-gather(f32[128,200]{0,1:T(8,128)S(1)} %subtract_multiply_fusion.1), channel_id=1, replica_groups=mesh['well'=4,'tile'=8] {'tile'}, dimensions={0}, use_global_device_ids=true | all-gather | bytes 921600 | tf_op jit(solution)/shard_map/all_gather | solution.py:41
  32.1 110.1 %all-reduce.8.cloned.1.call-done = (f32[200,200]{1,0:T(8,128)}, f32[200,200]{0,1:T(8,128)}) async-done(((f32[200,200]{1,0:T(8,128)}, f32[200,200]{0,1:T(8,128)}), (f32[200,200]{1,0:T(8,128)}, f32[200,200]{0,1:T(8,128)})) %all-reduce.8.cloned.1.call-update) | async-done | bytes 320016 | tf_op jit(solution)/shard_map/psum | solution.py:30
  142.2 1.7 convert_add_fusion
  143.9 1.7 copy.10
  145.6 1.1 fusion.18
  148.0 13.2 %cholesky.51 = f32[128,128]{1,0:T(8,128)} custom-call(f32[128,128]{1,0:T(8,128)} %cholesky.124), custom_call_target="Cholesky" | custom-call | tf_op jit(solution)/shard_map/jit(cholesky)/cholesky | solution.py:10
  161.1 2.0 select_reduce_fusion
  163.2 1.5 cholesky.119
  164.7 11.3 %custom-call.16 = f32[1,128,128]{1,2,0:T(8,128)} custom-call(f32[1,128,128]{2,1,0:T(8,128)} %get-tuple-element.30), custom_call_target="InvertDiagBlocksLowerTriangular" | custom-call | tf_op jit(solution)/shard_map/jit(cholesky)/cholesky | solution.py:10
  176.0 1.7 constant_dynamic-update-slice_fusion.1
  177.7 1.6 convolution_subtract_fusion.3
  179.3 8.0 %cholesky.110 = f32[72,72]{1,0:T(8,128)} custom-call(f32[72,72]{1,0:T(8,128)} %convolution_subtract_fusion.3), custom_call_target="Cholesky" | custom-call | tf_op jit(solution)/shard_map/jit(cholesky)/cholesky | solution.py:10
  187.2 1.4 select_reduce_fusion.1
  189.2 1.3 compare_reduce_fusion.1
  191.8 1.0 select_select_fusion
  194.2 21.1 %custom-call.17 = f32[2,128,128]{1,2,0:T(8,128)} custom-call(f32[2,128,128]{2,1,0:T(8,128)} %pad_maximum_fusion), custom_call_target="InvertDiagBlocksLowerTriangular" | custom-call | tf_op jit(solution)/shard_map/triangular_solve | solution.py:14
  215.3 1.4 fusion.19
  216.6 1.2 convolution_subtract_fusion.2
  217.9 1.0 fusion.36
  218.9 1.0 fusion.35
  219.9 1.1 convolution_subtract_fusion
  221.0 1.2 fusion.26
  222.3 1.2 convolution_subtract_fusion.1
  223.5 17.3 %all_gather.7 = f32[1024,200]{0,1:T(8,128)S(1)} all-gather(f32[128,200]{0,1:T(8,128)S(1)} %convolution_subtract_fusion.1), channel_id=1, replica_groups=mesh['well'=4,'tile'=8] {'tile'}, dimensions={0}, use_global_device_ids=true | all-gather | bytes 921600 | tf_op jit(solution)/shard_map/all_gather | solution.py:42
  241.7 22.3 %fusion = f32[200,64]{0,1:T(8,128)S(1)} fusion(f32[200,200]{0,1:T(8,128)S(1)} %fusion.12), kind=kCustom, calls=%all-reduce-scatter | all-reduce-scatter fusion | flops 51201 | bytes 211712
  264.1 2.5 collective-permute-start
  268.5 2.6 fusion.7
  (39 shorter events, 6.3 us)
Async XLA Ops:
  6.5 24.7 %copy-start.9 = (s32[1,8]{1,0:T(1,128)S(1)}, s32[1,8]{1,0:T(1,128)}, u32[]{:S(2)}) copy-start(s32[1,8]{1,0:T(1,128)} %param.10) | copy-start | bytes 100
  6.5 24.7 %copy-start.8 = (s32[1,8]{1,0:T(1,128)S(1)}, s32[1,8]{1,0:T(1,128)}, u32[]{:S(2)}) copy-start(s32[1,8]{1,0:T(1,128)} %param.11) | copy-start | bytes 100
  6.5 24.8 %copy-start = (f32[3,200,1024]{2,1,0:T(8,128)S(1)}, f32[3,200,1024]{2,1,0:T(8,128)}, u32[]{:S(2)}) copy-start(f32[3,200,1024]{2,1,0:T(8,128)} %param.6) | copy-start | bytes 7372804
  6.5 135.7 %all-reduce.8.cloned.1.call-start = ((), (), s32[]{:S(2)}) async-start(), calls=%async_computation | async-start | bytes 819200 | tf_op jit(solution)/shard_map/psum | solution.py:30
  8.8 2.0 copy-start.6
  142.2 80.0 %copy-start.1 = (f32[128,200]{0,1:T(8,128)S(1)}, f32[128,200]{0,1:T(8,128)}, u32[]{:S(2)}) copy-start(f32[128,200]{0,1:T(8,128)} %param.7) | copy-start | bytes 307204
  142.2 80.0 %copy-start.4 = (f32[128,200]{0,1:T(8,128)S(1)}, f32[128,200]{0,1:T(8,128)}, u32[]{:S(2)}) copy-start(f32[128,200]{0,1:T(8,128)} %param.8) | copy-start | bytes 307204
  146.7 0.7 copy-start.3
  192.7 0.7 copy-start.2
  216.6 49.9 %copy-start.5 = (f32[3,1024]{1,0:T(4,128)S(1)}, f32[3,1024]{1,0:T(4,128)}, u32[]{:S(2)}) copy-start(f32[3,1024]{1,0:T(4,128)} %reduce_sum.19) | copy-start | bytes 36868
  216.6 49.9 %copy-start.7 = (u32[32]{0:T(128)S(1)}, u32[32]{0:T(128)}, u32[]{:S(2)}) copy-start(u32[32]{0:T(128)} %constant.155) | copy-start | bytes 388
  264.1 4.2 %collective-permute-start = (f32[200,42]{0,1:T(8,128)S(1)}, f32[200,42]{0,1:T(8,128)S(1)}, u32[]{:S(2)}, u32[]{:S(2)}) collective-permute-start(f32[200,42]{0,1:T(8,128)S(1)} %slice.74), channel_id=1, source_target_pairs={{0,8},{8,16},{16,24},{1,9},{9,17},{17,25},{2,10},{10,18},{18,26},{... | collective-permute-start | bytes 100808
Sparse Core Ops, SparseCore 0:
  13.0 129.1 all-reduce.7
where the time goes:
time: 279 us; the launch traced here: 278 us
  waiting for transfers between devices  111 us (40%)
  other arithmetic  67.3 us (24%)
  blocking collectives  57.1 us (20%)
  matrix products  19 us (7%)
  between operations  15.4 us (6%)
  local copies, waits for them, and re-layouts  6.11 us (2%)
    psum x1, waiting for transfers between devices, shards(): lax.psum((jnp.dot(data_anom.T, scaled, precision=highest), jnp.dot(scaled...  110 us
    another operation x7, other arithmetic, chol_apply(): factor = jnp.linalg.cholesky(system)  37.8 us
    another operation x6, other arithmetic, chol_apply(): lax.linalg.triangular_solve(factor, middle, left_side=True, lower=True, t...  22.8 us
    unnamed x1, blocking collectives  22.3 us
    all_gather x1, blocking collectives, shards(): lax.all_gather(data_anom, 'tile', axis=0, tiled=True)  17.5 us
    all_gather x1, blocking collectives, shards(): lax.all_gather(gain_rows, 'tile', axis=0, tiled=True)  17.3 us
  transfers between devices with their start and end apart: 2, of which 2 were waited for; matrix products, arithmetic and copies ran while one was open for 1% of the time, Pallas kernels for 0%

commit v1 on v0

--- a/solution.py
+++ b/solution.py
@@ -22,33 +22,103 @@
     return (data_anom, innov, row_weight, scaled)
 
 
+def bit_of(axis, k):
+    return (lax.axis_index(axis) // k) % 2
+
+
+def swap(x, axis, k):
+    size = lax.axis_size(axis)
+    return lax.ppermute(x, axis, [(i, i ^ k) for i in range(size)])
+
+
+def axis_bits(axis):
+    size = lax.axis_size(axis)
+    out, k = [], 1
+    while k < size:
+        out.append((axis, k))
+        k *= 2
+    return out
+
+
+def all_sum(x, steps):
+    halved = []
+    for axis, k in steps:
+        rows = x.shape[0]
+        if rows % 2 == 0:
+            half = rows // 2
+            hi = bit_of(axis, k) == 1
+            keep = jnp.where(hi, x[half:], x[:half])
+            send = jnp.where(hi, x[:half], x[half:])
+            x = keep + swap(send, axis, k)
+            halved.append((axis, k))
+        else:
+            x = x + swap(x, axis, k)
+    for axis, k in reversed(halved):
+        other = swap(x, axis, k)
+        hi = bit_of(axis, k) == 1
+        x = jnp.where(hi, jnp.concatenate([other, x], 0), jnp.concatenate([x, other], 0))
+    return x
+
+
+def well_reduce(full, split):
+    for axis, k in reversed(axis_bits("well")):
+        rows = split.shape[0]
+        half = rows // 2
+        hi = bit_of(axis, k) == 1
+        keep = jnp.where(hi, split[half:], split[:half])
+        send = jnp.where(hi, split[:half], split[half:])
+        got = swap(jnp.concatenate([full, send], 0), axis, k)
+        full = full + got[: full.shape[0]]
+        split = keep + got[full.shape[0]:]
+    return full, split
+
+
 def shards(prior_state, pred_data, obs_pert, obs_std, loc_mask, taper_level):
     highest = lax.Precision.HIGHEST
     members = pred_data.shape[1]
     norm_factor = 1.0 / jnp.sqrt(jnp.float32(members - 1))
     data_anom, innov, row_weight, scaled = prepare(pred_data, obs_pert, obs_std, norm_factor)
-    gram_matrix, cross_matrix = lax.psum(
-        (
+
+    stacked = jnp.concatenate(
+        [
             jnp.dot(data_anom.T, scaled, precision=highest),
             jnp.dot(scaled.T, innov, precision=highest),
-        ),
-        ("well", "tile"),
+        ],
+        0,
     )
+    order = axis_bits("tile")[:1] + axis_bits("well") + axis_bits("tile")[1:]
+    stacked = all_sum(stacked, order)
+    gram_matrix, cross_matrix = stacked[:members], stacked[members:]
+    own_count = members // lax.axis_size("well")
+    own_start = lax.axis_index("well") * own_count
+    cross_mine = lax.dynamic_slice_in_dim(cross_matrix, own_start, own_count, 1)
     system = jnp.eye(members, dtype=jnp.float32) + gram_matrix
-    solved = chol_apply(system, cross_matrix)
-    gain_rows = row_weight[:, None] * innov - jnp.dot(scaled, solved, precision=highest)
-    group_anom, group_gain = (
-        lax.all_gather(data_anom, "tile", axis=0, tiled=True),
-        lax.all_gather(gain_rows, "tile", axis=0, tiled=True),
+    solved_mine = chol_apply(system, cross_mine)
+
+    packed = jnp.concatenate([data_anom, innov, row_weight[:, None]], 1)
+    group = lax.all_gather(packed, "tile", axis=0, tiled=True)
+    group_anom, group_innov, group_weight = (
+        group[:, :members],
+        group[:, members : 2 * members],
+        group[:, 2 * members],
     )
     taper_row = loc_mask[0].astype(jnp.float32) * taper_level[0].astype(jnp.float32) / 4.0
+    row_taper = jnp.repeat(taper_row, BLOCK)
+    tapered = (row_taper * group_weight)[:, None] * group_anom
+    both = lax.dot_general(
+        jnp.concatenate([group_anom, group_innov], 1),
+        tapered,
+        (((0,), (0,)), ((), ())),
+        precision=highest,
+    )
+    taper_gram, taper_cross_t = both[:members], both[members:]
+    taper_gram, cross_t_mine = well_reduce(taper_gram, taper_cross_t)
+
+    space_t = cross_t_mine - lax.dot_general(
+        solved_mine, taper_gram, (((0,), (1,)), ((), ())), precision=highest
+    )
     state_anom = (prior_state - jnp.mean(prior_state, axis=1, keepdims=True)) * norm_factor
-    own_count = members // lax.axis_size("well")
-    own_start = lax.axis_index("well") * own_count
-    row_taper = jnp.repeat(taper_row, BLOCK)
-    space = jnp.dot((group_anom * row_taper[:, None]).T, group_gain, precision=highest)
-    space_mine = lax.psum_scatter(space, "well", scatter_dimension=1, tiled=True)
-    increment = jnp.einsum("vnc,nm->vmc", state_anom, space_mine, precision=highest)
+    increment = jnp.einsum("vnc,mn->vmc", state_anom, space_t, precision=highest)
     prior_mine = lax.dynamic_slice_in_dim(prior_state, own_start, own_count, 1)
     return prior_mine + increment
 

time: 279 us -> 140 us (0.50)
  waiting for transfers between devices: 111 us -> 34.9 us
  blocking collectives: 57.1 us -> 0 us
  starting transfers between devices: 2.47 us -> 17.3 us
  other arithmetic: 67.3 us -> 58 us
  matrix products: 19 us -> 13.3 us
  local copies, waits for them, and re-layouts: 6.11 us -> 0.97 us
    psum x1 -> x0, waiting for transfers between devices: 110 us -> none  [shards(): lax.psum((jnp.dot(data_anom.T, scaled, precision=highest), jnp.dot(scaled...]
    ppermute x0 -> x11, waiting for transfers between devices: none -> 34.9 us  [swap(): return lax.ppermute(x, axis, [(i, i ^ k) for i in range(size)])]
    all_gather x2 -> x0, blocking collectives: 34.8 us -> none  [the longest x1 17.5 us: shards(): lax.all_gather(data_anom, 'tile', axis=0, tiled=True)]
    unnamed x1 -> x0, blocking collectives: 22.3 us -> none
    ppermute x0 -> x11, starting transfers between devices: none -> 17.3 us  [swap(): return lax.ppermute(x, axis, [(i, i ^ k) for i in range(size)])]
    another operation x7, other arithmetic: 37.8 us -> 29.6 us  [chol_apply(): factor = jnp.linalg.cholesky(system)]
    another operation x2, matrix products: 3.27 us -> 0.42 us  [chol_apply(): factor = jnp.linalg.cholesky(system)]
    another operation x6, other arithmetic: 22.8 us -> 20 us  [chol_apply(): lax.linalg.triangular_solve(factor, middle, left_side=True, lower=True, t...]
  transfers between devices with their start and end apart: 2 -> 12, of which waited for: 2 -> 11; matrix products, arithmetic and copies ran while one was open for 1% -> 40% of each run, Pallas kernels for 0% -> 0%
where the time goes in v1:
time: 140 us
  other arithmetic  58 us (41%)
  waiting for transfers between devices  34.9 us (25%)
  starting transfers between devices  17.3 us (12%)
  between operations  15.2 us (11%)
  matrix products  13.3 us (10%)
    ppermute x11, waiting for transfers between devices, swap(): return lax.ppermute(x, axis, [(i, i ^ k) for i in range(size)])  34.9 us
    another operation x7, other arithmetic, chol_apply(): factor = jnp.linalg.cholesky(system)  29.6 us
    another operation x6, other arithmetic, chol_apply(): lax.linalg.triangular_solve(factor, middle, left_side=True, lower=True, t...  20 us
    ppermute x11, starting transfers between devices, swap(): return lax.ppermute(x, axis, [(i, i ^ k) for i in range(size)])  17.3 us
    dot_general x1, matrix products, shards(): lax.dot_general(jnp.concatenate([group_anom, group_innov], 1), tapered, (...  3.38 us
  transfers between devices with their start and end apart: 12, of which 11 were waited for; matrix products, arithmetic and copies ran while one was open for 40% of the time, Pallas kernels for 0%

profile of v1, /device:TPU:0, one launch (start us, length us, event | category | flops | bytes accessed | tf_op | source)
XLA Modules:
  0.0 139.7 jit_solution(7078163577064638061)
XLA Ops:
  6.5 0.9 reduce_sum.18
  8.1 1.0 subtract_multiply_fusion
  9.1 1.2 fusion.27
  10.4 1.5 %broadcast_select_fusion = (f32[200,200]{0,1:T(8,128)S(1)}, f32[200,200]{0,1:T(8,128)S(1)}) fusion(f32[200,200]{0,1:T(8,128)S(1)} %fusion.27, pred[]{:T(512)S(6)} %eq.35, f32[128,200]{0,1:T(8,128)} %param.7, f32[128]{0:T(128)S(1)} %get-tuple-element.25, f32[128]{0:T(128)S(1)} %get-tuple-element.39), kind=kOutput, calls=%fused_computation.42 | convolution fusion | flops 61582400 | bytes 583425 | tf_op jit(solution)/shard_map/dot_general | solution.py:84
  12.3 1.2 collective-permute-done.2
  13.6 1.0 select_add_fusion
  14.6 2.9 %collective-permute-start.3 = (f32[100,200]{0,1:T(8,128)S(1)}, f32[100,200]{0,1:T(8,128)S(1)}, u32[]{:S(2)}, u32[]{:S(2)}) collective-permute-start(f32[100,200]{0,1:T(8,128)S(1)} %slice_select_fusion.2), channel_id=1, source_target_pairs={{0,8},{8,0},{16,24},{24,16},{1,9},{9,1},{17,25},{25,17},{2,10},{10... | collective-permute-start | bytes 240008 | tf_op jit(solution)/shard_map/ppermute | solution.py:31
  17.6 3.2 %collective-permute-done.3 = f32[100,200]{0,1:T(8,128)S(1)} collective-permute-done((f32[100,200]{0,1:T(8,128)S(1)}, f32[100,200]{0,1:T(8,128)S(1)}, u32[]{:S(2)}, u32[]{:S(2)}) %collective-permute-start.3) | collective-permute-done | bytes 80032 | tf_op jit(solution)/shard_map/ppermute | solution.py:31
  20.9 1.8 %collective-permute-start.4 = (f32[50,200]{0,1:T(8,128)S(1)}, f32[50,200]{0,1:T(8,128)S(1)}, u32[]{:S(2)}, u32[]{:S(2)}) collective-permute-start(f32[50,200]{0,1:T(8,128)S(1)} %slice_select_fusion.1), channel_id=1, source_target_pairs={{0,16},{8,24},{16,0},{24,8},{1,17},{9,25},{17,1},{25,9},{2,18},{10... | collective-permute-start | bytes 120008 | tf_op jit(solution)/shard_map/ppermute | solution.py:31
  22.8 2.9 %collective-permute-done.4 = f32[50,200]{0,1:T(8,128)S(1)} collective-permute-done((f32[50,200]{0,1:T(8,128)S(1)}, f32[50,200]{0,1:T(8,128)S(1)}, u32[]{:S(2)}, u32[]{:S(2)}) %collective-permute-start.4) | collective-permute-done | bytes 40032 | tf_op jit(solution)/shard_map/ppermute | solution.py:31
  25.9 1.9 %collective-permute-start.5 = (f32[25,200]{0,1:T(8,128)S(1)}, f32[25,200]{0,1:T(8,128)S(1)}, u32[]{:S(2)}, u32[]{:S(2)}) collective-permute-start(f32[25,200]{0,1:T(8,128)S(1)} %slice_select_fusion), channel_id=1, source_target_pairs={{0,2},{1,3},{2,0},{3,1},{4,6},{5,7},{6,4},{7,5},{8,10},{9,11},{10,... | collective-permute-start | bytes 60008 | tf_op jit(solution)/shard_map/ppermute | solution.py:31
  27.8 2.8 %collective-permute-done.5 = f32[25,200]{0,1:T(8,128)S(1)} collective-permute-done((f32[25,200]{0,1:T(8,128)S(1)}, f32[25,200]{0,1:T(8,128)S(1)}, u32[]{:S(2)}, u32[]{:S(2)}) %collective-permute-start.5) | collective-permute-done | bytes 20032 | tf_op jit(solution)/shard_map/ppermute | solution.py:31
  30.7 3.3 %collective-permute-start.6 = (f32[25,200]{0,1:T(8,128)S(1)}, f32[25,200]{0,1:T(8,128)S(1)}, u32[]{:S(2)}, u32[]{:S(2)}) collective-permute-start(f32[25,200]{0,1:T(8,128)S(1)} %select_add_fusion.1), channel_id=1, source_target_pairs={{0,4},{1,5},{2,6},{3,7},{4,0},{5,1},{6,2},{7,3},{8,12},{9,13},{10,... | collective-permute-start | bytes 60008 | tf_op jit(solution)/shard_map/ppermute | solution.py:31
  34.0 3.7 %collective-permute-done.6 = f32[25,200]{0,1:T(8,128)S(1)} collective-permute-done((f32[25,200]{0,1:T(8,128)S(1)}, f32[25,200]{0,1:T(8,128)S(1)}, u32[]{:S(2)}, u32[]{:S(2)}) %collective-permute-start.6) | collective-permute-done | bytes 20032 | tf_op jit(solution)/shard_map/ppermute | solution.py:31
  39.2 3.2 %collective-permute-done.7 = f32[25,200]{0,1:T(8,128)S(1)} collective-permute-done((f32[25,200]{0,1:T(8,128)S(1)}, f32[25,200]{0,1:T(8,128)S(1)}, u32[]{:S(2)}, u32[]{:S(2)}) %collective-permute-start.7) | collective-permute-done | bytes 20032 | tf_op jit(solution)/shard_map/ppermute | solution.py:31
  42.6 1.6 %collective-permute-start.8 = (f32[50,200]{0,1:T(8,128)S(1)}, f32[50,200]{0,1:T(8,128)S(1)}, u32[]{:S(2)}, u32[]{:S(2)}) collective-permute-start(f32[50,200]{0,1:T(8,128)S(1)} %maximum_select_fusion.2), channel_id=1, source_target_pairs={{0,16},{8,24},{16,0},{24,8},{1,17},{9,25},{17,1},{25,9},{2,18},{10... | collective-permute-start | bytes 120008 | tf_op jit(solution)/shard_map/ppermute | solution.py:31
  44.8 2.5 %collective-permute-done.8 = f32[50,200]{0,1:T(8,128)S(1)} collective-permute-done((f32[50,200]{0,1:T(8,128)S(1)}, f32[50,200]{0,1:T(8,128)S(1)}, u32[]{:S(2)}, u32[]{:S(2)}) %collective-permute-start.8) | collective-permute-done | bytes 40032 | tf_op jit(solution)/shard_map/ppermute | solution.py:31
  47.5 1.6 %collective-permute-start.9 = (f32[100,200]{0,1:T(8,128)S(1)}, f32[100,200]{0,1:T(8,128)S(1)}, u32[]{:S(2)}, u32[]{:S(2)}) collective-permute-start(f32[100,200]{0,1:T(8,128)S(1)} %maximum_select_fusion.3), channel_id=1, source_target_pairs={{0,8},{8,0},{16,24},{24,16},{1,9},{9,1},{17,25},{25,17},{2,10},{10... | collective-permute-start | bytes 240008 | tf_op jit(solution)/shard_map/ppermute | solution.py:31
  49.0 3.1 %collective-permute-done.9 = f32[100,200]{0,1:T(8,128)S(1)} collective-permute-done((f32[100,200]{0,1:T(8,128)S(1)}, f32[100,200]{0,1:T(8,128)S(1)}, u32[]{:S(2)}, u32[]{:S(2)}) %collective-permute-start.9) | collective-permute-done | bytes 80032 | tf_op jit(solution)/shard_map/ppermute | solution.py:31
  52.5 1.4 %collective-permute-done.10 = f32[200,200]{0,1:T(8,128)S(1)} collective-permute-done((f32[200,200]{0,1:T(8,128)S(1)}, f32[200,200]{0,1:T(8,128)S(1)}, u32[]{:S(2)}, u32[]{:S(2)}) %collective-permute-start.10) | collective-permute-done | bytes 160032 | tf_op jit(solution)/shard_map/ppermute | solution.py:31
  54.4 11.7 %cholesky.51 = f32[128,128]{1,0:T(8,128)S(1)} custom-call(f32[128,128]{1,0:T(8,128)S(1)} %cholesky.124), custom_call_target="Cholesky" | custom-call | tf_op jit(solution)/shard_map/jit(cholesky)/cholesky | solution.py:10
  66.2 9.8 %custom-call.16 = f32[1,128,128]{1,2,0:T(8,128)S(1)} custom-call(f32[1,128,128]{2,1,0:T(8,128)S(1)} %get-tuple-element.32), custom_call_target="InvertDiagBlocksLowerTriangular" | custom-call | tf_op jit(solution)/shard_map/jit(cholesky)/cholesky | solution.py:10
  76.4 6.6 %cholesky.110 = f32[72,72]{1,0:T(8,128)S(1)} custom-call(f32[72,72]{1,0:T(8,128)S(1)} %convolution_subtract_fusion), custom_call_target="Cholesky" | custom-call | tf_op jit(solution)/shard_map/jit(cholesky)/cholesky | solution.py:10
  86.0 19.9 %custom-call.17 = f32[2,128,128]{1,2,0:T(8,128)S(1)} custom-call(f32[2,128,128]{2,1,0:T(8,128)S(1)} %pad_maximum_fusion.3), custom_call_target="InvertDiagBlocksLowerTriangular" | custom-call | tf_op jit(solution)/shard_map/triangular_solve | solution.py:14
  108.1 3.4 %fusion.3 = f32[400,200]{0,1:T(8,128)S(1)} fusion(f32[1024,401]{0,1:T(8,128)} %all-gather.2.cloned.1.call-done, f32[1024]{0:T(1024)S(1)} %bitcast.42), kind=kOutput, calls=%fused_computation.3 | convolution fusion | flops 983244800 | bytes 2781696 | tf_op jit(solution)/shard_map/dot_general | solution.py:108
  112.5 1.5 %collective-permute-start = (f32[300,200]{0,1:T(8,128)}, f32[300,200]{0,1:T(8,128)S(1)}, u32[]{:S(2)}, u32[]{:S(2)}) collective-permute-start(f32[300,200]{0,1:T(8,128)} %pad_maximum_fusion), channel_id=1, source_target_pairs={{0,16},{8,24},{16,0},{24,8},{1,17},{9,25},{17,1},{25,9},{2,18},{10... | collective-permute-start | bytes 720008 | tf_op jit(solution)/shard_map/ppermute | solution.py:31
  115.0 0.9 convolution_subtract_fusion.1
  115.9 6.1 %collective-permute-done = f32[300,200]{0,1:T(8,128)S(1)} collective-permute-done((f32[300,200]{0,1:T(8,128)}, f32[300,200]{0,1:T(8,128)S(1)}, u32[]{:S(2)}, u32[]{:S(2)}) %collective-permute-start) | collective-permute-done | bytes 240032 | tf_op jit(solution)/shard_map/ppermute | solution.py:31
  122.4 1.6 %collective-permute-start.1 = (f32[250,200]{0,1:T(8,128)S(1)}, f32[250,200]{0,1:T(8,128)S(1)}, u32[]{:S(2)}, u32[]{:S(2)}) collective-permute-start(f32[250,200]{0,1:T(8,128)S(1)} %pad_maximum_fusion.2), channel_id=1, source_target_pairs={{0,8},{8,0},{16,24},{24,16},{1,9},{9,1},{17,25},{25,17},{2,10},{10... | collective-permute-start | bytes 600008 | tf_op jit(solution)/shard_map/ppermute | solution.py:31
  124.2 4.6 %collective-permute-done.1 = f32[250,200]{0,1:T(8,128)S(1)} collective-permute-done((f32[250,200]{0,1:T(8,128)S(1)}, f32[250,200]{0,1:T(8,128)S(1)}, u32[]{:S(2)}, u32[]{:S(2)}) %collective-permute-start.1) | collective-permute-done | bytes 200032 | tf_op jit(solution)/shard_map/ppermute | solution.py:31
  128.8 1.3 fusion.14
  130.1 2.7 %fusion.8 = f32[3,50,1024]{2,1,0:T(8,128)} fusion(f32[3,200,1024]{2,1,0:T(8,128)S(1)} %copy-done, f32[3,1024]{1,0:T(4,128)S(1)} %copy-done.3, s32[]{:T(128)S(6)} %select_n.146, f32[50,200]{0,1:T(8,128)S(1)} %fusion.14, f32[250,200]{0,1:T(8,128)S(1)} %collective-permute-done.1, f32[100,200]{0,1:T(8,128)S(1)} %slice_add_fusion.5, pred[]{:T(512)S(6)} %eq.32), kind=kOutput, calls=%fused_computation.6 | convolution fusion | flops 370052416 | bytes 4186117 | tf_op jit(solution)/shard_map/vnc,mn->vmc/dot_general | solution.py:121
  (67 shorter events, 11.6 us)
Async XLA Ops:
  6.5 100.7 %all-gather.2.cloned.1.call-start = ((), (), s32[]{:S(2)}) async-start(), calls=%async_computation | async-start | bytes 1880064 | tf_op jit(solution)/shard_map/all_gather | solution.py:99
  10.4 28.7 %copy-start = (f32[3,200,1024]{2,1,0:T(8,128)S(1)}, f32[3,200,1024]{2,1,0:T(8,128)}, u32[]{:S(2)}) copy-start(f32[3,200,1024]{2,1,0:T(8,128)} %param.6) | copy-start | bytes 7372804
  11.8 1.7 %collective-permute-start.2 = (f32[200,200]{0,1:T(8,128)S(1)}, f32[200,200]{0,1:T(8,128)}, u32[]{:S(2)}, u32[]{:S(2)}) collective-permute-start(f32[200,200]{0,1:T(8,128)S(1)} %get-tuple-element.35), channel_id=1, source_target_pairs={{0,1},{1,0},{2,3},{3,2},{4,5},{5,4},{6,7},{7,6},{8,9},{9,8},{10,11... | collective-permute-start | bytes 480008 | tf_op jit(solution)/shard_map/ppermute | solution.py:31
  14.6 6.1 %collective-permute-start.3 = (f32[100,200]{0,1:T(8,128)S(1)}, f32[100,200]{0,1:T(8,128)S(1)}, u32[]{:S(2)}, u32[]{:S(2)}) collective-permute-start(f32[100,200]{0,1:T(8,128)S(1)} %slice_select_fusion.2), channel_id=1, source_target_pairs={{0,8},{8,0},{16,24},{24,16},{1,9},{9,1},{17,25},{25,17},{2,10},{10... | collective-permute-start | bytes 240008 | tf_op jit(solution)/shard_map/ppermute | solution.py:31
  20.9 4.7 %collective-permute-start.4 = (f32[50,200]{0,1:T(8,128)S(1)}, f32[50,200]{0,1:T(8,128)S(1)}, u32[]{:S(2)}, u32[]{:S(2)}) collective-permute-start(f32[50,200]{0,1:T(8,128)S(1)} %slice_select_fusion.1), channel_id=1, source_target_pairs={{0,16},{8,24},{16,0},{24,8},{1,17},{9,25},{17,1},{25,9},{2,18},{10... | collective-permute-start | bytes 120008 | tf_op jit(solution)/shard_map/ppermute | solution.py:31
  25.8 23.3 %copy-start.4 = (s32[1,8]{1,0:T(1,128)S(1)}, s32[1,8]{1,0:T(1,128)}, u32[]{:S(2)}) copy-start(s32[1,8]{1,0:T(1,128)} %param.11) | copy-start | bytes 100
  25.8 23.2 %copy-start.5 = (s32[1,8]{1,0:T(1,128)S(1)}, s32[1,8]{1,0:T(1,128)}, u32[]{:S(2)}) copy-start(s32[1,8]{1,0:T(1,128)} %param.10) | copy-start | bytes 100
  25.9 4.7 %collective-permute-start.5 = (f32[25,200]{0,1:T(8,128)S(1)}, f32[25,200]{0,1:T(8,128)S(1)}, u32[]{:S(2)}, u32[]{:S(2)}) collective-permute-start(f32[25,200]{0,1:T(8,128)S(1)} %slice_select_fusion), channel_id=1, source_target_pairs={{0,2},{1,3},{2,0},{3,1},{4,6},{5,7},{6,4},{7,5},{8,10},{9,11},{10,... | collective-permute-start | bytes 60008 | tf_op jit(solution)/shard_map/ppermute | solution.py:31
  30.7 7.0 %collective-permute-start.6 = (f32[25,200]{0,1:T(8,128)S(1)}, f32[25,200]{0,1:T(8,128)S(1)}, u32[]{:S(2)}, u32[]{:S(2)}) collective-permute-start(f32[25,200]{0,1:T(8,128)S(1)} %select_add_fusion.1), channel_id=1, source_target_pairs={{0,4},{1,5},{2,6},{3,7},{4,0},{5,1},{6,2},{7,3},{8,12},{9,13},{10,... | collective-permute-start | bytes 60008 | tf_op jit(solution)/shard_map/ppermute | solution.py:31
  37.8 4.7 %collective-permute-start.7 = (f32[25,200]{0,1:T(8,128)S(1)}, f32[25,200]{0,1:T(8,128)S(1)}, u32[]{:S(2)}, u32[]{:S(2)}) collective-permute-start(f32[25,200]{0,1:T(8,128)S(1)} %add.98), channel_id=1, source_target_pairs={{0,2},{1,3},{2,0},{3,1},{4,6},{5,7},{6,4},{7,5},{8,10},{9,11},{10,... | collective-permute-start | bytes 60008 | tf_op jit(solution)/shard_map/ppermute | solution.py:31
  42.6 4.7 %collective-permute-start.8 = (f32[50,200]{0,1:T(8,128)S(1)}, f32[50,200]{0,1:T(8,128)S(1)}, u32[]{:S(2)}, u32[]{:S(2)}) collective-permute-start(f32[50,200]{0,1:T(8,128)S(1)} %maximum_select_fusion.2), channel_id=1, source_target_pairs={{0,16},{8,24},{16,0},{24,8},{1,17},{9,25},{17,1},{25,9},{2,18},{10... | collective-permute-start | bytes 120008 | tf_op jit(solution)/shard_map/ppermute | solution.py:31
  47.5 4.7 %collective-permute-start.9 = (f32[100,200]{0,1:T(8,128)S(1)}, f32[100,200]{0,1:T(8,128)S(1)}, u32[]{:S(2)}, u32[]{:S(2)}) collective-permute-start(f32[100,200]{0,1:T(8,128)S(1)} %maximum_select_fusion.3), channel_id=1, source_target_pairs={{0,8},{8,0},{16,24},{24,16},{1,9},{9,1},{17,25},{25,17},{2,10},{10... | collective-permute-start | bytes 240008 | tf_op jit(solution)/shard_map/ppermute | solution.py:31
  52.4 1.5 %collective-permute-start.10 = (f32[200,200]{0,1:T(8,128)S(1)}, f32[200,200]{0,1:T(8,128)S(1)}, u32[]{:S(2)}, u32[]{:S(2)}) collective-permute-start(f32[200,200]{0,1:T(8,128)S(1)} %maximum_select_fusion.1), channel_id=1, source_target_pairs={{0,1},{1,0},{2,3},{3,2},{4,5},{5,4},{6,7},{7,6},{8,9},{9,8},{10,11... | collective-permute-start | bytes 480008 | tf_op jit(solution)/shard_map/ppermute | solution.py:31
  106.1 5.5 %copy-start.1 = (f32[128,50]{0,1:T(8,128)}, f32[128,50]{0,1:T(8,128)S(1)}, u32[]{:S(2)}) copy-start(f32[128,50]{0,1:T(8,128)S(1)} %fusion.35) | copy-start | bytes 76804
  107.2 6.8 %copy-start.2 = (f32[72,50]{1,0:T(8,128)S(1)}, f32[72,50]{1,0:T(8,128)}, u32[]{:S(2)}) copy-start(f32[72,50]{1,0:T(8,128)} %fusion.43) | copy-start | bytes 43204
  111.5 18.6 %copy-start.3 = (f32[3,1024]{1,0:T(4,128)S(1)}, f32[3,1024]{1,0:T(4,128)}, u32[]{:S(2)}) copy-start(f32[3,1024]{1,0:T(4,128)} %broadcast_multiply_fusion) | copy-start | bytes 36868
  112.5 9.5 %collective-permute-start = (f32[300,200]{0,1:T(8,128)}, f32[300,200]{0,1:T(8,128)S(1)}, u32[]{:S(2)}, u32[]{:S(2)}) collective-permute-start(f32[300,200]{0,1:T(8,128)} %pad_maximum_fusion), channel_id=1, source_target_pairs={{0,16},{8,24},{16,0},{24,8},{1,17},{9,25},{17,1},{25,9},{2,18},{10... | collective-permute-start | bytes 720008 | tf_op jit(solution)/shard_map/ppermute | solution.py:31
  122.4 6.4 %collective-permute-start.1 = (f32[250,200]{0,1:T(8,128)S(1)}, f32[250,200]{0,1:T(8,128)S(1)}, u32[]{:S(2)}, u32[]{:S(2)}) collective-permute-start(f32[250,200]{0,1:T(8,128)S(1)} %pad_maximum_fusion.2), channel_id=1, source_target_pairs={{0,8},{8,0},{16,24},{24,16},{1,9},{9,1},{17,25},{25,17},{2,10},{10... | collective-permute-start | bytes 600008 | tf_op jit(solution)/shard_map/ppermute | solution.py:31
Sparse Core Ops, SparseCore 0:
  39.2 29.3 all-gather.1

commit v2 on v1

--- a/solution.py
+++ b/solution.py
@@ -92,9 +92,6 @@
     own_count = members // lax.axis_size("well")
     own_start = lax.axis_index("well") * own_count
     cross_mine = lax.dynamic_slice_in_dim(cross_matrix, own_start, own_count, 1)
-    system = jnp.eye(members, dtype=jnp.float32) + gram_matrix
-    solved_mine = chol_apply(system, cross_mine)
-
     packed = jnp.concatenate([data_anom, innov, row_weight[:, None]], 1)
     group = lax.all_gather(packed, "tile", axis=0, tiled=True)
     group_anom, group_innov, group_weight = (
@@ -113,6 +110,11 @@
     )
     taper_gram, taper_cross_t = both[:members], both[members:]
     taper_gram, cross_t_mine = well_reduce(taper_gram, taper_cross_t)
+    gram_matrix, cross_mine, taper_gram, cross_t_mine = lax.optimization_barrier(
+        (gram_matrix, cross_mine, taper_gram, cross_t_mine)
+    )
+    system = jnp.eye(members, dtype=jnp.float32) + gram_matrix
+    solved_mine = chol_apply(system, cross_mine)
 
     space_t = cross_t_mine - lax.dot_general(
         solved_mine, taper_gram, (((0,), (1,)), ((), ())), precision=highest

time: 140 us -> 144 us (1.029)
  waiting for transfers between devices: 34.9 us -> 45.9 us
  starting transfers between devices: 17.3 us -> 14 us
  matrix products: 13.3 us -> 11.1 us
    ppermute x11, waiting for transfers between devices: 34.9 us -> 45.9 us  [swap(): return lax.ppermute(x, axis, [(i, i ^ k) for i in range(size)])]
    ppermute x11, starting transfers between devices: 17.3 us -> 14 us  [swap(): return lax.ppermute(x, axis, [(i, i ^ k) for i in range(size)])]
  transfers between devices with their start and end apart: 12 -> 12, of which waited for: 11 -> 10; matrix products, arithmetic and copies ran while one was open for 40% -> 7% of each run, Pallas kernels for 0% -> 0%
where the time goes in v2:
time: 144 us
  other arithmetic  57.4 us (40%)
  waiting for transfers between devices  45.9 us (32%)
  between operations  15.1 us (10%)
  starting transfers between devices  14 us (10%)
  matrix products  11.1 us (8%)
    ppermute x11, waiting for transfers between devices, swap(): return lax.ppermute(x, axis, [(i, i ^ k) for i in range(size)])  45.9 us
    another operation x7, other arithmetic, chol_apply(): factor = jnp.linalg.cholesky(system)  29.6 us
    another operation x6, other arithmetic, chol_apply(): lax.linalg.triangular_solve(factor, middle, left_side=True, lower=True, t...  19.8 us
    ppermute x11, starting transfers between devices, swap(): return lax.ppermute(x, axis, [(i, i ^ k) for i in range(size)])  14 us
    dot_general x1, matrix products, shards(): lax.dot_general(jnp.concatenate([group_anom, group_innov], 1), tapered, (...  3.38 us
  transfers between devices with their start and end apart: 12, of which 10 were waited for; matrix products, arithmetic and copies ran while one was open for 7% of the time, Pallas kernels for 0%

profile of v2, /device:TPU:0, one launch (start us, length us, event | category | flops | bytes accessed | tf_op | source)
XLA Modules:
  0.0 144.1 jit_solution(591065765375854897)
XLA Ops:
  6.5 0.9 reduce_sum.18
  8.1 1.0 subtract_multiply_fusion
  9.1 0.7 pad_maximum_fusion.1
  9.8 1.4 fusion.23
  11.2 1.3 broadcast_select_fusion
  13.1 1.1 collective-permute-done
  14.3 2.9 %collective-permute-start.1 = (f32[100,200]{0,1:T(8,128)S(1)}, f32[100,200]{0,1:T(8,128)S(1)}, u32[]{:S(2)}, u32[]{:S(2)}) collective-permute-start(f32[100,200]{0,1:T(8,128)S(1)} %slice_select_fusion.4), channel_id=1, source_target_pairs={{0,8},{8,0},{16,24},{24,16},{1,9},{9,1},{17,25},{25,17},{2,10},{10... | collective-permute-start | bytes 240008 | tf_op jit(solution)/shard_map/ppermute | solution.py:31
  17.2 3.2 %collective-permute-done.1 = f32[100,200]{0,1:T(8,128)S(1)} collective-permute-done((f32[100,200]{0,1:T(8,128)S(1)}, f32[100,200]{0,1:T(8,128)S(1)}, u32[]{:S(2)}, u32[]{:S(2)}) %collective-permute-start.1) | collective-permute-done | bytes 80032 | tf_op jit(solution)/shard_map/ppermute | solution.py:31
  20.7 1.8 %collective-permute-start.2 = (f32[50,200]{0,1:T(8,128)S(1)}, f32[50,200]{0,1:T(8,128)S(1)}, u32[]{:S(2)}, u32[]{:S(2)}) collective-permute-start(f32[50,200]{0,1:T(8,128)S(1)} %slice_select_fusion.3), channel_id=1, source_target_pairs={{0,16},{8,24},{16,0},{24,8},{1,17},{9,25},{17,1},{25,9},{2,18},{10... | collective-permute-start | bytes 120008 | tf_op jit(solution)/shard_map/ppermute | solution.py:31
  22.5 2.9 %collective-permute-done.2 = f32[50,200]{0,1:T(8,128)S(1)} collective-permute-done((f32[50,200]{0,1:T(8,128)S(1)}, f32[50,200]{0,1:T(8,128)S(1)}, u32[]{:S(2)}, u32[]{:S(2)}) %collective-permute-start.2) | collective-permute-done | bytes 40032 | tf_op jit(solution)/shard_map/ppermute | solution.py:31
  25.6 1.9 %collective-permute-start.3 = (f32[25,200]{0,1:T(8,128)S(1)}, f32[25,200]{0,1:T(8,128)S(1)}, u32[]{:S(2)}, u32[]{:S(2)}) collective-permute-start(f32[25,200]{0,1:T(8,128)S(1)} %slice_select_fusion.2), channel_id=1, source_target_pairs={{0,2},{1,3},{2,0},{3,1},{4,6},{5,7},{6,4},{7,5},{8,10},{9,11},{10,... | collective-permute-start | bytes 60008 | tf_op jit(solution)/shard_map/ppermute | solution.py:31
  27.5 7.5 %collective-permute-done.3 = f32[25,200]{0,1:T(8,128)S(1)} collective-permute-done((f32[25,200]{0,1:T(8,128)S(1)}, f32[25,200]{0,1:T(8,128)S(1)}, u32[]{:S(2)}, u32[]{:S(2)}) %collective-permute-start.3) | collective-permute-done | bytes 20032 | tf_op jit(solution)/shard_map/ppermute | solution.py:31
  35.6 8.3 %collective-permute-done.4 = f32[25,200]{0,1:T(8,128)S(1)} collective-permute-done((f32[25,200]{0,1:T(8,128)S(1)}, f32[25,200]{0,1:T(8,128)S(1)}, u32[]{:S(2)}, u32[]{:S(2)}) %collective-permute-start.4) | collective-permute-done | bytes 20032 | tf_op jit(solution)/shard_map/ppermute | solution.py:31
  44.2 4.5 %collective-permute-done.5 = f32[25,200]{0,1:T(8,128)S(1)} collective-permute-done((f32[25,200]{0,1:T(8,128)S(1)}, f32[25,200]{0,1:T(8,128)S(1)}, u32[]{:S(2)}, u32[]{:S(2)}) %collective-permute-start.5) | collective-permute-done | bytes 20032 | tf_op jit(solution)/shard_map/ppermute | solution.py:31
  48.8 1.6 %collective-permute-start.6 = (f32[50,200]{0,1:T(8,128)S(1)}, f32[50,200]{0,1:T(8,128)S(1)}, u32[]{:S(2)}, u32[]{:S(2)}) collective-permute-start(f32[50,200]{0,1:T(8,128)S(1)} %maximum_select_fusion.2), channel_id=1, source_target_pairs={{0,16},{8,24},{16,0},{24,8},{1,17},{9,25},{17,1},{25,9},{2,18},{10... | collective-permute-start | bytes 120008 | tf_op jit(solution)/shard_map/ppermute | solution.py:31
  50.4 3.2 %collective-permute-done.6 = f32[50,200]{0,1:T(8,128)S(1)} collective-permute-done((f32[50,200]{0,1:T(8,128)S(1)}, f32[50,200]{0,1:T(8,128)S(1)}, u32[]{:S(2)}, u32[]{:S(2)}) %collective-permute-start.6) | collective-permute-done | bytes 40032 | tf_op jit(solution)/shard_map/ppermute | solution.py:31
  53.6 1.5 %collective-permute-start.7 = (f32[100,200]{0,1:T(8,128)S(1)}, f32[100,200]{0,1:T(8,128)S(1)}, u32[]{:S(2)}, u32[]{:S(2)}) collective-permute-start(f32[100,200]{0,1:T(8,128)S(1)} %maximum_select_fusion.3), channel_id=1, source_target_pairs={{0,8},{8,0},{16,24},{24,16},{1,9},{9,1},{17,25},{25,17},{2,10},{10... | collective-permute-start | bytes 240008 | tf_op jit(solution)/shard_map/ppermute | solution.py:31
  55.2 3.2 %collective-permute-done.7 = f32[100,200]{0,1:T(8,128)S(1)} collective-permute-done((f32[100,200]{0,1:T(8,128)S(1)}, f32[100,200]{0,1:T(8,128)S(1)}, u32[]{:S(2)}, u32[]{:S(2)}) %collective-permute-start.7) | collective-permute-done | bytes 80032 | tf_op jit(solution)/shard_map/ppermute | solution.py:31
  58.7 0.8 slice_multiply_fusion.2
  59.5 3.4 %fusion.3 = f32[400,200]{0,1:T(8,128)S(1)} fusion(f32[1024,401]{0,1:T(8,128)} %all-gather.2.cloned.1.call-done, f32[1024]{0:T(1024)S(1)} %bitcast.44), kind=kOutput, calls=%fused_computation.3 | convolution fusion | flops 983244800 | bytes 2781696 | tf_op jit(solution)/shard_map/dot_general | solution.py:105
  63.0 0.8 pad_maximum_fusion
  63.9 1.5 %collective-permute-start.9 = (f32[300,200]{0,1:T(8,128)}, f32[300,200]{0,1:T(8,128)S(1)}, u32[]{:S(2)}, u32[]{:S(2)}) collective-permute-start(f32[300,200]{0,1:T(8,128)} %pad_maximum_fusion), channel_id=1, source_target_pairs={{0,16},{8,24},{16,0},{24,8},{1,17},{9,25},{17,1},{25,9},{2,18},{10... | collective-permute-start | bytes 720008 | tf_op jit(solution)/shard_map/ppermute | solution.py:31
  65.4 1.3 maximum_select_fusion
  66.7 7.1 %collective-permute-done.9 = f32[300,200]{0,1:T(8,128)S(1)} collective-permute-done((f32[300,200]{0,1:T(8,128)}, f32[300,200]{0,1:T(8,128)S(1)}, u32[]{:S(2)}, u32[]{:S(2)}) %collective-permute-start.9) | collective-permute-done | bytes 240032 | tf_op jit(solution)/shard_map/ppermute | solution.py:31
  74.1 1.5 %collective-permute-start.10 = (f32[250,200]{0,1:T(8,128)S(1)}, f32[250,200]{0,1:T(8,128)S(1)}, u32[]{:S(2)}, u32[]{:S(2)}) collective-permute-start(f32[250,200]{0,1:T(8,128)S(1)} %pad_maximum_fusion.2), channel_id=1, source_target_pairs={{0,8},{8,0},{16,24},{24,16},{1,9},{9,1},{17,25},{25,17},{2,10},{10... | collective-permute-start | bytes 600008 | tf_op jit(solution)/shard_map/ppermute | solution.py:31
  75.8 5.0 %collective-permute-done.10 = f32[250,200]{0,1:T(8,128)S(1)} collective-permute-done((f32[250,200]{0,1:T(8,128)S(1)}, f32[250,200]{0,1:T(8,128)S(1)}, u32[]{:S(2)}, u32[]{:S(2)}) %collective-permute-start.10) | collective-permute-done | bytes 200032 | tf_op jit(solution)/shard_map/ppermute | solution.py:31
  81.2 11.7 %cholesky.51 = f32[128,128]{1,0:T(8,128)S(1)} custom-call(f32[128,128]{1,0:T(8,128)S(1)} %cholesky.124), custom_call_target="Cholesky" | custom-call | tf_op jit(solution)/shard_map/jit(cholesky)/cholesky | solution.py:10
  93.0 9.8 %custom-call.16 = f32[1,128,128]{1,2,0:T(8,128)S(1)} custom-call(f32[1,128,128]{2,1,0:T(8,128)S(1)} %get-tuple-element.40), custom_call_target="InvertDiagBlocksLowerTriangular" | custom-call | tf_op jit(solution)/shard_map/jit(cholesky)/cholesky | solution.py:10
  103.2 6.7 %cholesky.110 = f32[72,72]{1,0:T(8,128)S(1)} custom-call(f32[72,72]{1,0:T(8,128)S(1)} %convolution_subtract_fusion), custom_call_target="Cholesky" | custom-call | tf_op jit(solution)/shard_map/jit(cholesky)/cholesky | solution.py:10
  110.0 0.7 compare_reduce_fusion
  112.8 19.7 %custom-call.17 = f32[2,128,128]{1,2,0:T(8,128)S(1)} custom-call(f32[2,128,128]{2,1,0:T(8,128)S(1)} %pad_maximum_fusion.3), custom_call_target="InvertDiagBlocksLowerTriangular" | custom-call | tf_op jit(solution)/shard_map/triangular_solve | solution.py:14
  134.5 2.7 %fusion.8 = f32[3,50,1024]{2,1,0:T(8,128)} fusion(f32[3,200,1024]{2,1,0:T(8,128)S(1)} %copy-done, f32[3,1024]{1,0:T(4,128)S(1)} %broadcast_multiply_fusion, s32[]{:T(128)S(6)} %select_n.146, f32[50,200]{0,1:T(8,128)S(1)} %slice_add_fusion.2, f32[50,200]{0,1:T(8,128)S(1)} %fusion.15), kind=kOutput, calls=%fused_computation.6 | convolution fusion | flops 370032384 | bytes 3981316 | tf_op jit(solution)/shard_map/vnc,mn->vmc/dot_general | solution.py:123
  (65 shorter events, 7.4 us)
Async XLA Ops:
  6.5 52.1 %all-gather.2.cloned.1.call-start = ((), (), s32[]{:S(2)}) async-start(), calls=%async_computation | async-start | bytes 1880064 | tf_op jit(solution)/shard_map/all_gather | solution.py:96
  9.8 34.2 %copy-start = (f32[3,200,1024]{2,1,0:T(8,128)S(1)}, f32[3,200,1024]{2,1,0:T(8,128)}, u32[]{:S(2)}) copy-start(f32[3,200,1024]{2,1,0:T(8,128)} %param.6) | copy-start | bytes 7372804
  12.6 1.6 %collective-permute-start = (f32[200,200]{0,1:T(8,128)S(1)}, f32[200,200]{0,1:T(8,128)S(1)}, u32[]{:S(2)}, u32[]{:S(2)}) collective-permute-start(f32[200,200]{0,1:T(8,128)S(1)} %get-tuple-element.43), channel_id=1, source_target_pairs={{0,1},{1,0},{2,3},{3,2},{4,5},{5,4},{6,7},{7,6},{8,9},{9,8},{10,11... | collective-permute-start | bytes 480008 | tf_op jit(solution)/shard_map/ppermute | solution.py:31
  14.3 6.1 %collective-permute-start.1 = (f32[100,200]{0,1:T(8,128)S(1)}, f32[100,200]{0,1:T(8,128)S(1)}, u32[]{:S(2)}, u32[]{:S(2)}) collective-permute-start(f32[100,200]{0,1:T(8,128)S(1)} %slice_select_fusion.4), channel_id=1, source_target_pairs={{0,8},{8,0},{16,24},{24,16},{1,9},{9,1},{17,25},{25,17},{2,10},{10... | collective-permute-start | bytes 240008 | tf_op jit(solution)/shard_map/ppermute | solution.py:31
  20.5 34.7 %copy-start.1 = (s32[1,8]{1,0:T(1,128)S(1)}, s32[1,8]{1,0:T(1,128)}, u32[]{:S(2)}) copy-start(s32[1,8]{1,0:T(1,128)} %param.11) | copy-start | bytes 100
  20.5 34.7 %copy-start.2 = (s32[1,8]{1,0:T(1,128)S(1)}, s32[1,8]{1,0:T(1,128)}, u32[]{:S(2)}) copy-start(s32[1,8]{1,0:T(1,128)} %param.10) | copy-start | bytes 100
  20.7 4.7 %collective-permute-start.2 = (f32[50,200]{0,1:T(8,128)S(1)}, f32[50,200]{0,1:T(8,128)S(1)}, u32[]{:S(2)}, u32[]{:S(2)}) collective-permute-start(f32[50,200]{0,1:T(8,128)S(1)} %slice_select_fusion.3), channel_id=1, source_target_pairs={{0,16},{8,24},{16,0},{24,8},{1,17},{9,25},{17,1},{25,9},{2,18},{10... | collective-permute-start | bytes 120008 | tf_op jit(solution)/shard_map/ppermute | solution.py:31
  25.6 9.4 %collective-permute-start.3 = (f32[25,200]{0,1:T(8,128)S(1)}, f32[25,200]{0,1:T(8,128)S(1)}, u32[]{:S(2)}, u32[]{:S(2)}) collective-permute-start(f32[25,200]{0,1:T(8,128)S(1)} %slice_select_fusion.2), channel_id=1, source_target_pairs={{0,2},{1,3},{2,0},{3,1},{4,6},{5,7},{6,4},{7,5},{8,10},{9,11},{10,... | collective-permute-start | bytes 60008 | tf_op jit(solution)/shard_map/ppermute | solution.py:31
  35.1 8.9 %collective-permute-start.4 = (f32[25,200]{0,1:T(8,128)S(1)}, f32[25,200]{0,1:T(8,128)S(1)}, u32[]{:S(2)}, u32[]{:S(2)}) collective-permute-start(f32[25,200]{0,1:T(8,128)S(1)} %select_add_fusion.1), channel_id=1, source_target_pairs={{0,4},{1,5},{2,6},{3,7},{4,0},{5,1},{6,2},{7,3},{8,12},{9,13},{10,... | collective-permute-start | bytes 60008 | tf_op jit(solution)/shard_map/ppermute | solution.py:31
  43.9 4.7 %collective-permute-start.5 = (f32[25,200]{0,1:T(8,128)S(1)}, f32[25,200]{0,1:T(8,128)S(1)}, u32[]{:S(2)}, u32[]{:S(2)}) collective-permute-start(f32[25,200]{0,1:T(8,128)S(1)} %add.95), channel_id=1, source_target_pairs={{0,2},{1,3},{2,0},{3,1},{4,6},{5,7},{6,4},{7,5},{8,10},{9,11},{10,... | collective-permute-start | bytes 60008 | tf_op jit(solution)/shard_map/ppermute | solution.py:31
  48.8 4.7 %collective-permute-start.6 = (f32[50,200]{0,1:T(8,128)S(1)}, f32[50,200]{0,1:T(8,128)S(1)}, u32[]{:S(2)}, u32[]{:S(2)}) collective-permute-start(f32[50,200]{0,1:T(8,128)S(1)} %maximum_select_fusion.2), channel_id=1, source_target_pairs={{0,16},{8,24},{16,0},{24,8},{1,17},{9,25},{17,1},{25,9},{2,18},{10... | collective-permute-start | bytes 120008 | tf_op jit(solution)/shard_map/ppermute | solution.py:31
  53.6 4.7 %collective-permute-start.7 = (f32[100,200]{0,1:T(8,128)S(1)}, f32[100,200]{0,1:T(8,128)S(1)}, u32[]{:S(2)}, u32[]{:S(2)}) collective-permute-start(f32[100,200]{0,1:T(8,128)S(1)} %maximum_select_fusion.3), channel_id=1, source_target_pairs={{0,8},{8,0},{16,24},{24,16},{1,9},{9,1},{17,25},{25,17},{2,10},{10... | collective-permute-start | bytes 240008 | tf_op jit(solution)/shard_map/ppermute | solution.py:31
  58.6 6.8 %collective-permute-start.8 = (f32[200,200]{0,1:T(8,128)S(1)}, f32[200,200]{0,1:T(8,128)}, u32[]{:S(2)}, u32[]{:S(2)}) collective-permute-start(f32[200,200]{0,1:T(8,128)S(1)} %maximum_select_fusion.1), channel_id=1, source_target_pairs={{0,1},{1,0},{2,3},{3,2},{4,5},{5,4},{6,7},{7,6},{8,9},{9,8},{10,11... | collective-permute-start | bytes 480008 | tf_op jit(solution)/shard_map/ppermute | solution.py:31
  63.9 9.9 %collective-permute-start.9 = (f32[300,200]{0,1:T(8,128)}, f32[300,200]{0,1:T(8,128)S(1)}, u32[]{:S(2)}, u32[]{:S(2)}) collective-permute-start(f32[300,200]{0,1:T(8,128)} %pad_maximum_fusion), channel_id=1, source_target_pairs={{0,16},{8,24},{16,0},{24,8},{1,17},{9,25},{17,1},{25,9},{2,18},{10... | collective-permute-start | bytes 720008 | tf_op jit(solution)/shard_map/ppermute | solution.py:31
  74.1 6.7 %collective-permute-start.10 = (f32[250,200]{0,1:T(8,128)S(1)}, f32[250,200]{0,1:T(8,128)S(1)}, u32[]{:S(2)}, u32[]{:S(2)}) collective-permute-start(f32[250,200]{0,1:T(8,128)S(1)} %pad_maximum_fusion.2), channel_id=1, source_target_pairs={{0,8},{8,0},{16,24},{24,16},{1,9},{9,1},{17,25},{25,17},{2,10},{10... | collective-permute-start | bytes 600008 | tf_op jit(solution)/shard_map/ppermute | solution.py:31
Sparse Core Ops, SparseCore 0:
  9.9 35.6 all-gather.1

commit v3 on v1

--- a/solution.py
+++ b/solution.py
@@ -4,14 +4,6 @@
 from jax.sharding import PartitionSpec as P
 
 BLOCK = 128
-
-
-def chol_apply(system, right):
-    factor = jnp.linalg.cholesky(system)
-    middle = lax.linalg.triangular_solve(
-        factor, right, left_side=True, lower=True, transpose_a=False
-    )
-    return lax.linalg.triangular_solve(factor, middle, left_side=True, lower=True, transpose_a=True)
 
 
 def prepare(pred_rows, obs_rows, std_rows, norm_factor):
@@ -40,7 +32,7 @@
     return out
 
 
-def all_sum(x, steps):
+def all_sum(x, steps, tie):
     halved = []
     for axis, k in steps:
         rows = x.shape[0]
@@ -53,24 +45,22 @@
             halved.append((axis, k))
         else:
             x = x + swap(x, axis, k)
+    x, tie = lax.optimization_barrier((x, tie))
     for axis, k in reversed(halved):
         other = swap(x, axis, k)
         hi = bit_of(axis, k) == 1
         x = jnp.where(hi, jnp.concatenate([other, x], 0), jnp.concatenate([x, other], 0))
-    return x
+    return x, tie
 
 
-def well_reduce(full, split):
-    for axis, k in reversed(axis_bits("well")):
-        rows = split.shape[0]
-        half = rows // 2
-        hi = bit_of(axis, k) == 1
-        keep = jnp.where(hi, split[half:], split[:half])
-        send = jnp.where(hi, split[:half], split[half:])
-        got = swap(jnp.concatenate([full, send], 0), axis, k)
-        full = full + got[: full.shape[0]]
-        split = keep + got[full.shape[0]:]
-    return full, split
+def well_step(full, split, axis, k):
+    rows = split.shape[0]
+    half = rows // 2
+    hi = bit_of(axis, k) == 1
+    keep = jnp.where(hi, split[half:], split[:half])
+    send = jnp.where(hi, split[:half], split[half:])
+    got = swap(jnp.concatenate([full, send], 0), axis, k)
+    return full + got[: full.shape[0]], keep + got[full.shape[0]:]
 
 
 def shards(prior_state, pred_data, obs_pert, obs_std, loc_mask, taper_level):
@@ -86,17 +76,18 @@
         ],
         0,
     )
+    packed = jnp.concatenate([data_anom, innov, row_weight[:, None]], 1)
     order = axis_bits("tile")[:1] + axis_bits("well") + axis_bits("tile")[1:]
-    stacked = all_sum(stacked, order)
+    stacked, packed = all_sum(stacked, order, packed)
     gram_matrix, cross_matrix = stacked[:members], stacked[members:]
     own_count = members // lax.axis_size("well")
     own_start = lax.axis_index("well") * own_count
     cross_mine = lax.dynamic_slice_in_dim(cross_matrix, own_start, own_count, 1)
     system = jnp.eye(members, dtype=jnp.float32) + gram_matrix
-    solved_mine = chol_apply(system, cross_mine)
+    factor = jnp.linalg.cholesky(system)
 
-    packed = jnp.concatenate([data_anom, innov, row_weight[:, None]], 1)
     group = lax.all_gather(packed, "tile", axis=0, tiled=True)
+    factor, group = lax.optimization_barrier((factor, group))
     group_anom, group_innov, group_weight = (
         group[:, :members],
         group[:, members : 2 * members],
@@ -112,7 +103,18 @@
         precision=highest,
     )
     taper_gram, taper_cross_t = both[:members], both[members:]
-    taper_gram, cross_t_mine = well_reduce(taper_gram, taper_cross_t)
+    steps = list(reversed(axis_bits("well")))
+    factor, taper_gram, taper_cross_t = lax.optimization_barrier((factor, taper_gram, taper_cross_t))
+    taper_gram, cross_t_mine = well_step(taper_gram, taper_cross_t, *steps[0])
+    middle = lax.linalg.triangular_solve(
+        factor, cross_mine, left_side=True, lower=True, transpose_a=False
+    )
+    middle, taper_gram, cross_t_mine = lax.optimization_barrier((middle, taper_gram, cross_t_mine))
+    for axis, k in steps[1:]:
+        taper_gram, cross_t_mine = well_step(taper_gram, cross_t_mine, axis, k)
+    solved_mine = lax.linalg.triangular_solve(
+        factor, middle, left_side=True, lower=True, transpose_a=True
+    )
 
     space_t = cross_t_mine - lax.dot_general(
         solved_mine, taper_gram, (((0,), (1,)), ((), ())), precision=highest

time: 140 us -> 137 us (0.979)
  waiting for transfers between devices: 34.9 us -> 28.5 us
  other arithmetic: 58 us -> 61.1 us
    ppermute x11, waiting for transfers between devices: 34.9 us -> 28.5 us  [swap(): return lax.ppermute(x, axis, [(i, i ^ k) for i in range(size)])]
    add x2, other arithmetic: 0.18 us -> 2.01 us  [well_step(): return (full + got[:full.shape[0]], keep + got[full.shape[0]:])]
    another operation x13 -> x14, other arithmetic: 49.6 us -> 50.8 us  [the longest x7 29.5 us: shards(): factor = jnp.linalg.cholesky(system)]
  transfers between devices with their start and end apart: 12 -> 12, of which waited for: 11 -> 10; matrix products, arithmetic and copies ran while one was open for 40% -> 41% of each run, Pallas kernels for 0% -> 0%
where the time goes in v3:
time: 137 us; the launch traced here: 136 us
  other arithmetic  61.1 us (45%)
  waiting for transfers between devices  28.5 us (21%)
  starting transfers between devices  17.3 us (13%)
  between operations  15.1 us (11%)
  matrix products  13.6 us (10%)
    another operation x7, other arithmetic, shards(): factor = jnp.linalg.cholesky(system)  29.5 us
    ppermute x11, waiting for transfers between devices, swap(): return lax.ppermute(x, axis, [(i, i ^ k) for i in range(size)])  28.5 us
    another operation x7, other arithmetic, shards(): lax.linalg.triangular_solve(factor, cross_mine, left_side=True, lower=Tru...  21.3 us
    ppermute x11, starting transfers between devices, swap(): return lax.ppermute(x, axis, [(i, i ^ k) for i in range(size)])  17.3 us
    dot_general x1, matrix products, shards(): lax.dot_general(jnp.concatenate([group_anom, group_innov], 1), tapered, (...  3.58 us
    dot_general x1, matrix products, shards(): jnp.einsum('vnc,mn->vmc', state_anom, space_t, precision=highest)  3.46 us
  transfers between devices with their start and end apart: 12, of which 10 were waited for; matrix products, arithmetic and copies ran while one was open for 41% of the time, Pallas kernels for 0%

profile of v3, /device:TPU:0, one launch (start us, length us, event | category | flops | bytes accessed | tf_op | source)
XLA Modules:
  0.0 136.1 jit_solution(9945510196024286035)
XLA Ops:
  8.1 1.0 subtract_multiply_fusion
  9.1 1.4 %fusion.30 = f32[200,200]{0,1:T(8,128)S(1)} fusion(f32[128,200]{0,1:T(8,128)S(1)} %get-tuple-element.52, f32[128,200]{0,1:T(8,128)} %param.7, f32[128]{0:T(128)S(1)} %get-tuple-element.45, f32[128]{0:T(128)S(1)} %get-tuple-element.61), kind=kOutput, calls=%fused_computation.54 | convolution fusion | flops 61491200 | bytes 365824 | tf_op jit(solution)/shard_map/dot_general | solution.py:75
  10.5 1.3 broadcast_select_fusion
  12.4 1.2 collective-permute-done
  13.6 1.0 select_add_fusion
  14.7 2.9 %collective-permute-start.1 = (f32[100,200]{0,1:T(8,128)S(1)}, f32[100,200]{0,1:T(8,128)S(1)}, u32[]{:S(2)}, u32[]{:S(2)}) collective-permute-start(f32[100,200]{0,1:T(8,128)S(1)} %slice_select_fusion.2), channel_id=1, source_target_pairs={{0,8},{8,0},{16,24},{24,16},{1,9},{9,1},{17,25},{25,17},{2,10},{10... | collective-permute-start | bytes 240008 | tf_op jit(solution)/shard_map/ppermute | solution.py:23
  17.6 3.2 %collective-permute-done.1 = f32[100,200]{0,1:T(8,128)S(1)} collective-permute-done((f32[100,200]{0,1:T(8,128)S(1)}, f32[100,200]{0,1:T(8,128)S(1)}, u32[]{:S(2)}, u32[]{:S(2)}) %collective-permute-start.1) | collective-permute-done | bytes 80032 | tf_op jit(solution)/shard_map/ppermute | solution.py:23
  21.0 1.8 %collective-permute-start.2 = (f32[50,200]{0,1:T(8,128)S(1)}, f32[50,200]{0,1:T(8,128)S(1)}, u32[]{:S(2)}, u32[]{:S(2)}) collective-permute-start(f32[50,200]{0,1:T(8,128)S(1)} %slice_select_fusion.1), channel_id=1, source_target_pairs={{0,16},{8,24},{16,0},{24,8},{1,17},{9,25},{17,1},{25,9},{2,18},{10... | collective-permute-start | bytes 120008 | tf_op jit(solution)/shard_map/ppermute | solution.py:23
  22.8 2.9 %collective-permute-done.2 = f32[50,200]{0,1:T(8,128)S(1)} collective-permute-done((f32[50,200]{0,1:T(8,128)S(1)}, f32[50,200]{0,1:T(8,128)S(1)}, u32[]{:S(2)}, u32[]{:S(2)}) %collective-permute-start.2) | collective-permute-done | bytes 40032 | tf_op jit(solution)/shard_map/ppermute | solution.py:23
  25.9 1.9 %collective-permute-start.3 = (f32[25,200]{0,1:T(8,128)S(1)}, f32[25,200]{0,1:T(8,128)S(1)}, u32[]{:S(2)}, u32[]{:S(2)}) collective-permute-start(f32[25,200]{0,1:T(8,128)S(1)} %slice_select_fusion), channel_id=1, source_target_pairs={{0,2},{1,3},{2,0},{3,1},{4,6},{5,7},{6,4},{7,5},{8,10},{9,11},{10,... | collective-permute-start | bytes 60008 | tf_op jit(solution)/shard_map/ppermute | solution.py:23
  27.8 2.8 %collective-permute-done.3 = f32[25,200]{0,1:T(8,128)S(1)} collective-permute-done((f32[25,200]{0,1:T(8,128)S(1)}, f32[25,200]{0,1:T(8,128)S(1)}, u32[]{:S(2)}, u32[]{:S(2)}) %collective-permute-start.3) | collective-permute-done | bytes 20032 | tf_op jit(solution)/shard_map/ppermute | solution.py:23
  30.7 3.3 %collective-permute-start.4 = (f32[25,200]{0,1:T(8,128)S(1)}, f32[25,200]{0,1:T(8,128)S(1)}, u32[]{:S(2)}, u32[]{:S(2)}) collective-permute-start(f32[25,200]{0,1:T(8,128)S(1)} %select_add_fusion.1), channel_id=1, source_target_pairs={{0,4},{1,5},{2,6},{3,7},{4,0},{5,1},{6,2},{7,3},{8,12},{9,13},{10,... | collective-permute-start | bytes 60008 | tf_op jit(solution)/shard_map/ppermute | solution.py:23
  34.7 3.0 %collective-permute-done.4 = f32[25,200]{0,1:T(8,128)S(1)} collective-permute-done((f32[25,200]{0,1:T(8,128)S(1)}, f32[25,200]{0,1:T(8,128)S(1)}, u32[]{:S(2)}, u32[]{:S(2)}) %collective-permute-start.4) | collective-permute-done | bytes 20032 | tf_op jit(solution)/shard_map/ppermute | solution.py:23
  38.6 3.9 %collective-permute-done.5 = f32[25,200]{0,1:T(8,128)S(1)} collective-permute-done((f32[25,200]{0,1:T(8,128)S(1)}, f32[25,200]{0,1:T(8,128)S(1)}, u32[]{:S(2)}, u32[]{:S(2)}) %collective-permute-start.5) | collective-permute-done | bytes 20032 | tf_op jit(solution)/shard_map/ppermute | solution.py:23
  42.6 1.6 %collective-permute-start.6 = (f32[50,200]{0,1:T(8,128)S(1)}, f32[50,200]{0,1:T(8,128)S(1)}, u32[]{:S(2)}, u32[]{:S(2)}) collective-permute-start(f32[50,200]{0,1:T(8,128)S(1)} %maximum_select_fusion.2), channel_id=1, source_target_pairs={{0,16},{8,24},{16,0},{24,8},{1,17},{9,25},{17,1},{25,9},{2,18},{10... | collective-permute-start | bytes 120008 | tf_op jit(solution)/shard_map/ppermute | solution.py:23
  44.8 2.5 %collective-permute-done.6 = f32[50,200]{0,1:T(8,128)S(1)} collective-permute-done((f32[50,200]{0,1:T(8,128)S(1)}, f32[50,200]{0,1:T(8,128)S(1)}, u32[]{:S(2)}, u32[]{:S(2)}) %collective-permute-start.6) | collective-permute-done | bytes 40032 | tf_op jit(solution)/shard_map/ppermute | solution.py:23
  47.5 1.6 %collective-permute-start.7 = (f32[100,200]{0,1:T(8,128)S(1)}, f32[100,200]{0,1:T(8,128)S(1)}, u32[]{:S(2)}, u32[]{:S(2)}) collective-permute-start(f32[100,200]{0,1:T(8,128)S(1)} %maximum_select_fusion.3), channel_id=1, source_target_pairs={{0,8},{8,0},{16,24},{24,16},{1,9},{9,1},{17,25},{25,17},{2,10},{10... | collective-permute-start | bytes 240008 | tf_op jit(solution)/shard_map/ppermute | solution.py:23
  49.1 3.2 %collective-permute-done.7 = f32[100,200]{0,1:T(8,128)S(1)} collective-permute-done((f32[100,200]{0,1:T(8,128)S(1)}, f32[100,200]{0,1:T(8,128)S(1)}, u32[]{:S(2)}, u32[]{:S(2)}) %collective-permute-start.7) | collective-permute-done | bytes 80032 | tf_op jit(solution)/shard_map/ppermute | solution.py:23
  52.5 1.4 %collective-permute-done.8 = f32[200,200]{0,1:T(8,128)S(1)} collective-permute-done((f32[200,200]{0,1:T(8,128)S(1)}, f32[200,200]{0,1:T(8,128)S(1)}, u32[]{:S(2)}, u32[]{:S(2)}) %collective-permute-start.8) | collective-permute-done | bytes 160032 | tf_op jit(solution)/shard_map/ppermute | solution.py:23
  54.5 11.7 %cholesky.51 = f32[128,128]{1,0:T(8,128)S(1)} custom-call(f32[128,128]{1,0:T(8,128)S(1)} %cholesky.124), custom_call_target="Cholesky" | custom-call | tf_op jit(solution)/shard_map/jit(cholesky)/cholesky | solution.py:87
  66.2 9.8 %custom-call.16 = f32[1,128,128]{1,2,0:T(8,128)S(1)} custom-call(f32[1,128,128]{2,1,0:T(8,128)S(1)} %get-tuple-element.54), custom_call_target="InvertDiagBlocksLowerTriangular" | custom-call | tf_op jit(solution)/shard_map/jit(cholesky)/cholesky | solution.py:87
  76.5 6.6 %cholesky.110 = f32[72,72]{1,0:T(8,128)S(1)} custom-call(f32[72,72]{1,0:T(8,128)S(1)} %convolution_subtract_fusion), custom_call_target="Cholesky" | custom-call | tf_op jit(solution)/shard_map/jit(cholesky)/cholesky | solution.py:87
  86.6 3.6 %fusion.3 = f32[400,200]{0,1:T(8,128)S(1)} fusion(f32[1024,401]{0,1:T(8,128)} %all-gather.2.cloned.1.call-done, f32[1024]{0:T(1024)S(1)} %bitcast.41), kind=kOutput, calls=%fused_computation.3 | convolution fusion | flops 983244800 | bytes 2781696 | tf_op jit(solution)/shard_map/dot_general | solution.py:99
  91.3 1.5 %collective-permute-start.9 = (f32[300,200]{0,1:T(8,128)}, f32[300,200]{0,1:T(8,128)}, u32[]{:S(2)}, u32[]{:S(2)}) collective-permute-start(f32[300,200]{0,1:T(8,128)} %pad_maximum_fusion), channel_id=1, source_target_pairs={{0,16},{8,24},{16,0},{24,8},{1,17},{9,25},{17,1},{25,9},{2,18},{10... | collective-permute-start | bytes 720008 | tf_op jit(solution)/shard_map/ppermute | solution.py:23
  93.6 20.5 %custom-call.17 = f32[2,128,128]{1,2,0:T(8,128)S(1)} custom-call(f32[2,128,128]{2,1,0:T(8,128)} %pad_maximum_fusion.3), custom_call_target="InvertDiagBlocksLowerTriangular" | custom-call | tf_op jit(solution)/shard_map/triangular_solve | solution.py:109
  114.8 1.1 slice_add_fusion.5
  115.9 1.0 slice_add_fusion.2
  116.8 1.0 fusion.45
  118.3 1.6 %collective-permute-start.10 = (f32[250,200]{0,1:T(8,128)S(1)}, f32[250,200]{0,1:T(8,128)S(1)}, u32[]{:S(2)}, u32[]{:S(2)}) collective-permute-start(f32[250,200]{0,1:T(8,128)S(1)} %pad_maximum_fusion.2), channel_id=1, source_target_pairs={{0,8},{8,0},{16,24},{24,16},{1,9},{9,1},{17,25},{25,17},{2,10},{10... | collective-permute-start | bytes 600008 | tf_op jit(solution)/shard_map/ppermute | solution.py:23
  119.8 1.0 fusion.37
  120.9 4.3 %collective-permute-done.10 = f32[250,200]{0,1:T(8,128)S(1)} collective-permute-done((f32[250,200]{0,1:T(8,128)S(1)}, f32[250,200]{0,1:T(8,128)S(1)}, u32[]{:S(2)}, u32[]{:S(2)}) %collective-permute-start.10) | collective-permute-done | bytes 200032 | tf_op jit(solution)/shard_map/ppermute | solution.py:23
  125.8 3.5 %fusion.8 = f32[3,50,1024]{2,1,0:T(8,128)} fusion(f32[3,200,1024]{2,1,0:T(8,128)S(1)} %copy-done, f32[3,1024]{1,0:T(4,128)} %broadcast_multiply_fusion, s32[]{:T(128)S(6)} %select_n.146, f32[50,200]{0,1:T(8,128)S(1)} %fusion.16, f32[250,200]{0,1:T(8,128)S(1)} %collective-permute-done.10, f32[100,200]{0,1:T(8,128)S(1)} %slice_add_fusion.5, pred[]{:T(512)S(6)} %eq.32), kind=kOutput, calls=%fused_computation.6 | convolution fusion | flops 370052416 | bytes 4182021 | tf_op jit(solution)/shard_map/vnc,mn->vmc/dot_general | solution.py:123
  (65 shorter events, 12.1 us)
Async XLA Ops:
  6.5 79.2 %all-gather.2.cloned.1.call-start = ((), (), s32[]{:S(2)}) async-start(), calls=%async_computation | async-start | bytes 1880064 | tf_op jit(solution)/shard_map/all_gather | solution.py:89
  9.1 29.3 %copy-start = (f32[3,200,1024]{2,1,0:T(8,128)S(1)}, f32[3,200,1024]{2,1,0:T(8,128)}, u32[]{:S(2)}) copy-start(f32[3,200,1024]{2,1,0:T(8,128)} %param.6) | copy-start | bytes 7372804
  11.9 1.7 %collective-permute-start = (f32[200,200]{0,1:T(8,128)S(1)}, f32[200,200]{0,1:T(8,128)}, u32[]{:S(2)}, u32[]{:S(2)}) collective-permute-start(f32[200,200]{0,1:T(8,128)S(1)} %get-tuple-element.57), channel_id=1, source_target_pairs={{0,1},{1,0},{2,3},{3,2},{4,5},{5,4},{6,7},{7,6},{8,9},{9,8},{10,11... | collective-permute-start | bytes 480008 | tf_op jit(solution)/shard_map/ppermute | solution.py:23
  14.7 6.1 %collective-permute-start.1 = (f32[100,200]{0,1:T(8,128)S(1)}, f32[100,200]{0,1:T(8,128)S(1)}, u32[]{:S(2)}, u32[]{:S(2)}) collective-permute-start(f32[100,200]{0,1:T(8,128)S(1)} %slice_select_fusion.2), channel_id=1, source_target_pairs={{0,8},{8,0},{16,24},{24,16},{1,9},{9,1},{17,25},{25,17},{2,10},{10... | collective-permute-start | bytes 240008 | tf_op jit(solution)/shard_map/ppermute | solution.py:23
  21.0 4.7 %collective-permute-start.2 = (f32[50,200]{0,1:T(8,128)S(1)}, f32[50,200]{0,1:T(8,128)S(1)}, u32[]{:S(2)}, u32[]{:S(2)}) collective-permute-start(f32[50,200]{0,1:T(8,128)S(1)} %slice_select_fusion.1), channel_id=1, source_target_pairs={{0,16},{8,24},{16,0},{24,8},{1,17},{9,25},{17,1},{25,9},{2,18},{10... | collective-permute-start | bytes 120008 | tf_op jit(solution)/shard_map/ppermute | solution.py:23
  25.8 23.3 %copy-start.2 = (s32[1,8]{1,0:T(1,128)S(1)}, s32[1,8]{1,0:T(1,128)}, u32[]{:S(2)}) copy-start(s32[1,8]{1,0:T(1,128)} %param.11) | copy-start | bytes 100
  25.8 23.2 %copy-start.3 = (s32[1,8]{1,0:T(1,128)S(1)}, s32[1,8]{1,0:T(1,128)}, u32[]{:S(2)}) copy-start(s32[1,8]{1,0:T(1,128)} %param.10) | copy-start | bytes 100
  25.9 4.7 %collective-permute-start.3 = (f32[25,200]{0,1:T(8,128)S(1)}, f32[25,200]{0,1:T(8,128)S(1)}, u32[]{:S(2)}, u32[]{:S(2)}) collective-permute-start(f32[25,200]{0,1:T(8,128)S(1)} %slice_select_fusion), channel_id=1, source_target_pairs={{0,2},{1,3},{2,0},{3,1},{4,6},{5,7},{6,4},{7,5},{8,10},{9,11},{10,... | collective-permute-start | bytes 60008 | tf_op jit(solution)/shard_map/ppermute | solution.py:23
  30.7 7.0 %collective-permute-start.4 = (f32[25,200]{0,1:T(8,128)S(1)}, f32[25,200]{0,1:T(8,128)S(1)}, u32[]{:S(2)}, u32[]{:S(2)}) collective-permute-start(f32[25,200]{0,1:T(8,128)S(1)} %select_add_fusion.1), channel_id=1, source_target_pairs={{0,4},{1,5},{2,6},{3,7},{4,0},{5,1},{6,2},{7,3},{8,12},{9,13},{10,... | collective-permute-start | bytes 60008 | tf_op jit(solution)/shard_map/ppermute | solution.py:23
  37.8 4.7 %collective-permute-start.5 = (f32[25,200]{0,1:T(8,128)S(1)}, f32[25,200]{0,1:T(8,128)S(1)}, u32[]{:S(2)}, u32[]{:S(2)}) collective-permute-start(f32[25,200]{0,1:T(8,128)S(1)} %add.95), channel_id=1, source_target_pairs={{0,2},{1,3},{2,0},{3,1},{4,6},{5,7},{6,4},{7,5},{8,10},{9,11},{10,... | collective-permute-start | bytes 60008 | tf_op jit(solution)/shard_map/ppermute | solution.py:23
  42.6 4.7 %collective-permute-start.6 = (f32[50,200]{0,1:T(8,128)S(1)}, f32[50,200]{0,1:T(8,128)S(1)}, u32[]{:S(2)}, u32[]{:S(2)}) collective-permute-start(f32[50,200]{0,1:T(8,128)S(1)} %maximum_select_fusion.2), channel_id=1, source_target_pairs={{0,16},{8,24},{16,0},{24,8},{1,17},{9,25},{17,1},{25,9},{2,18},{10... | collective-permute-start | bytes 120008 | tf_op jit(solution)/shard_map/ppermute | solution.py:23
  47.5 4.7 %collective-permute-start.7 = (f32[100,200]{0,1:T(8,128)S(1)}, f32[100,200]{0,1:T(8,128)S(1)}, u32[]{:S(2)}, u32[]{:S(2)}) collective-permute-start(f32[100,200]{0,1:T(8,128)S(1)} %maximum_select_fusion.3), channel_id=1, source_target_pairs={{0,8},{8,0},{16,24},{24,16},{1,9},{9,1},{17,25},{25,17},{2,10},{10... | collective-permute-start | bytes 240008 | tf_op jit(solution)/shard_map/ppermute | solution.py:23
  52.4 1.5 %collective-permute-start.8 = (f32[200,200]{0,1:T(8,128)S(1)}, f32[200,200]{0,1:T(8,128)S(1)}, u32[]{:S(2)}, u32[]{:S(2)}) collective-permute-start(f32[200,200]{0,1:T(8,128)S(1)} %maximum_select_fusion.1), channel_id=1, source_target_pairs={{0,1},{1,0},{2,3},{3,2},{4,5},{5,4},{6,7},{7,6},{8,9},{9,8},{10,11... | collective-permute-start | bytes 480008 | tf_op jit(solution)/shard_map/ppermute | solution.py:23
  91.3 23.5 %collective-permute-start.9 = (f32[300,200]{0,1:T(8,128)}, f32[300,200]{0,1:T(8,128)}, u32[]{:S(2)}, u32[]{:S(2)}) collective-permute-start(f32[300,200]{0,1:T(8,128)} %pad_maximum_fusion), channel_id=1, source_target_pairs={{0,16},{8,24},{16,0},{24,8},{1,17},{9,25},{17,1},{25,9},{2,18},{10... | collective-permute-start | bytes 720008 | tf_op jit(solution)/shard_map/ppermute | solution.py:23
  114.1 0.7 copy-start.1
  118.3 6.9 %collective-permute-start.10 = (f32[250,200]{0,1:T(8,128)S(1)}, f32[250,200]{0,1:T(8,128)S(1)}, u32[]{:S(2)}, u32[]{:S(2)}) collective-permute-start(f32[250,200]{0,1:T(8,128)S(1)} %pad_maximum_fusion.2), channel_id=1, source_target_pairs={{0,8},{8,0},{16,24},{24,16},{1,9},{9,1},{17,25},{25,17},{2,10},{10... | collective-permute-start | bytes 600008 | tf_op jit(solution)/shard_map/ppermute | solution.py:23
Sparse Core Ops, SparseCore 0:
  38.7 29.2 all-gather.1

commit v4 on v3

--- a/solution.py
+++ b/solution.py
@@ -63,6 +63,44 @@
     return full + got[: full.shape[0]], keep + got[full.shape[0]:]
 
 
+def line_gather(packed, taper_row):
+    size = lax.axis_size("tile")
+    me = lax.axis_index("tile")
+    chips = size // 2
+    z = me // 2
+    rows = packed.shape[0]
+    partner_row = swap(taper_row, "tile", 1)
+    left, right = [packed], [packed]
+    for _ in range(1, chips):
+        left.append(lax.ppermute(left[-1], "tile", [(i, i + 2) for i in range(size - 2)]))
+        right.append(lax.ppermute(right[-1], "tile", [(i, i - 2) for i in range(2, size)]))
+    pieces, sources = [packed], [me]
+    for k in range(1, chips):
+        ahead = z + k <= chips - 1
+        pieces.append(jnp.where(ahead, right[k], left[chips - k]))
+        sources.append(jnp.where(ahead, me + 2 * k, me - 2 * (chips - k)))
+    row_tapers = []
+    for row in (taper_row, partner_row):
+        per_piece = [
+            jnp.broadcast_to(lax.dynamic_index_in_dim(row, (src * rows) // BLOCK, 0, False), (rows,))
+            for src in sources
+        ]
+        row_tapers.append(jnp.concatenate(per_piece, 0))
+    return pieces, row_tapers
+
+
+def tapered_sums(pieces, row_tapers, members, precision):
+    group = jnp.concatenate(pieces, 0)
+    anom, innov, weight = group[:, :members], group[:, members : 2 * members], group[:, 2 * members]
+    cols = [(row_taper * weight)[:, None] * anom for row_taper in row_tapers]
+    return lax.dot_general(
+        jnp.concatenate([anom, innov], 1),
+        jnp.concatenate(cols, 1),
+        (((0,), (0,)), ((), ())),
+        precision=precision,
+    )
+
+
 def shards(prior_state, pred_data, obs_pert, obs_std, loc_mask, taper_level):
     highest = lax.Precision.HIGHEST
     members = pred_data.shape[1]
@@ -86,25 +124,22 @@
     system = jnp.eye(members, dtype=jnp.float32) + gram_matrix
     factor = jnp.linalg.cholesky(system)
 
-    group = lax.all_gather(packed, "tile", axis=0, tiled=True)
-    factor, group = lax.optimization_barrier((factor, group))
-    group_anom, group_innov, group_weight = (
-        group[:, :members],
-        group[:, members : 2 * members],
-        group[:, 2 * members],
-    )
     taper_row = loc_mask[0].astype(jnp.float32) * taper_level[0].astype(jnp.float32) / 4.0
-    row_taper = jnp.repeat(taper_row, BLOCK)
-    tapered = (row_taper * group_weight)[:, None] * group_anom
-    both = lax.dot_general(
-        jnp.concatenate([group_anom, group_innov], 1),
-        tapered,
-        (((0,), (0,)), ((), ())),
-        precision=highest,
-    )
+    if lax.axis_size("tile") == 8:
+        pieces, weights = line_gather(packed, taper_row)
+        factor, pieces = lax.optimization_barrier((factor, pieces))
+        both = tapered_sums(pieces, weights, members, highest)
+        mine, theirs = both[:, :members], both[:, members:]
+        both = mine + swap(theirs, "tile", 1)
+    else:
+        group = lax.all_gather(packed, "tile", axis=0, tiled=True)
+        factor, group = lax.optimization_barrier((factor, group))
+        row_taper = jnp.repeat(taper_row, BLOCK)
+        both = tapered_sums([group], [row_taper], members, highest)
     taper_gram, taper_cross_t = both[:members], both[members:]
+    factor, taper_gram, taper_cross_t = lax.optimization_barrier((factor, taper_gram, taper_cross_t))
+
     steps = list(reversed(axis_bits("well")))
-    factor, taper_gram, taper_cross_t = lax.optimization_barrier((factor, taper_gram, taper_cross_t))
     taper_gram, cross_t_mine = well_step(taper_gram, taper_cross_t, *steps[0])
     middle = lax.linalg.triangular_solve(
         factor, cross_mine, left_side=True, lower=True, transpose_a=False

time: 137 us -> 149 us (1.088)
  starting transfers between devices: 17.3 us -> 36.1 us
  between operations: 15.1 us -> 2.01 us
  local copies, waits for them, and re-layouts: 0.44 us -> 6.72 us
  waiting for transfers between devices: 28.5 us -> 31.9 us
  matrix products: 13.6 us -> 10.6 us
    ppermute x0 -> x6, starting transfers between devices: none -> 19.1 us  [the longest x3 15.2 us: line_gather(): lax.ppermute(left[-1], 'tile', [(i, i + 2) for i in range(size - 2)])]
    broadcast_in_dim x1 -> x8, local copies, waits for them, and re-layouts: 0.07 us -> 4.95 us  [line_gather(): jnp.broadcast_to(lax.dynamic_index_in_dim(row, src * rows // BLOCK, 0, Fa...]
    ppermute x0 -> x6, waiting for transfers between devices: none -> 3 us  [the longest x3 1.73 us: line_gather(): lax.ppermute(right[-1], 'tile', [(i, i - 2) for i in range(2, size)])]
    dot_general x1, matrix products: 3.58 us -> 1.47 us  [tapered_sums(): lax.dot_general(jnp.concatenate([anom, innov], 1), jnp.concatenate(cols,...]
    select_n x0 -> x3, other arithmetic: none -> 1.95 us  [line_gather(): pieces.append(jnp.where(ahead, right[k], left[chips - k]))]
    another operation x3, matrix products: 2.2 us -> 0.6 us  [shards(): lax.linalg.triangular_solve(factor, middle, left_side=True, lower=True, t...]
    another operation x3, matrix products: 0.66 us -> 2.19 us  [shards(): lax.linalg.triangular_solve(factor, cross_mine, left_side=True, lower=Tru...]
    ppermute x11 -> x13, waiting for transfers between devices: 28.5 us -> 28.9 us  [swap(): return lax.ppermute(x, axis, [(i, i ^ k) for i in range(size)])]
  transfers between devices with their start and end apart: 12 -> 19, of which waited for: 10 -> 11; matrix products, arithmetic and copies ran while one was open for 41% -> 41% of each run, Pallas kernels for 0% -> 0%
where the time goes in v4:
time: 149 us; the launch traced here: 148 us
  other arithmetic  60.5 us (41%)
  starting transfers between devices  36.1 us (24%)
  waiting for transfers between devices  31.9 us (21%)
  matrix products  10.6 us (7%)
  local copies, waits for them, and re-layouts  6.72 us (5%)
  between operations  2.01 us (1%)
    another operation x7, other arithmetic, shards(): factor = jnp.linalg.cholesky(system)  29.5 us
    ppermute x13, waiting for transfers between devices, swap(): return lax.ppermute(x, axis, [(i, i ^ k) for i in range(size)])  28.9 us
    another operation x7, other arithmetic, shards(): lax.linalg.triangular_solve(factor, cross_mine, left_side=True, lower=Tru...  19.8 us
    ppermute x13, starting transfers between devices, swap(): return lax.ppermute(x, axis, [(i, i ^ k) for i in range(size)])  17 us
    ppermute x3, starting transfers between devices, line_gather(): lax.ppermute(left[-1], 'tile', [(i, i + 2) for i in range(size - 2)])  15.2 us
    broadcast_in_dim x8, local copies, waits for them, and re-layouts, line_gather(): jnp.broadcast_to(lax.dynamic_index_in_dim(row, src * rows // BLOCK, 0, Fa...  4.95 us
    ppermute x3, starting transfers between devices, line_gather(): lax.ppermute(right[-1], 'tile', [(i, i - 2) for i in range(2, size)])  3.86 us
  transfers between devices with their start and end apart: 19, of which 11 were waited for; matrix products, arithmetic and copies ran while one was open for 41% of the time, Pallas kernels for 0%

profile of v4, /device:TPU:0, one launch (start us, length us, event | category | flops | bytes accessed | tf_op | source)
XLA Modules:
  0.0 147.8 jit_solution(674048057561919773)
XLA Ops:
  2.6 1.2 fusion.30
  3.8 1.3 broadcast_select_fusion.3
  5.7 1.2 collective-permute-done
  8.1 2.9 %collective-permute-start.1 = (f32[100,200]{0,1:T(8,128)S(1)}, f32[100,200]{0,1:T(8,128)S(1)}, u32[]{:S(2)}, u32[]{:S(2)}) collective-permute-start(f32[100,200]{0,1:T(8,128)S(1)} %slice_select_fusion.2), channel_id=1, source_target_pairs={{0,8},{8,0},{16,24},{24,16},{1,9},{9,1},{17,25},{25,17},{2,10},{10... | collective-permute-start | bytes 240008 | tf_op jit(solution)/shard_map/ppermute | solution.py:23
  11.1 3.2 %collective-permute-done.1 = f32[100,200]{0,1:T(8,128)S(1)} collective-permute-done((f32[100,200]{0,1:T(8,128)S(1)}, f32[100,200]{0,1:T(8,128)S(1)}, u32[]{:S(2)}, u32[]{:S(2)}) %collective-permute-start.1) | collective-permute-done | bytes 80032 | tf_op jit(solution)/shard_map/ppermute | solution.py:23
  14.4 1.8 %collective-permute-start.2 = (f32[50,200]{0,1:T(8,128)S(1)}, f32[50,200]{0,1:T(8,128)S(1)}, u32[]{:S(2)}, u32[]{:S(2)}) collective-permute-start(f32[50,200]{0,1:T(8,128)S(1)} %slice_select_fusion.1), channel_id=1, source_target_pairs={{0,16},{8,24},{16,0},{24,8},{1,17},{9,25},{17,1},{25,9},{2,18},{10... | collective-permute-start | bytes 120008 | tf_op jit(solution)/shard_map/ppermute | solution.py:23
  16.3 2.9 %collective-permute-done.2 = f32[50,200]{0,1:T(8,128)S(1)} collective-permute-done((f32[50,200]{0,1:T(8,128)S(1)}, f32[50,200]{0,1:T(8,128)S(1)}, u32[]{:S(2)}, u32[]{:S(2)}) %collective-permute-start.2) | collective-permute-done | bytes 40032 | tf_op jit(solution)/shard_map/ppermute | solution.py:23
  19.4 1.9 %collective-permute-start.3 = (f32[25,200]{0,1:T(8,128)S(1)}, f32[25,200]{0,1:T(8,128)S(1)}, u32[]{:S(2)}, u32[]{:S(2)}) collective-permute-start(f32[25,200]{0,1:T(8,128)S(1)} %slice_select_fusion), channel_id=1, source_target_pairs={{0,2},{1,3},{2,0},{3,1},{4,6},{5,7},{6,4},{7,5},{8,10},{9,11},{10,... | collective-permute-start | bytes 60008 | tf_op jit(solution)/shard_map/ppermute | solution.py:23
  21.3 2.8 %collective-permute-done.3 = f32[25,200]{0,1:T(8,128)S(1)} collective-permute-done((f32[25,200]{0,1:T(8,128)S(1)}, f32[25,200]{0,1:T(8,128)S(1)}, u32[]{:S(2)}, u32[]{:S(2)}) %collective-permute-start.3) | collective-permute-done | bytes 20032 | tf_op jit(solution)/shard_map/ppermute | solution.py:23
  24.2 3.3 %collective-permute-start.4 = (f32[25,200]{0,1:T(8,128)S(1)}, f32[25,200]{0,1:T(8,128)S(1)}, u32[]{:S(2)}, u32[]{:S(2)}) collective-permute-start(f32[25,200]{0,1:T(8,128)S(1)} %select_add_fusion.1), channel_id=1, source_target_pairs={{0,4},{1,5},{2,6},{3,7},{4,0},{5,1},{6,2},{7,3},{8,12},{9,13},{10,... | collective-permute-start | bytes 60008 | tf_op jit(solution)/shard_map/ppermute | solution.py:23
  27.5 3.7 %collective-permute-done.4 = f32[25,200]{0,1:T(8,128)S(1)} collective-permute-done((f32[25,200]{0,1:T(8,128)S(1)}, f32[25,200]{0,1:T(8,128)S(1)}, u32[]{:S(2)}, u32[]{:S(2)}) %collective-permute-start.4) | collective-permute-done | bytes 20032 | tf_op jit(solution)/shard_map/ppermute | solution.py:23
  31.8 4.1 %collective-permute-done.5 = f32[25,200]{0,1:T(8,128)S(1)} collective-permute-done((f32[25,200]{0,1:T(8,128)S(1)}, f32[25,200]{0,1:T(8,128)S(1)}, u32[]{:S(2)}, u32[]{:S(2)}) %collective-permute-start.5) | collective-permute-done | bytes 20032 | tf_op jit(solution)/shard_map/ppermute | solution.py:23
  36.1 1.6 %collective-permute-start.6 = (f32[50,200]{0,1:T(8,128)S(1)}, f32[50,200]{0,1:T(8,128)S(1)}, u32[]{:S(2)}, u32[]{:S(2)}) collective-permute-start(f32[50,200]{0,1:T(8,128)S(1)} %maximum_select_fusion.2), channel_id=1, source_target_pairs={{0,16},{8,24},{16,0},{24,8},{1,17},{9,25},{17,1},{25,9},{2,18},{10... | collective-permute-start | bytes 120008 | tf_op jit(solution)/shard_map/ppermute | solution.py:23
  37.7 3.1 %collective-permute-done.6 = f32[50,200]{0,1:T(8,128)S(1)} collective-permute-done((f32[50,200]{0,1:T(8,128)S(1)}, f32[50,200]{0,1:T(8,128)S(1)}, u32[]{:S(2)}, u32[]{:S(2)}) %collective-permute-start.6) | collective-permute-done | bytes 40032 | tf_op jit(solution)/shard_map/ppermute | solution.py:23
  40.9 1.6 %collective-permute-start.7 = (f32[100,200]{0,1:T(8,128)S(1)}, f32[100,200]{0,1:T(8,128)S(1)}, u32[]{:S(2)}, u32[]{:S(2)}) collective-permute-start(f32[100,200]{0,1:T(8,128)S(1)} %maximum_select_fusion.3), channel_id=1, source_target_pairs={{0,8},{8,0},{16,24},{24,16},{1,9},{9,1},{17,25},{25,17},{2,10},{10... | collective-permute-start | bytes 240008 | tf_op jit(solution)/shard_map/ppermute | solution.py:23
  42.5 1.3 collective-permute-start.9
  43.8 5.2 %collective-permute-start.10 = (f32[128,401]{0,1:T(8,128)S(1)}, f32[128,401]{0,1:T(8,128)}, u32[]{:S(2)}, u32[]{:S(2)}) collective-permute-start(f32[128,401]{0,1:T(8,128)S(1)} %pad_maximum_fusion.1), channel_id=1, source_target_pairs={{0,2},{1,3},{2,4},{3,5},{4,6},{5,7},{8,10},{9,11},{10,12},{11,13},... | collective-permute-start | bytes 615944 | tf_op jit(solution)/shard_map/ppermute | solution.py:75
  56.5 1.3 collective-permute-start.13
  57.8 5.2 %collective-permute-start.11 = (f32[128,401]{0,1:T(8,128)}, f32[128,401]{0,1:T(8,128)}, u32[]{:S(2)}, u32[]{:S(2)}) collective-permute-start(f32[128,401]{0,1:T(8,128)} %collective-permute-done.10), channel_id=1, source_target_pairs={{0,2},{1,3},{2,4},{3,5},{4,6},{5,7},{8,10},{9,11},{10,12},{11,13},... | collective-permute-start | bytes 615944 | tf_op jit(solution)/shard_map/ppermute | solution.py:75
  64.2 11.7 %cholesky.51 = f32[128,128]{1,0:T(8,128)S(1)} custom-call(f32[128,128]{1,0:T(8,128)S(1)} %cholesky.124), custom_call_target="Cholesky" | custom-call | tf_op jit(solution)/shard_map/jit(cholesky)/cholesky | solution.py:125
  76.0 9.8 %custom-call.16 = f32[1,128,128]{1,2,0:T(8,128)S(1)} custom-call(f32[1,128,128]{2,1,0:T(8,128)S(1)} %get-tuple-element.64), custom_call_target="InvertDiagBlocksLowerTriangular" | custom-call | tf_op jit(solution)/shard_map/jit(cholesky)/cholesky | solution.py:125
  86.2 6.6 %cholesky.110 = f32[72,72]{1,0:T(8,128)S(1)} custom-call(f32[72,72]{1,0:T(8,128)S(1)} %convolution_subtract_fusion), custom_call_target="Cholesky" | custom-call | tf_op jit(solution)/shard_map/jit(cholesky)/cholesky | solution.py:125
  95.6 1.3 collective-permute-start.14
  96.9 4.7 %collective-permute-start.12 = (f32[128,401]{0,1:T(8,128)}, f32[128,401]{0,1:T(8,128)S(1)}, u32[]{:S(2)}, u32[]{:S(2)}) collective-permute-start(f32[128,401]{0,1:T(8,128)} %collective-permute-done.11), channel_id=1, source_target_pairs={{0,2},{1,3},{2,4},{3,5},{4,6},{5,7},{8,10},{9,11},{10,12},{11,13},... | collective-permute-start | bytes 615944 | tf_op jit(solution)/shard_map/ppermute | solution.py:75
  102.6 1.7 %collective-permute-done.14 = f32[128,401]{0,1:T(8,128)S(1)} collective-permute-done((f32[128,401]{0,1:T(8,128)}, f32[128,401]{0,1:T(8,128)S(1)}, u32[]{:S(2)}, u32[]{:S(2)}) %collective-permute-start.14) | collective-permute-done | bytes 205344 | tf_op jit(solution)/shard_map/ppermute | solution.py:76
  104.3 1.3 collective-permute-done.12
  106.8 1.5 fusion.11
  108.4 1.7 %collective-permute-done.16 = f32[400,200]{0,1:T(8,128)S(1)} collective-permute-done((f32[400,200]{0,1:T(8,128)S(1)}, f32[400,200]{0,1:T(8,128)S(1)}, u32[]{:S(2)}, u32[]{:S(2)}) %collective-permute-start.16) | collective-permute-done | bytes 320032 | tf_op jit(solution)/shard_map/ppermute | solution.py:23
  111.3 1.5 %collective-permute-start.17 = (f32[300,200]{0,1:T(8,128)}, f32[300,200]{0,1:T(8,128)}, u32[]{:S(2)}, u32[]{:S(2)}) collective-permute-start(f32[300,200]{0,1:T(8,128)} %pad_maximum_fusion), channel_id=1, source_target_pairs={{0,16},{8,24},{16,0},{24,8},{1,17},{9,25},{17,1},{25,9},{2,18},{10... | collective-permute-start | bytes 720008 | tf_op jit(solution)/shard_map/ppermute | solution.py:23
  112.9 19.7 %custom-call.17 = f32[2,128,128]{1,2,0:T(8,128)S(1)} custom-call(f32[2,128,128]{2,1,0:T(8,128)S(1)} %pad_maximum_fusion.3), custom_call_target="InvertDiagBlocksLowerTriangular" | custom-call | tf_op jit(solution)/shard_map/triangular_solve | solution.py:144
  138.4 6.1 %collective-permute-done.18 = f32[250,200]{0,1:T(8,128)S(1)} collective-permute-done((f32[250,200]{0,1:T(8,128)S(1)}, f32[250,200]{0,1:T(8,128)S(1)}, u32[]{:S(2)}, u32[]{:S(2)}) %collective-permute-start.18) | collective-permute-done | bytes 200032 | tf_op jit(solution)/shard_map/ppermute | solution.py:23
  145.1 2.7 %fusion.6 = f32[3,50,1024]{2,1,0:T(8,128)} fusion(f32[3,200,1024]{2,1,0:T(8,128)S(1)} %copy-done, f32[3,1024]{1,0:T(4,128)S(1)} %broadcast_multiply_fusion, s32[]{:T(128)S(6)} %select_n.209, f32[50,200]{0,1:T(8,128)S(1)} %fusion.16, f32[250,200]{0,1:T(8,128)S(1)} %collective-permute-done.18, f32[100,200]{0,1:T(8,128)S(1)} %slice_add_fusion.6, pred[]{:T(512)S(6)} %eq.32), kind=kOutput, calls=%fused_computation.4 | convolution fusion | flops 370052416 | bytes 4186117 | tf_op jit(solution)/shard_map/vnc,mn->vmc/dot_general | solution.py:158
  (103 shorter events, 25.7 us)
Async XLA Ops:
  5.2 44.1 %copy-start.1 = (s32[1,8]{1,0:T(1,128)S(1)}, s32[1,8]{1,0:T(1,128)}, u32[]{:S(2)}) copy-start(s32[1,8]{1,0:T(1,128)} %param.11) | copy-start | bytes 100
  5.2 44.1 %copy-start.2 = (s32[1,8]{1,0:T(1,128)S(1)}, s32[1,8]{1,0:T(1,128)}, u32[]{:S(2)}) copy-start(s32[1,8]{1,0:T(1,128)} %param.10) | copy-start | bytes 100
  5.2 1.7 %collective-permute-start = (f32[200,200]{0,1:T(8,128)S(1)}, f32[200,200]{0,1:T(8,128)}, u32[]{:S(2)}, u32[]{:S(2)}) collective-permute-start(f32[200,200]{0,1:T(8,128)S(1)} %get-tuple-element.75), channel_id=1, source_target_pairs={{0,1},{1,0},{2,3},{3,2},{4,5},{5,4},{6,7},{7,6},{8,9},{9,8},{10,11... | collective-permute-start | bytes 480008 | tf_op jit(solution)/shard_map/ppermute | solution.py:23
  6.9 46.1 %copy-start = (f32[3,200,1024]{2,1,0:T(8,128)S(1)}, f32[3,200,1024]{2,1,0:T(8,128)}, u32[]{:S(2)}) copy-start(f32[3,200,1024]{2,1,0:T(8,128)} %param.6) | copy-start | bytes 7372804
  8.1 6.1 %collective-permute-start.1 = (f32[100,200]{0,1:T(8,128)S(1)}, f32[100,200]{0,1:T(8,128)S(1)}, u32[]{:S(2)}, u32[]{:S(2)}) collective-permute-start(f32[100,200]{0,1:T(8,128)S(1)} %slice_select_fusion.2), channel_id=1, source_target_pairs={{0,8},{8,0},{16,24},{24,16},{1,9},{9,1},{17,25},{25,17},{2,10},{10... | collective-permute-start | bytes 240008 | tf_op jit(solution)/shard_map/ppermute | solution.py:23
  14.4 4.7 %collective-permute-start.2 = (f32[50,200]{0,1:T(8,128)S(1)}, f32[50,200]{0,1:T(8,128)S(1)}, u32[]{:S(2)}, u32[]{:S(2)}) collective-permute-start(f32[50,200]{0,1:T(8,128)S(1)} %slice_select_fusion.1), channel_id=1, source_target_pairs={{0,16},{8,24},{16,0},{24,8},{1,17},{9,25},{17,1},{25,9},{2,18},{10... | collective-permute-start | bytes 120008 | tf_op jit(solution)/shard_map/ppermute | solution.py:23
  19.4 4.7 %collective-permute-start.3 = (f32[25,200]{0,1:T(8,128)S(1)}, f32[25,200]{0,1:T(8,128)S(1)}, u32[]{:S(2)}, u32[]{:S(2)}) collective-permute-start(f32[25,200]{0,1:T(8,128)S(1)} %slice_select_fusion), channel_id=1, source_target_pairs={{0,2},{1,3},{2,0},{3,1},{4,6},{5,7},{6,4},{7,5},{8,10},{9,11},{10,... | collective-permute-start | bytes 60008 | tf_op jit(solution)/shard_map/ppermute | solution.py:23
  24.2 7.0 %collective-permute-start.4 = (f32[25,200]{0,1:T(8,128)S(1)}, f32[25,200]{0,1:T(8,128)S(1)}, u32[]{:S(2)}, u32[]{:S(2)}) collective-permute-start(f32[25,200]{0,1:T(8,128)S(1)} %select_add_fusion.1), channel_id=1, source_target_pairs={{0,4},{1,5},{2,6},{3,7},{4,0},{5,1},{6,2},{7,3},{8,12},{9,13},{10,... | collective-permute-start | bytes 60008 | tf_op jit(solution)/shard_map/ppermute | solution.py:23
  31.2 4.7 %collective-permute-start.5 = (f32[25,200]{0,1:T(8,128)S(1)}, f32[25,200]{0,1:T(8,128)S(1)}, u32[]{:S(2)}, u32[]{:S(2)}) collective-permute-start(f32[25,200]{0,1:T(8,128)S(1)} %add.140), channel_id=1, source_target_pairs={{0,2},{1,3},{2,0},{3,1},{4,6},{5,7},{6,4},{7,5},{8,10},{9,11},{10,... | collective-permute-start | bytes 60008 | tf_op jit(solution)/shard_map/ppermute | solution.py:23
  36.1 4.7 %collective-permute-start.6 = (f32[50,200]{0,1:T(8,128)S(1)}, f32[50,200]{0,1:T(8,128)S(1)}, u32[]{:S(2)}, u32[]{:S(2)}) collective-permute-start(f32[50,200]{0,1:T(8,128)S(1)} %maximum_select_fusion.2), channel_id=1, source_target_pairs={{0,16},{8,24},{16,0},{24,8},{1,17},{9,25},{17,1},{25,9},{2,18},{10... | collective-permute-start | bytes 120008 | tf_op jit(solution)/shard_map/ppermute | solution.py:23
  40.9 8.1 %collective-permute-start.7 = (f32[100,200]{0,1:T(8,128)S(1)}, f32[100,200]{0,1:T(8,128)S(1)}, u32[]{:S(2)}, u32[]{:S(2)}) collective-permute-start(f32[100,200]{0,1:T(8,128)S(1)} %maximum_select_fusion.3), channel_id=1, source_target_pairs={{0,8},{8,0},{16,24},{24,16},{1,9},{9,1},{17,25},{25,17},{2,10},{10... | collective-permute-start | bytes 240008 | tf_op jit(solution)/shard_map/ppermute | solution.py:23
  42.5 13.9 %collective-permute-start.9 = (f32[128,401]{0,1:T(8,128)S(1)}, f32[128,401]{0,1:T(8,128)}, u32[]{:S(2)}, u32[]{:S(2)}) collective-permute-start(f32[128,401]{0,1:T(8,128)S(1)} %pad_maximum_fusion.1), channel_id=1, source_target_pairs={{2,0},{3,1},{4,2},{5,3},{6,4},{7,5},{10,8},{11,9},{12,10},{13,11},... | collective-permute-start | bytes 615944 | tf_op jit(solution)/shard_map/ppermute | solution.py:76
  43.8 14.0 %collective-permute-start.10 = (f32[128,401]{0,1:T(8,128)S(1)}, f32[128,401]{0,1:T(8,128)}, u32[]{:S(2)}, u32[]{:S(2)}) collective-permute-start(f32[128,401]{0,1:T(8,128)S(1)} %pad_maximum_fusion.1), channel_id=1, source_target_pairs={{0,2},{1,3},{2,4},{3,5},{4,6},{5,7},{8,10},{9,11},{10,12},{11,13},... | collective-permute-start | bytes 615944 | tf_op jit(solution)/shard_map/ppermute | solution.py:75
  49.2 13.8 %collective-permute-start.8 = (f32[200,200]{0,1:T(8,128)S(1)}, f32[200,200]{0,1:T(8,128)S(1)}, u32[]{:S(2)}, u32[]{:S(2)}) collective-permute-start(f32[200,200]{0,1:T(8,128)S(1)} %maximum_select_fusion.1), channel_id=1, source_target_pairs={{0,1},{1,0},{2,3},{3,2},{4,5},{5,4},{6,7},{7,6},{8,9},{9,8},{10,11... | collective-permute-start | bytes 480008 | tf_op jit(solution)/shard_map/ppermute | solution.py:23
  49.3 3.9 %collective-permute-start.15 = (f32[8]{0:T(128)S(1)}, f32[8]{0:T(128)S(1)}, u32[]{:S(2)}, u32[]{:S(2)}) collective-permute-start(f32[8]{0:T(128)S(1)} %bitcast.58), channel_id=1, source_target_pairs={{0,1},{1,0},{2,3},{3,2},{4,5},{5,4},{6,7},{7,6},{8,9},{9,8},{10,11... | collective-permute-start | bytes 104 | tf_op jit(solution)/shard_map/ppermute | solution.py:23
  56.5 39.1 %collective-permute-start.13 = (f32[128,401]{0,1:T(8,128)}, f32[128,401]{0,1:T(8,128)}, u32[]{:S(2)}, u32[]{:S(2)}) collective-permute-start(f32[128,401]{0,1:T(8,128)} %collective-permute-done.9), channel_id=1, source_target_pairs={{2,0},{3,1},{4,2},{5,3},{6,4},{7,5},{10,8},{11,9},{12,10},{13,11},... | collective-permute-start | bytes 615944 | tf_op jit(solution)/shard_map/ppermute | solution.py:76
  57.8 39.1 %collective-permute-start.11 = (f32[128,401]{0,1:T(8,128)}, f32[128,401]{0,1:T(8,128)}, u32[]{:S(2)}, u32[]{:S(2)}) collective-permute-start(f32[128,401]{0,1:T(8,128)} %collective-permute-done.10), channel_id=1, source_target_pairs={{0,2},{1,3},{2,4},{3,5},{4,6},{5,7},{8,10},{9,11},{10,12},{11,13},... | collective-permute-start | bytes 615944 | tf_op jit(solution)/shard_map/ppermute | solution.py:75
  95.6 8.8 %collective-permute-start.14 = (f32[128,401]{0,1:T(8,128)}, f32[128,401]{0,1:T(8,128)S(1)}, u32[]{:S(2)}, u32[]{:S(2)}) collective-permute-start(f32[128,401]{0,1:T(8,128)} %collective-permute-done.13), channel_id=1, source_target_pairs={{2,0},{3,1},{4,2},{5,3},{6,4},{7,5},{10,8},{11,9},{12,10},{13,11},... | collective-permute-start | bytes 615944 | tf_op jit(solution)/shard_map/ppermute | solution.py:76
  96.9 8.7 %collective-permute-start.12 = (f32[128,401]{0,1:T(8,128)}, f32[128,401]{0,1:T(8,128)S(1)}, u32[]{:S(2)}, u32[]{:S(2)}) collective-permute-start(f32[128,401]{0,1:T(8,128)} %collective-permute-done.11), channel_id=1, source_target_pairs={{0,2},{1,3},{2,4},{3,5},{4,6},{5,7},{8,10},{9,11},{10,12},{11,13},... | collective-permute-start | bytes 615944 | tf_op jit(solution)/shard_map/ppermute | solution.py:75
  108.3 1.8 %collective-permute-start.16 = (f32[400,200]{0,1:T(8,128)S(1)}, f32[400,200]{0,1:T(8,128)S(1)}, u32[]{:S(2)}, u32[]{:S(2)}) collective-permute-start(f32[400,200]{0,1:T(8,128)S(1)} %slice.183), channel_id=1, source_target_pairs={{0,1},{1,0},{2,3},{3,2},{4,5},{5,4},{6,7},{7,6},{8,9},{9,8},{10,11... | collective-permute-start | bytes 960008 | tf_op jit(solution)/shard_map/ppermute | solution.py:23
  111.3 23.5 %collective-permute-start.17 = (f32[300,200]{0,1:T(8,128)}, f32[300,200]{0,1:T(8,128)}, u32[]{:S(2)}, u32[]{:S(2)}) collective-permute-start(f32[300,200]{0,1:T(8,128)} %pad_maximum_fusion), channel_id=1, source_target_pairs={{0,16},{8,24},{16,0},{24,8},{1,17},{9,25},{17,1},{25,9},{2,18},{10... | collective-permute-start | bytes 720008 | tf_op jit(solution)/shard_map/ppermute | solution.py:23
  137.6 6.9 %collective-permute-start.18 = (f32[250,200]{0,1:T(8,128)S(1)}, f32[250,200]{0,1:T(8,128)S(1)}, u32[]{:S(2)}, u32[]{:S(2)}) collective-permute-start(f32[250,200]{0,1:T(8,128)S(1)} %pad_maximum_fusion.2), channel_id=1, source_target_pairs={{0,8},{8,0},{16,24},{24,16},{1,9},{9,1},{17,25},{25,17},{2,10},{10... | collective-permute-start | bytes 600008 | tf_op jit(solution)/shard_map/ppermute | solution.py:23

commit v5 on v3

--- a/solution.py
+++ b/solution.py
@@ -4,6 +4,37 @@
 from jax.sharding import PartitionSpec as P
 
 BLOCK = 128
+
+
+def lower_inverse(factor, precision):
+    eye = jnp.eye(factor.shape[0], dtype=factor.dtype)
+    return lax.linalg.triangular_solve(factor, eye, left_side=True, lower=True, transpose_a=False)
+
+
+def block_cholesky(system, split, precision):
+    system = (system + system.T) * 0.5
+    a11, a21, a22 = system[:split, :split], system[split:, :split], system[split:, split:]
+    l11 = lax.linalg.cholesky(a11, symmetrize_input=False)
+    inv11 = lower_inverse(l11, precision)
+    l21 = jnp.dot(a21, inv11.T, precision=precision)
+    l22 = lax.linalg.cholesky(a22 - jnp.dot(l21, l21.T, precision=precision), symmetrize_input=False)
+    inv22 = lower_inverse(l22, precision)
+    return inv11, l21, inv22
+
+
+def forward(parts, right, precision):
+    inv11, l21, inv22 = parts
+    split = inv11.shape[0]
+    y1 = jnp.dot(inv11, right[:split], precision=precision)
+    y2 = jnp.dot(inv22, right[split:] - jnp.dot(l21, y1, precision=precision), precision=precision)
+    return y1, y2
+
+
+def backward(parts, y1, y2, precision):
+    inv11, l21, inv22 = parts
+    x2 = jnp.dot(inv22.T, y2, precision=precision)
+    x1 = jnp.dot(inv11.T, y1 - jnp.dot(l21.T, x2, precision=precision), precision=precision)
+    return jnp.concatenate([x1, x2], 0)
 
 
 def prepare(pred_rows, obs_rows, std_rows, norm_factor):
@@ -84,7 +115,7 @@
     own_start = lax.axis_index("well") * own_count
     cross_mine = lax.dynamic_slice_in_dim(cross_matrix, own_start, own_count, 1)
     system = jnp.eye(members, dtype=jnp.float32) + gram_matrix
-    factor = jnp.linalg.cholesky(system)
+    factor = block_cholesky(system, min(BLOCK, members - 8), highest)
 
     group = lax.all_gather(packed, "tile", axis=0, tiled=True)
     factor, group = lax.optimization_barrier((factor, group))
@@ -106,15 +137,11 @@
     steps = list(reversed(axis_bits("well")))
     factor, taper_gram, taper_cross_t = lax.optimization_barrier((factor, taper_gram, taper_cross_t))
     taper_gram, cross_t_mine = well_step(taper_gram, taper_cross_t, *steps[0])
-    middle = lax.linalg.triangular_solve(
-        factor, cross_mine, left_side=True, lower=True, transpose_a=False
-    )
+    middle = forward(factor, cross_mine, highest)
     middle, taper_gram, cross_t_mine = lax.optimization_barrier((middle, taper_gram, cross_t_mine))
     for axis, k in steps[1:]:
         taper_gram, cross_t_mine = well_step(taper_gram, cross_t_mine, axis, k)
-    solved_mine = lax.linalg.triangular_solve(
-        factor, middle, left_side=True, lower=True, transpose_a=True
-    )
+    solved_mine = backward(factor, *middle, highest)
 
     space_t = cross_t_mine - lax.dot_general(
         solved_mine, taper_gram, (((0,), (1,)), ((), ())), precision=highest

time: 137 us -> 123 us (0.90)
  other arithmetic: 61.1 us -> 43.1 us
  waiting for transfers between devices: 28.5 us -> 36.1 us
  matrix products: 13.6 us -> 12 us
  between operations: 15.1 us -> 13.7 us
    another operation x14 -> x10, other arithmetic: 50.8 us -> 36 us  [the longest x4 16.4 us: lower_inverse(): lax.linalg.triangular_solve(factor, eye, left_side=True, lower=True, tran...]
    ppermute x11, waiting for transfers between devices: 28.5 us -> 36.1 us  [swap(): return lax.ppermute(x, axis, [(i, i ^ k) for i in range(size)])]
    another operation x8 -> x2, matrix products: 3.29 us -> 0.48 us  [lower_inverse(): lax.linalg.triangular_solve(factor, eye, left_side=True, lower=True, tran...]
    dot_general x0 -> x8, matrix products: none -> 1.87 us  [the longest x1 0.28 us: backward(): jnp.dot(inv11.T, y1 - jnp.dot(l21.T, x2, precision=precision), precision=...]
    add x2, other arithmetic: 2.01 us -> 0.15 us  [well_step(): return (full + got[:full.shape[0]], keep + got[full.shape[0]:])]
  transfers between devices with their start and end apart: 12 -> 12, of which waited for: 10 -> 11; matrix products, arithmetic and copies ran while one was open for 41% -> 32% of each run, Pallas kernels for 0% -> 0%
where the time goes in v5:
time: 123 us
  other arithmetic  43.1 us (35%)
  waiting for transfers between devices  36.1 us (29%)
  starting transfers between devices  17.7 us (14%)
  between operations  13.7 us (11%)
  matrix products  12 us (10%)
    ppermute x11, waiting for transfers between devices, swap(): return lax.ppermute(x, axis, [(i, i ^ k) for i in range(size)])  36.1 us
    ppermute x11, starting transfers between devices, swap(): return lax.ppermute(x, axis, [(i, i ^ k) for i in range(size)])  17.7 us
    another operation x4, other arithmetic, lower_inverse(): lax.linalg.triangular_solve(factor, eye, left_side=True, lower=True, tran...  16.4 us
    another operation x3, other arithmetic, block_cholesky(): l11 = lax.linalg.cholesky(a11, symmetrize_input=False)  12.4 us
    another operation x3, other arithmetic, block_cholesky(): lax.linalg.cholesky(a22 - jnp.dot(l21, l21.T, precision=precision), symme...  7.22 us
    dot_general x1, matrix products, shards(): lax.dot_general(jnp.concatenate([group_anom, group_innov], 1), tapered, (...  3.57 us
    dot_general x1, matrix products, shards(): jnp.einsum('vnc,mn->vmc', state_anom, space_t, precision=highest)  2.75 us
  transfers between devices with their start and end apart: 12, of which 11 were waited for; matrix products, arithmetic and copies ran while one was open for 32% of the time, Pallas kernels for 0%

profile of v5, /device:TPU:0, one launch (start us, length us, event | category | flops | bytes accessed | tf_op | source)
XLA Modules:
  0.0 123.0 jit_solution(17307976529125598198)
XLA Ops:
  6.5 0.9 reduce_sum.18
  8.1 1.0 subtract_multiply_fusion
  9.1 1.2 %fusion.29 = f32[200,200]{0,1:T(8,128)S(1)} fusion(f32[128,200]{0,1:T(8,128)S(1)} %get-tuple-element.42, f32[128,200]{0,1:T(8,128)} %param.7, f32[128]{0:T(128)S(1)} %get-tuple-element.35, f32[128]{0:T(128)S(1)} %get-tuple-element.45), kind=kOutput, calls=%fused_computation.49 | convolution fusion | flops 61491200 | bytes 365824 | tf_op jit(solution)/shard_map/dot_general | solution.py:106
  10.4 1.5 %broadcast_select_fusion = (f32[200,200]{0,1:T(8,128)S(1)}, f32[200,200]{0,1:T(8,128)S(1)}) fusion(f32[200,200]{0,1:T(8,128)S(1)} %fusion.29, pred[]{:T(512)S(6)} %eq.36, f32[128,200]{0,1:T(8,128)} %param.7, f32[128]{0:T(128)S(1)} %get-tuple-element.35, f32[128]{0:T(128)S(1)} %get-tuple-element.45), kind=kOutput, calls=%fused_computation.39 | convolution fusion | flops 61582400 | bytes 583425 | tf_op jit(solution)/shard_map/dot_general | solution.py:105
  12.3 1.2 collective-permute-done
  13.6 1.0 select_add_fusion
  14.6 2.9 %collective-permute-start.1 = (f32[100,200]{0,1:T(8,128)S(1)}, f32[100,200]{0,1:T(8,128)S(1)}, u32[]{:S(2)}, u32[]{:S(2)}) collective-permute-start(f32[100,200]{0,1:T(8,128)S(1)} %slice_select_fusion.2), channel_id=1, source_target_pairs={{0,8},{8,0},{16,24},{24,16},{1,9},{9,1},{17,25},{25,17},{2,10},{10... | collective-permute-start | bytes 240008 | tf_op jit(solution)/shard_map/ppermute | solution.py:54
  17.6 3.2 %collective-permute-done.1 = f32[100,200]{0,1:T(8,128)S(1)} collective-permute-done((f32[100,200]{0,1:T(8,128)S(1)}, f32[100,200]{0,1:T(8,128)S(1)}, u32[]{:S(2)}, u32[]{:S(2)}) %collective-permute-start.1) | collective-permute-done | bytes 80032 | tf_op jit(solution)/shard_map/ppermute | solution.py:54
  20.9 1.8 %collective-permute-start.2 = (f32[50,200]{0,1:T(8,128)S(1)}, f32[50,200]{0,1:T(8,128)S(1)}, u32[]{:S(2)}, u32[]{:S(2)}) collective-permute-start(f32[50,200]{0,1:T(8,128)S(1)} %slice_select_fusion.1), channel_id=1, source_target_pairs={{0,16},{8,24},{16,0},{24,8},{1,17},{9,25},{17,1},{25,9},{2,18},{10... | collective-permute-start | bytes 120008 | tf_op jit(solution)/shard_map/ppermute | solution.py:54
  22.8 2.9 %collective-permute-done.2 = f32[50,200]{0,1:T(8,128)S(1)} collective-permute-done((f32[50,200]{0,1:T(8,128)S(1)}, f32[50,200]{0,1:T(8,128)S(1)}, u32[]{:S(2)}, u32[]{:S(2)}) %collective-permute-start.2) | collective-permute-done | bytes 40032 | tf_op jit(solution)/shard_map/ppermute | solution.py:54
  25.9 1.9 %collective-permute-start.3 = (f32[25,200]{0,1:T(8,128)S(1)}, f32[25,200]{0,1:T(8,128)S(1)}, u32[]{:S(2)}, u32[]{:S(2)}) collective-permute-start(f32[25,200]{0,1:T(8,128)S(1)} %slice_select_fusion), channel_id=1, source_target_pairs={{0,2},{1,3},{2,0},{3,1},{4,6},{5,7},{6,4},{7,5},{8,10},{9,11},{10,... | collective-permute-start | bytes 60008 | tf_op jit(solution)/shard_map/ppermute | solution.py:54
  27.8 2.8 %collective-permute-done.3 = f32[25,200]{0,1:T(8,128)S(1)} collective-permute-done((f32[25,200]{0,1:T(8,128)S(1)}, f32[25,200]{0,1:T(8,128)S(1)}, u32[]{:S(2)}, u32[]{:S(2)}) %collective-permute-start.3) | collective-permute-done | bytes 20032 | tf_op jit(solution)/shard_map/ppermute | solution.py:54
  30.7 3.3 %collective-permute-start.4 = (f32[25,200]{0,1:T(8,128)S(1)}, f32[25,200]{0,1:T(8,128)S(1)}, u32[]{:S(2)}, u32[]{:S(2)}) collective-permute-start(f32[25,200]{0,1:T(8,128)S(1)} %select_add_fusion.1), channel_id=1, source_target_pairs={{0,4},{1,5},{2,6},{3,7},{4,0},{5,1},{6,2},{7,3},{8,12},{9,13},{10,... | collective-permute-start | bytes 60008 | tf_op jit(solution)/shard_map/ppermute | solution.py:54
  34.0 0.7 pad_maximum_fusion.1
  34.7 3.0 %collective-permute-done.4 = f32[25,200]{0,1:T(8,128)S(1)} collective-permute-done((f32[25,200]{0,1:T(8,128)S(1)}, f32[25,200]{0,1:T(8,128)S(1)}, u32[]{:S(2)}, u32[]{:S(2)}) %collective-permute-start.4) | collective-permute-done | bytes 20032 | tf_op jit(solution)/shard_map/ppermute | solution.py:54
  38.3 4.1 %collective-permute-done.5 = f32[25,200]{0,1:T(8,128)S(1)} collective-permute-done((f32[25,200]{0,1:T(8,128)S(1)}, f32[25,200]{0,1:T(8,128)S(1)}, u32[]{:S(2)}, u32[]{:S(2)}) %collective-permute-start.5) | collective-permute-done | bytes 20032 | tf_op jit(solution)/shard_map/ppermute | solution.py:54
  42.6 1.6 %collective-permute-start.6 = (f32[50,200]{0,1:T(8,128)S(1)}, f32[50,200]{0,1:T(8,128)S(1)}, u32[]{:S(2)}, u32[]{:S(2)}) collective-permute-start(f32[50,200]{0,1:T(8,128)S(1)} %maximum_select_fusion.2), channel_id=1, source_target_pairs={{0,16},{8,24},{16,0},{24,8},{1,17},{9,25},{17,1},{25,9},{2,18},{10... | collective-permute-start | bytes 120008 | tf_op jit(solution)/shard_map/ppermute | solution.py:54
  44.4 3.0 %collective-permute-done.6 = f32[50,200]{0,1:T(8,128)S(1)} collective-permute-done((f32[50,200]{0,1:T(8,128)S(1)}, f32[50,200]{0,1:T(8,128)S(1)}, u32[]{:S(2)}, u32[]{:S(2)}) %collective-permute-start.6) | collective-permute-done | bytes 40032 | tf_op jit(solution)/shard_map/ppermute | solution.py:54
  47.5 1.6 %collective-permute-start.7 = (f32[100,200]{0,1:T(8,128)S(1)}, f32[100,200]{0,1:T(8,128)S(1)}, u32[]{:S(2)}, u32[]{:S(2)}) collective-permute-start(f32[100,200]{0,1:T(8,128)S(1)} %maximum_select_fusion.3), channel_id=1, source_target_pairs={{0,8},{8,0},{16,24},{24,16},{1,9},{9,1},{17,25},{25,17},{2,10},{10... | collective-permute-start | bytes 240008 | tf_op jit(solution)/shard_map/ppermute | solution.py:54
  49.0 3.2 %collective-permute-done.7 = f32[100,200]{0,1:T(8,128)S(1)} collective-permute-done((f32[100,200]{0,1:T(8,128)S(1)}, f32[100,200]{0,1:T(8,128)S(1)}, u32[]{:S(2)}, u32[]{:S(2)}) %collective-permute-start.7) | collective-permute-done | bytes 80032 | tf_op jit(solution)/shard_map/ppermute | solution.py:54
  52.5 1.4 %collective-permute-done.8 = f32[200,200]{0,1:T(8,128)S(1)} collective-permute-done((f32[200,200]{0,1:T(8,128)S(1)}, f32[200,200]{0,1:T(8,128)S(1)}, u32[]{:S(2)}, u32[]{:S(2)}) %collective-permute-start.8) | collective-permute-done | bytes 160032 | tf_op jit(solution)/shard_map/ppermute | solution.py:54
  54.4 11.7 %cholesky.35 = f32[128,128]{1,0:T(8,128)S(1)} custom-call(f32[128,128]{1,0:T(8,128)S(1)} %cholesky.77), custom_call_target="Cholesky" | custom-call | tf_op jit(solution)/shard_map/cholesky | solution.py:17
  67.4 9.8 %custom-call.10 = f32[1,128,128]{1,2,0:T(8,128)S(1)} custom-call(f32[1,128,128]{2,1,0:T(8,128)S(1)} %fusion.33), custom_call_target="InvertDiagBlocksLowerTriangular" | custom-call | tf_op jit(solution)/shard_map/triangular_solve | solution.py:11
  77.9 6.6 %cholesky.68 = f32[72,72]{1,0:T(8,128)S(1)} custom-call(f32[72,72]{1,0:T(8,128)S(1)} %convolution_subtract_fusion), custom_call_target="Cholesky" | custom-call | tf_op jit(solution)/shard_map/cholesky | solution.py:20
  85.7 5.5 %custom-call.11 = f32[1,72,72]{1,2,0:T(8,128)S(1)} custom-call(f32[1,72,72]{2,1,0:T(8,128)S(1)} %fusion.41), custom_call_target="InvertDiagBlocksLowerTriangular" | custom-call | tf_op jit(solution)/shard_map/triangular_solve | solution.py:11
  91.6 0.8 slice_multiply_fusion
  92.3 3.6 %fusion.3 = f32[400,200]{0,1:T(8,128)S(1)} fusion(f32[1024,401]{0,1:T(8,128)} %all-gather.2.cloned.1.call-done, f32[1024]{0:T(1024)S(1)} %bitcast.39), kind=kOutput, calls=%fused_computation.3 | convolution fusion | flops 983244800 | bytes 2781696 | tf_op jit(solution)/shard_map/dot_general | solution.py:130
  96.3 1.7 %collective-permute-start.9 = (f32[300,200]{0,1:T(8,128)S(1)}, f32[300,200]{0,1:T(8,128)S(1)}, u32[]{:S(2)}, u32[]{:S(2)}) collective-permute-start(f32[300,200]{0,1:T(8,128)S(1)} %pad_maximum_fusion), channel_id=1, source_target_pairs={{0,16},{8,24},{16,0},{24,8},{1,17},{9,25},{17,1},{25,9},{2,18},{10... | collective-permute-start | bytes 720008 | tf_op jit(solution)/shard_map/ppermute | solution.py:54
  98.7 6.9 %collective-permute-done.9 = f32[300,200]{0,1:T(8,128)S(1)} collective-permute-done((f32[300,200]{0,1:T(8,128)S(1)}, f32[300,200]{0,1:T(8,128)S(1)}, u32[]{:S(2)}, u32[]{:S(2)}) %collective-permute-start.9) | collective-permute-done | bytes 240032 | tf_op jit(solution)/shard_map/ppermute | solution.py:54
  106.5 1.7 %collective-permute-start.10 = (f32[250,200]{0,1:T(8,128)S(1)}, f32[250,200]{0,1:T(8,128)S(1)}, u32[]{:S(2)}, u32[]{:S(2)}) collective-permute-start(f32[250,200]{0,1:T(8,128)S(1)} %pad_maximum_fusion.2), channel_id=1, source_target_pairs={{0,8},{8,0},{16,24},{24,16},{1,9},{9,1},{17,25},{25,17},{2,10},{10... | collective-permute-start | bytes 600008 | tf_op jit(solution)/shard_map/ppermute | solution.py:54
  108.5 4.4 %collective-permute-done.10 = f32[250,200]{0,1:T(8,128)S(1)} collective-permute-done((f32[250,200]{0,1:T(8,128)S(1)}, f32[250,200]{0,1:T(8,128)S(1)}, u32[]{:S(2)}, u32[]{:S(2)}) %collective-permute-start.10) | collective-permute-done | bytes 200032 | tf_op jit(solution)/shard_map/ppermute | solution.py:54
  113.4 2.8 %fusion.8 = f32[3,50,1024]{2,1,0:T(8,128)} fusion(f32[3,200,1024]{2,1,0:T(8,128)S(1)} %copy-done, f32[3,1024]{1,0:T(4,128)S(1)} %broadcast_multiply_fusion, s32[]{:T(128)S(6)} %select_n.148, f32[50,200]{0,1:T(8,128)S(1)} %fusion.16, f32[250,200]{0,1:T(8,128)S(1)} %collective-permute-done.10, f32[100,200]{0,1:T(8,128)S(1)} %slice_add_fusion.5, pred[]{:T(512)S(6)} %eq.34), kind=kOutput, calls=%fused_computation.6 | convolution fusion | flops 370052416 | bytes 4186117 | tf_op jit(solution)/shard_map/vnc,mn->vmc/dot_general | solution.py:150
  (57 shorter events, 9.7 us)
Async XLA Ops:
  6.5 85.0 %all-gather.2.cloned.1.call-start = ((), (), s32[]{:S(2)}) async-start(), calls=%async_computation | async-start | bytes 1880064 | tf_op jit(solution)/shard_map/all_gather | solution.py:120
  10.4 33.8 %copy-start = (f32[3,200,1024]{2,1,0:T(8,128)S(1)}, f32[3,200,1024]{2,1,0:T(8,128)}, u32[]{:S(2)}) copy-start(f32[3,200,1024]{2,1,0:T(8,128)} %param.6) | copy-start | bytes 7372804
  11.8 1.7 %collective-permute-start = (f32[200,200]{0,1:T(8,128)S(1)}, f32[200,200]{0,1:T(8,128)}, u32[]{:S(2)}, u32[]{:S(2)}) collective-permute-start(f32[200,200]{0,1:T(8,128)S(1)} %get-tuple-element.43), channel_id=1, source_target_pairs={{0,1},{1,0},{2,3},{3,2},{4,5},{5,4},{6,7},{7,6},{8,9},{9,8},{10,11... | collective-permute-start | bytes 480008 | tf_op jit(solution)/shard_map/ppermute | solution.py:54
  14.6 6.1 %collective-permute-start.1 = (f32[100,200]{0,1:T(8,128)S(1)}, f32[100,200]{0,1:T(8,128)S(1)}, u32[]{:S(2)}, u32[]{:S(2)}) collective-permute-start(f32[100,200]{0,1:T(8,128)S(1)} %slice_select_fusion.2), channel_id=1, source_target_pairs={{0,8},{8,0},{16,24},{24,16},{1,9},{9,1},{17,25},{25,17},{2,10},{10... | collective-permute-start | bytes 240008 | tf_op jit(solution)/shard_map/ppermute | solution.py:54
  20.9 4.7 %collective-permute-start.2 = (f32[50,200]{0,1:T(8,128)S(1)}, f32[50,200]{0,1:T(8,128)S(1)}, u32[]{:S(2)}, u32[]{:S(2)}) collective-permute-start(f32[50,200]{0,1:T(8,128)S(1)} %slice_select_fusion.1), channel_id=1, source_target_pairs={{0,16},{8,24},{16,0},{24,8},{1,17},{9,25},{17,1},{25,9},{2,18},{10... | collective-permute-start | bytes 120008 | tf_op jit(solution)/shard_map/ppermute | solution.py:54
  25.9 26.6 %copy-start.1 = (s32[1,8]{1,0:T(1,128)S(1)}, s32[1,8]{1,0:T(1,128)}, u32[]{:S(2)}) copy-start(s32[1,8]{1,0:T(1,128)} %param.11) | copy-start | bytes 100
  25.9 26.6 %copy-start.2 = (s32[1,8]{1,0:T(1,128)S(1)}, s32[1,8]{1,0:T(1,128)}, u32[]{:S(2)}) copy-start(s32[1,8]{1,0:T(1,128)} %param.10) | copy-start | bytes 100
  25.9 4.7 %collective-permute-start.3 = (f32[25,200]{0,1:T(8,128)S(1)}, f32[25,200]{0,1:T(8,128)S(1)}, u32[]{:S(2)}, u32[]{:S(2)}) collective-permute-start(f32[25,200]{0,1:T(8,128)S(1)} %slice_select_fusion), channel_id=1, source_target_pairs={{0,2},{1,3},{2,0},{3,1},{4,6},{5,7},{6,4},{7,5},{8,10},{9,11},{10,... | collective-permute-start | bytes 60008 | tf_op jit(solution)/shard_map/ppermute | solution.py:54
  30.7 7.0 %collective-permute-start.4 = (f32[25,200]{0,1:T(8,128)S(1)}, f32[25,200]{0,1:T(8,128)S(1)}, u32[]{:S(2)}, u32[]{:S(2)}) collective-permute-start(f32[25,200]{0,1:T(8,128)S(1)} %select_add_fusion.1), channel_id=1, source_target_pairs={{0,4},{1,5},{2,6},{3,7},{4,0},{5,1},{6,2},{7,3},{8,12},{9,13},{10,... | collective-permute-start | bytes 60008 | tf_op jit(solution)/shard_map/ppermute | solution.py:54
  37.8 4.7 %collective-permute-start.5 = (f32[25,200]{0,1:T(8,128)S(1)}, f32[25,200]{0,1:T(8,128)S(1)}, u32[]{:S(2)}, u32[]{:S(2)}) collective-permute-start(f32[25,200]{0,1:T(8,128)S(1)} %add.84), channel_id=1, source_target_pairs={{0,2},{1,3},{2,0},{3,1},{4,6},{5,7},{6,4},{7,5},{8,10},{9,11},{10,... | collective-permute-start | bytes 60008 | tf_op jit(solution)/shard_map/ppermute | solution.py:54
  42.6 4.7 %collective-permute-start.6 = (f32[50,200]{0,1:T(8,128)S(1)}, f32[50,200]{0,1:T(8,128)S(1)}, u32[]{:S(2)}, u32[]{:S(2)}) collective-permute-start(f32[50,200]{0,1:T(8,128)S(1)} %maximum_select_fusion.2), channel_id=1, source_target_pairs={{0,16},{8,24},{16,0},{24,8},{1,17},{9,25},{17,1},{25,9},{2,18},{10... | collective-permute-start | bytes 120008 | tf_op jit(solution)/shard_map/ppermute | solution.py:54
  47.5 4.7 %collective-permute-start.7 = (f32[100,200]{0,1:T(8,128)S(1)}, f32[100,200]{0,1:T(8,128)S(1)}, u32[]{:S(2)}, u32[]{:S(2)}) collective-permute-start(f32[100,200]{0,1:T(8,128)S(1)} %maximum_select_fusion.3), channel_id=1, source_target_pairs={{0,8},{8,0},{16,24},{24,16},{1,9},{9,1},{17,25},{25,17},{2,10},{10... | collective-permute-start | bytes 240008 | tf_op jit(solution)/shard_map/ppermute | solution.py:54
  52.4 1.5 %collective-permute-start.8 = (f32[200,200]{0,1:T(8,128)S(1)}, f32[200,200]{0,1:T(8,128)S(1)}, u32[]{:S(2)}, u32[]{:S(2)}) collective-permute-start(f32[200,200]{0,1:T(8,128)S(1)} %maximum_select_fusion.1), channel_id=1, source_target_pairs={{0,1},{1,0},{2,3},{3,2},{4,5},{5,4},{6,7},{7,6},{8,9},{9,8},{10,11... | collective-permute-start | bytes 480008 | tf_op jit(solution)/shard_map/ppermute | solution.py:54
  96.3 9.4 %collective-permute-start.9 = (f32[300,200]{0,1:T(8,128)S(1)}, f32[300,200]{0,1:T(8,128)S(1)}, u32[]{:S(2)}, u32[]{:S(2)}) collective-permute-start(f32[300,200]{0,1:T(8,128)S(1)} %pad_maximum_fusion), channel_id=1, source_target_pairs={{0,16},{8,24},{16,0},{24,8},{1,17},{9,25},{17,1},{25,9},{2,18},{10... | collective-permute-start | bytes 720008 | tf_op jit(solution)/shard_map/ppermute | solution.py:54
  106.5 6.4 %collective-permute-start.10 = (f32[250,200]{0,1:T(8,128)S(1)}, f32[250,200]{0,1:T(8,128)S(1)}, u32[]{:S(2)}, u32[]{:S(2)}) collective-permute-start(f32[250,200]{0,1:T(8,128)S(1)} %pad_maximum_fusion.2), channel_id=1, source_target_pairs={{0,8},{8,0},{16,24},{24,16},{1,9},{9,1},{17,25},{25,17},{2,10},{10... | collective-permute-start | bytes 600008 | tf_op jit(solution)/shard_map/ppermute | solution.py:54
Sparse Core Ops, SparseCore 0:
  44.5 28.3 all-gather.1

commit v6 on v5

--- a/solution.py
+++ b/solution.py
@@ -84,16 +84,6 @@
     return x, tie
 
 
-def well_step(full, split, axis, k):
-    rows = split.shape[0]
-    half = rows // 2
-    hi = bit_of(axis, k) == 1
-    keep = jnp.where(hi, split[half:], split[:half])
-    send = jnp.where(hi, split[:half], split[half:])
-    got = swap(jnp.concatenate([full, send], 0), axis, k)
-    return full + got[: full.shape[0]], keep + got[full.shape[0]:]
-
-
 def shards(prior_state, pred_data, obs_pert, obs_std, loc_mask, taper_level):
     highest = lax.Precision.HIGHEST
     members = pred_data.shape[1]
@@ -113,7 +103,6 @@
     gram_matrix, cross_matrix = stacked[:members], stacked[members:]
     own_count = members // lax.axis_size("well")
     own_start = lax.axis_index("well") * own_count
-    cross_mine = lax.dynamic_slice_in_dim(cross_matrix, own_start, own_count, 1)
     system = jnp.eye(members, dtype=jnp.float32) + gram_matrix
     factor = block_cholesky(system, min(BLOCK, members - 8), highest)
 
@@ -134,18 +123,17 @@
         precision=highest,
     )
     taper_gram, taper_cross_t = both[:members], both[members:]
-    steps = list(reversed(axis_bits("well")))
-    factor, taper_gram, taper_cross_t = lax.optimization_barrier((factor, taper_gram, taper_cross_t))
-    taper_gram, cross_t_mine = well_step(taper_gram, taper_cross_t, *steps[0])
-    middle = forward(factor, cross_mine, highest)
-    middle, taper_gram, cross_t_mine = lax.optimization_barrier((middle, taper_gram, cross_t_mine))
-    for axis, k in steps[1:]:
-        taper_gram, cross_t_mine = well_step(taper_gram, cross_t_mine, axis, k)
-    solved_mine = backward(factor, *middle, highest)
 
-    space_t = cross_t_mine - lax.dot_general(
-        solved_mine, taper_gram, (((0,), (1,)), ((), ())), precision=highest
+    solved = backward(factor, *forward(factor, cross_matrix, highest), highest)
+    space_t = taper_cross_t - lax.dot_general(
+        solved, taper_gram, (((0,), (1,)), ((), ())), precision=highest
     )
+    for axis, k in reversed(axis_bits("well")):
+        half = space_t.shape[0] // 2
+        hi = bit_of(axis, k) == 1
+        keep = jnp.where(hi, space_t[half:], space_t[:half])
+        send = jnp.where(hi, space_t[:half], space_t[half:])
+        space_t = keep + swap(send, axis, k)
     state_anom = (prior_state - jnp.mean(prior_state, axis=1, keepdims=True)) * norm_factor
     increment = jnp.einsum("vnc,mn->vmc", state_anom, space_t, precision=highest)
     prior_mine = lax.dynamic_slice_in_dim(prior_state, own_start, own_count, 1)

time: 123 us -> 118 us (0.959)
  waiting for transfers between devices: 36.1 us -> 31.1 us
    ppermute x11, waiting for transfers between devices: 36.1 us -> 31.1 us  [swap(): return lax.ppermute(x, axis, [(i, i ^ k) for i in range(size)])]
  transfers between devices with their start and end apart: 12 -> 12, of which waited for: 11 -> 11; matrix products, arithmetic and copies ran while one was open for 32% -> 33% of each run, Pallas kernels for 0% -> 0%
where the time goes in v6:
time: 118 us; the launch traced here: 117 us
  other arithmetic  42.2 us (36%)
  waiting for transfers between devices  31.1 us (26%)
  starting transfers between devices  17.5 us (15%)
  between operations  13.7 us (12%)
  matrix products  12.5 us (11%)
    ppermute x11, waiting for transfers between devices, swap(): return lax.ppermute(x, axis, [(i, i ^ k) for i in range(size)])  31.1 us
    ppermute x11, starting transfers between devices, swap(): return lax.ppermute(x, axis, [(i, i ^ k) for i in range(size)])  17.5 us
    another operation x4, other arithmetic, lower_inverse(): lax.linalg.triangular_solve(factor, eye, left_side=True, lower=True, tran...  16.7 us
    another operation x3, other arithmetic, block_cholesky(): l11 = lax.linalg.cholesky(a11, symmetrize_input=False)  12.5 us
    another operation x3, other arithmetic, block_cholesky(): lax.linalg.cholesky(a22 - jnp.dot(l21, l21.T, precision=precision), symme...  7.32 us
    dot_general x1, matrix products, shards(): lax.dot_general(jnp.concatenate([group_anom, group_innov], 1), tapered, (...  3.38 us
    dot_general x1, matrix products, shards(): jnp.einsum('vnc,mn->vmc', state_anom, space_t, precision=highest)  2.73 us
  transfers between devices with their start and end apart: 12, of which 11 were waited for; matrix products, arithmetic and copies ran while one was open for 33% of the time, Pallas kernels for 0%

profile of v6, /device:TPU:0, one launch (start us, length us, event | category | flops | bytes accessed | tf_op | source)
XLA Modules:
  0.0 117.3 jit_solution(10634410161893136078)
XLA Ops:
  6.5 0.9 reduce_sum.18
  8.1 1.0 subtract_multiply_fusion
  9.1 1.2 %fusion.31 = f32[200,200]{0,1:T(8,128)S(1)} fusion(f32[128,200]{0,1:T(8,128)S(1)} %get-tuple-element.20, f32[128,200]{0,1:T(8,128)} %param.7, f32[128]{0:T(128)S(1)} %get-tuple-element.17, f32[128]{0:T(128)S(1)} %get-tuple-element.23), kind=kOutput, calls=%fused_computation.50 | convolution fusion | flops 61491200 | bytes 365824 | tf_op jit(solution)/shard_map/dot_general | solution.py:96
  10.4 1.3 %broadcast_select_fusion = (f32[200,200]{0,1:T(8,128)S(1)}, f32[200,200]{0,1:T(8,128)S(1)}) fusion(f32[200,200]{0,1:T(8,128)S(1)} %fusion.31, pred[]{:T(512)S(6)} %eq.37, f32[128,200]{0,1:T(8,128)} %param.7, f32[128]{0:T(128)S(1)} %get-tuple-element.17, f32[128]{0:T(128)S(1)} %get-tuple-element.23), kind=kOutput, calls=%fused_computation.40 | convolution fusion | flops 61582400 | bytes 583425 | tf_op jit(solution)/shard_map/dot_general | solution.py:95
  12.2 1.1 collective-permute-done
  13.4 2.9 %collective-permute-start.1 = (f32[100,200]{0,1:T(8,128)S(1)}, f32[100,200]{0,1:T(8,128)S(1)}, u32[]{:S(2)}, u32[]{:S(2)}) collective-permute-start(f32[100,200]{0,1:T(8,128)S(1)} %slice_select_fusion.4), channel_id=1, source_target_pairs={{0,8},{8,0},{16,24},{24,16},{1,9},{9,1},{17,25},{25,17},{2,10},{10... | collective-permute-start | bytes 240008 | tf_op jit(solution)/shard_map/ppermute | solution.py:54
  16.4 3.2 %collective-permute-done.1 = f32[100,200]{0,1:T(8,128)S(1)} collective-permute-done((f32[100,200]{0,1:T(8,128)S(1)}, f32[100,200]{0,1:T(8,128)S(1)}, u32[]{:S(2)}, u32[]{:S(2)}) %collective-permute-start.1) | collective-permute-done | bytes 80032 | tf_op jit(solution)/shard_map/ppermute | solution.py:54
  19.7 1.8 %collective-permute-start.2 = (f32[50,200]{0,1:T(8,128)S(1)}, f32[50,200]{0,1:T(8,128)S(1)}, u32[]{:S(2)}, u32[]{:S(2)}) collective-permute-start(f32[50,200]{0,1:T(8,128)S(1)} %slice_select_fusion.3), channel_id=1, source_target_pairs={{0,16},{8,24},{16,0},{24,8},{1,17},{9,25},{17,1},{25,9},{2,18},{10... | collective-permute-start | bytes 120008 | tf_op jit(solution)/shard_map/ppermute | solution.py:54
  21.6 2.9 %collective-permute-done.2 = f32[50,200]{0,1:T(8,128)S(1)} collective-permute-done((f32[50,200]{0,1:T(8,128)S(1)}, f32[50,200]{0,1:T(8,128)S(1)}, u32[]{:S(2)}, u32[]{:S(2)}) %collective-permute-start.2) | collective-permute-done | bytes 40032 | tf_op jit(solution)/shard_map/ppermute | solution.py:54
  24.7 1.9 %collective-permute-start.3 = (f32[25,200]{0,1:T(8,128)S(1)}, f32[25,200]{0,1:T(8,128)S(1)}, u32[]{:S(2)}, u32[]{:S(2)}) collective-permute-start(f32[25,200]{0,1:T(8,128)S(1)} %slice_select_fusion.2), channel_id=1, source_target_pairs={{0,2},{1,3},{2,0},{3,1},{4,6},{5,7},{6,4},{7,5},{8,10},{9,11},{10,... | collective-permute-start | bytes 60008 | tf_op jit(solution)/shard_map/ppermute | solution.py:54
  26.6 2.8 %collective-permute-done.3 = f32[25,200]{0,1:T(8,128)S(1)} collective-permute-done((f32[25,200]{0,1:T(8,128)S(1)}, f32[25,200]{0,1:T(8,128)S(1)}, u32[]{:S(2)}, u32[]{:S(2)}) %collective-permute-start.3) | collective-permute-done | bytes 20032 | tf_op jit(solution)/shard_map/ppermute | solution.py:54
  29.5 3.3 %collective-permute-start.4 = (f32[25,200]{0,1:T(8,128)S(1)}, f32[25,200]{0,1:T(8,128)S(1)}, u32[]{:S(2)}, u32[]{:S(2)}) collective-permute-start(f32[25,200]{0,1:T(8,128)S(1)} %select_add_fusion.2), channel_id=1, source_target_pairs={{0,4},{1,5},{2,6},{3,7},{4,0},{5,1},{6,2},{7,3},{8,12},{9,13},{10,... | collective-permute-start | bytes 60008 | tf_op jit(solution)/shard_map/ppermute | solution.py:54
  33.5 3.0 %collective-permute-done.4 = f32[25,200]{0,1:T(8,128)S(1)} collective-permute-done((f32[25,200]{0,1:T(8,128)S(1)}, f32[25,200]{0,1:T(8,128)S(1)}, u32[]{:S(2)}, u32[]{:S(2)}) %collective-permute-start.4) | collective-permute-done | bytes 20032 | tf_op jit(solution)/shard_map/ppermute | solution.py:54
  37.1 4.1 %collective-permute-done.5 = f32[25,200]{0,1:T(8,128)S(1)} collective-permute-done((f32[25,200]{0,1:T(8,128)S(1)}, f32[25,200]{0,1:T(8,128)S(1)}, u32[]{:S(2)}, u32[]{:S(2)}) %collective-permute-start.5) | collective-permute-done | bytes 20032 | tf_op jit(solution)/shard_map/ppermute | solution.py:54
  41.4 1.6 %collective-permute-start.6 = (f32[50,200]{0,1:T(8,128)S(1)}, f32[50,200]{0,1:T(8,128)S(1)}, u32[]{:S(2)}, u32[]{:S(2)}) collective-permute-start(f32[50,200]{0,1:T(8,128)S(1)} %maximum_select_fusion.2), channel_id=1, source_target_pairs={{0,16},{8,24},{16,0},{24,8},{1,17},{9,25},{17,1},{25,9},{2,18},{10... | collective-permute-start | bytes 120008 | tf_op jit(solution)/shard_map/ppermute | solution.py:54
  43.0 3.1 %collective-permute-done.6 = f32[50,200]{0,1:T(8,128)S(1)} collective-permute-done((f32[50,200]{0,1:T(8,128)S(1)}, f32[50,200]{0,1:T(8,128)S(1)}, u32[]{:S(2)}, u32[]{:S(2)}) %collective-permute-start.6) | collective-permute-done | bytes 40032 | tf_op jit(solution)/shard_map/ppermute | solution.py:54
  46.2 1.6 %collective-permute-start.7 = (f32[100,200]{0,1:T(8,128)S(1)}, f32[100,200]{0,1:T(8,128)S(1)}, u32[]{:S(2)}, u32[]{:S(2)}) collective-permute-start(f32[100,200]{0,1:T(8,128)S(1)} %maximum_select_fusion.3), channel_id=1, source_target_pairs={{0,8},{8,0},{16,24},{24,16},{1,9},{9,1},{17,25},{25,17},{2,10},{10... | collective-permute-start | bytes 240008 | tf_op jit(solution)/shard_map/ppermute | solution.py:54
  47.8 3.2 %collective-permute-done.7 = f32[100,200]{0,1:T(8,128)S(1)} collective-permute-done((f32[100,200]{0,1:T(8,128)S(1)}, f32[100,200]{0,1:T(8,128)S(1)}, u32[]{:S(2)}, u32[]{:S(2)}) %collective-permute-start.7) | collective-permute-done | bytes 80032 | tf_op jit(solution)/shard_map/ppermute | solution.py:54
  51.3 1.4 %collective-permute-done.8 = f32[200,200]{0,1:T(8,128)S(1)} collective-permute-done((f32[200,200]{0,1:T(8,128)S(1)}, f32[200,200]{0,1:T(8,128)S(1)}, u32[]{:S(2)}, u32[]{:S(2)}) %collective-permute-start.8) | collective-permute-done | bytes 160032 | tf_op jit(solution)/shard_map/ppermute | solution.py:54
  53.1 11.7 %cholesky.35 = f32[128,128]{1,0:T(8,128)S(1)} custom-call(f32[128,128]{1,0:T(8,128)S(1)} %cholesky.77), custom_call_target="Cholesky" | custom-call | tf_op jit(solution)/shard_map/cholesky | solution.py:17
  64.8 0.7 compare_reduce_fusion.1
  66.3 9.8 %custom-call.10 = f32[1,128,128]{1,2,0:T(8,128)S(1)} custom-call(f32[1,128,128]{2,1,0:T(8,128)S(1)} %fusion.35), custom_call_target="InvertDiagBlocksLowerTriangular" | custom-call | tf_op jit(solution)/shard_map/triangular_solve | solution.py:11
  76.8 6.6 %cholesky.68 = f32[72,72]{1,0:T(8,128)S(1)} custom-call(f32[72,72]{1,0:T(8,128)S(1)} %convolution_subtract_fusion.2), custom_call_target="Cholesky" | custom-call | tf_op jit(solution)/shard_map/cholesky | solution.py:20
  83.4 0.7 compare_reduce_fusion
  84.8 5.5 %custom-call.11 = f32[1,72,72]{1,2,0:T(8,128)S(1)} custom-call(f32[1,72,72]{2,1,0:T(8,128)S(1)} %fusion.43), custom_call_target="InvertDiagBlocksLowerTriangular" | custom-call | tf_op jit(solution)/shard_map/triangular_solve | solution.py:11
  93.0 0.8 slice_multiply_fusion
  93.8 3.4 %fusion.3 = f32[400,200]{0,1:T(8,128)S(1)} fusion(f32[1024,401]{0,1:T(8,128)} %all-gather.2.cloned.1.call-done, f32[1024]{0:T(1024)S(1)} %bitcast.40), kind=kOutput, calls=%fused_computation.3 | convolution fusion | flops 983244800 | bytes 2781696 | tf_op jit(solution)/shard_map/dot_general | solution.py:119
  97.8 1.6 %collective-permute-start.9 = (f32[100,200]{0,1:T(8,128)S(1)}, f32[100,200]{0,1:T(8,128)S(1)}, u32[]{:S(2)}, u32[]{:S(2)}) collective-permute-start(f32[100,200]{0,1:T(8,128)S(1)} %slice_select_fusion.1), channel_id=1, source_target_pairs={{0,16},{8,24},{16,0},{24,8},{1,17},{9,25},{17,1},{25,9},{2,18},{10... | collective-permute-start | bytes 240008 | tf_op jit(solution)/shard_map/ppermute | solution.py:54
  99.6 3.2 %collective-permute-done.9 = f32[100,200]{0,1:T(8,128)S(1)} collective-permute-done((f32[100,200]{0,1:T(8,128)S(1)}, f32[100,200]{0,1:T(8,128)S(1)}, u32[]{:S(2)}, u32[]{:S(2)}) %collective-permute-start.9) | collective-permute-done | bytes 80032 | tf_op jit(solution)/shard_map/ppermute | solution.py:54
  103.0 1.7 %collective-permute-start.10 = (f32[50,200]{0,1:T(8,128)S(1)}, f32[50,200]{0,1:T(8,128)S(1)}, u32[]{:S(2)}, u32[]{:S(2)}) collective-permute-start(f32[50,200]{0,1:T(8,128)S(1)} %slice_select_fusion), channel_id=1, source_target_pairs={{0,8},{8,0},{16,24},{24,16},{1,9},{9,1},{17,25},{25,17},{2,10},{10... | collective-permute-start | bytes 120008 | tf_op jit(solution)/shard_map/ppermute | solution.py:54
  104.7 3.0 %collective-permute-done.10 = f32[50,200]{0,1:T(8,128)S(1)} collective-permute-done((f32[50,200]{0,1:T(8,128)S(1)}, f32[50,200]{0,1:T(8,128)S(1)}, u32[]{:S(2)}, u32[]{:S(2)}) %collective-permute-start.10) | collective-permute-done | bytes 40032 | tf_op jit(solution)/shard_map/ppermute | solution.py:54
  107.7 2.7 %fusion.8 = f32[3,50,1024]{2,1,0:T(8,128)} fusion(f32[3,200,1024]{2,1,0:T(8,128)S(1)} %copy-done, f32[3,1024]{1,0:T(4,128)S(1)} %broadcast_multiply_fusion, s32[]{:T(128)S(6)} %select_n.147, f32[50,200]{0,1:T(8,128)S(1)} %collective-permute-done.10, f32[100,200]{0,1:T(8,128)S(1)} %select_add_fusion.1, pred[]{:T(512)S(6)} %eq.34), kind=kOutput, calls=%fused_computation.6 | convolution fusion | flops 370042400 | bytes 4083717 | tf_op jit(solution)/shard_map/vnc,mn->vmc/dot_general | solution.py:138
  (52 shorter events, 9.8 us)
Async XLA Ops:
  6.5 84.1 %all-gather.2.cloned.1.call-start = ((), (), s32[]{:S(2)}) async-start(), calls=%async_computation | async-start | bytes 1880064 | tf_op jit(solution)/shard_map/all_gather | solution.py:109
  11.7 1.6 %collective-permute-start = (f32[200,200]{0,1:T(8,128)S(1)}, f32[200,200]{0,1:T(8,128)S(1)}, u32[]{:S(2)}, u32[]{:S(2)}) collective-permute-start(f32[200,200]{0,1:T(8,128)S(1)} %get-tuple-element.21), channel_id=1, source_target_pairs={{0,1},{1,0},{2,3},{3,2},{4,5},{5,4},{6,7},{7,6},{8,9},{9,8},{10,11... | collective-permute-start | bytes 480008 | tf_op jit(solution)/shard_map/ppermute | solution.py:54
  13.3 37.9 %copy-start.1 = (s32[1,8]{1,0:T(1,128)S(1)}, s32[1,8]{1,0:T(1,128)}, u32[]{:S(2)}) copy-start(s32[1,8]{1,0:T(1,128)} %param.11) | copy-start | bytes 100
  13.3 37.9 %copy-start.2 = (s32[1,8]{1,0:T(1,128)S(1)}, s32[1,8]{1,0:T(1,128)}, u32[]{:S(2)}) copy-start(s32[1,8]{1,0:T(1,128)} %param.10) | copy-start | bytes 100
  13.4 6.1 %collective-permute-start.1 = (f32[100,200]{0,1:T(8,128)S(1)}, f32[100,200]{0,1:T(8,128)S(1)}, u32[]{:S(2)}, u32[]{:S(2)}) collective-permute-start(f32[100,200]{0,1:T(8,128)S(1)} %slice_select_fusion.4), channel_id=1, source_target_pairs={{0,8},{8,0},{16,24},{24,16},{1,9},{9,1},{17,25},{25,17},{2,10},{10... | collective-permute-start | bytes 240008 | tf_op jit(solution)/shard_map/ppermute | solution.py:54
  19.7 4.7 %collective-permute-start.2 = (f32[50,200]{0,1:T(8,128)S(1)}, f32[50,200]{0,1:T(8,128)S(1)}, u32[]{:S(2)}, u32[]{:S(2)}) collective-permute-start(f32[50,200]{0,1:T(8,128)S(1)} %slice_select_fusion.3), channel_id=1, source_target_pairs={{0,16},{8,24},{16,0},{24,8},{1,17},{9,25},{17,1},{25,9},{2,18},{10... | collective-permute-start | bytes 120008 | tf_op jit(solution)/shard_map/ppermute | solution.py:54
  24.7 4.7 %collective-permute-start.3 = (f32[25,200]{0,1:T(8,128)S(1)}, f32[25,200]{0,1:T(8,128)S(1)}, u32[]{:S(2)}, u32[]{:S(2)}) collective-permute-start(f32[25,200]{0,1:T(8,128)S(1)} %slice_select_fusion.2), channel_id=1, source_target_pairs={{0,2},{1,3},{2,0},{3,1},{4,6},{5,7},{6,4},{7,5},{8,10},{9,11},{10,... | collective-permute-start | bytes 60008 | tf_op jit(solution)/shard_map/ppermute | solution.py:54
  29.5 7.0 %collective-permute-start.4 = (f32[25,200]{0,1:T(8,128)S(1)}, f32[25,200]{0,1:T(8,128)S(1)}, u32[]{:S(2)}, u32[]{:S(2)}) collective-permute-start(f32[25,200]{0,1:T(8,128)S(1)} %select_add_fusion.2), channel_id=1, source_target_pairs={{0,4},{1,5},{2,6},{3,7},{4,0},{5,1},{6,2},{7,3},{8,12},{9,13},{10,... | collective-permute-start | bytes 60008 | tf_op jit(solution)/shard_map/ppermute | solution.py:54
  36.5 4.7 %collective-permute-start.5 = (f32[25,200]{0,1:T(8,128)S(1)}, f32[25,200]{0,1:T(8,128)S(1)}, u32[]{:S(2)}, u32[]{:S(2)}) collective-permute-start(f32[25,200]{0,1:T(8,128)S(1)} %add.77), channel_id=1, source_target_pairs={{0,2},{1,3},{2,0},{3,1},{4,6},{5,7},{6,4},{7,5},{8,10},{9,11},{10,... | collective-permute-start | bytes 60008 | tf_op jit(solution)/shard_map/ppermute | solution.py:54
  41.4 4.7 %collective-permute-start.6 = (f32[50,200]{0,1:T(8,128)S(1)}, f32[50,200]{0,1:T(8,128)S(1)}, u32[]{:S(2)}, u32[]{:S(2)}) collective-permute-start(f32[50,200]{0,1:T(8,128)S(1)} %maximum_select_fusion.2), channel_id=1, source_target_pairs={{0,16},{8,24},{16,0},{24,8},{1,17},{9,25},{17,1},{25,9},{2,18},{10... | collective-permute-start | bytes 120008 | tf_op jit(solution)/shard_map/ppermute | solution.py:54
  46.2 4.7 %collective-permute-start.7 = (f32[100,200]{0,1:T(8,128)S(1)}, f32[100,200]{0,1:T(8,128)S(1)}, u32[]{:S(2)}, u32[]{:S(2)}) collective-permute-start(f32[100,200]{0,1:T(8,128)S(1)} %maximum_select_fusion.3), channel_id=1, source_target_pairs={{0,8},{8,0},{16,24},{24,16},{1,9},{9,1},{17,25},{25,17},{2,10},{10... | collective-permute-start | bytes 240008 | tf_op jit(solution)/shard_map/ppermute | solution.py:54
  51.1 1.5 %collective-permute-start.8 = (f32[200,200]{0,1:T(8,128)S(1)}, f32[200,200]{0,1:T(8,128)S(1)}, u32[]{:S(2)}, u32[]{:S(2)}) collective-permute-start(f32[200,200]{0,1:T(8,128)S(1)} %maximum_select_fusion.1), channel_id=1, source_target_pairs={{0,1},{1,0},{2,3},{3,2},{4,5},{5,4},{6,7},{7,6},{8,9},{9,8},{10,11... | collective-permute-start | bytes 480008 | tf_op jit(solution)/shard_map/ppermute | solution.py:54
  91.3 8.1 %copy-start = (f32[3,200,1024]{2,1,0:T(8,128)S(1)}, f32[3,200,1024]{2,1,0:T(8,128)}, u32[]{:S(2)}) copy-start(f32[3,200,1024]{2,1,0:T(8,128)} %param.6) | copy-start | bytes 7372804
  97.8 5.0 %collective-permute-start.9 = (f32[100,200]{0,1:T(8,128)S(1)}, f32[100,200]{0,1:T(8,128)S(1)}, u32[]{:S(2)}, u32[]{:S(2)}) collective-permute-start(f32[100,200]{0,1:T(8,128)S(1)} %slice_select_fusion.1), channel_id=1, source_target_pairs={{0,16},{8,24},{16,0},{24,8},{1,17},{9,25},{17,1},{25,9},{2,18},{10... | collective-permute-start | bytes 240008 | tf_op jit(solution)/shard_map/ppermute | solution.py:54
  103.0 4.7 %collective-permute-start.10 = (f32[50,200]{0,1:T(8,128)S(1)}, f32[50,200]{0,1:T(8,128)S(1)}, u32[]{:S(2)}, u32[]{:S(2)}) collective-permute-start(f32[50,200]{0,1:T(8,128)S(1)} %slice_select_fusion), channel_id=1, source_target_pairs={{0,8},{8,0},{16,24},{24,16},{1,9},{9,1},{17,25},{25,17},{2,10},{10... | collective-permute-start | bytes 120008 | tf_op jit(solution)/shard_map/ppermute | solution.py:54
Sparse Core Ops, SparseCore 0:
  43.1 28.3 all-gather.1

commit v7 on v6

--- a/solution.py
+++ b/solution.py
@@ -106,7 +106,8 @@
     system = jnp.eye(members, dtype=jnp.float32) + gram_matrix
     factor = block_cholesky(system, min(BLOCK, members - 8), highest)
 
-    group = lax.all_gather(packed, "tile", axis=0, tiled=True)
+    copies = jnp.broadcast_to(packed[None], (lax.axis_size("tile"),) + packed.shape)
+    group = lax.all_to_all(copies, "tile", 0, 0, tiled=False).reshape((-1, packed.shape[1]))
     factor, group = lax.optimization_barrier((factor, group))
     group_anom, group_innov, group_weight = (
         group[:, :members],

time: 118 us -> 106 us (0.90)
  between operations: 13.7 us -> 0.35 us
  starting transfers between devices: 17.5 us -> 21.4 us
  waiting for transfers between devices: 31.1 us -> 28.7 us
  local copies, waits for them, and re-layouts: 0.2 us -> 2.37 us
  matrix products: 12.5 us -> 10.8 us
    all_to_all x0 -> x1, starting transfers between devices: none -> 5.06 us  [shards(): lax.all_to_all(copies, 'tile', 0, 0, tiled=False)]
    ppermute x11, waiting for transfers between devices: 31.1 us -> 28.6 us  [swap(): return lax.ppermute(x, axis, [(i, i ^ k) for i in range(size)])]
    reduce_sum x1, other arithmetic: 0.16 us -> 2 us  [shards(): jnp.mean(prior_state, axis=1, keepdims=True)]
    dot_general x1, matrix products: 3.38 us -> 1.93 us  [shards(): lax.dot_general(jnp.concatenate([group_anom, group_innov], 1), tapered, (...]
    broadcast_in_dim x0 -> x1, local copies, waits for them, and re-layouts: none -> 1.28 us  [shards(): jnp.broadcast_to(packed[None], (lax.axis_size('tile'),) + packed.shape)]
  transfers between devices with their start and end apart: 12 -> 12, of which waited for: 11 -> 10; matrix products, arithmetic and copies ran while one was open for 33% -> 39% of each run, Pallas kernels for 0% -> 0%
where the time goes in v7:
time: 106 us
  other arithmetic  42.5 us (40%)
  waiting for transfers between devices  28.7 us (27%)
  starting transfers between devices  21.4 us (20%)
  matrix products  10.8 us (10%)
  local copies, waits for them, and re-layouts  2.37 us (2%)
    ppermute x11, waiting for transfers between devices, swap(): return lax.ppermute(x, axis, [(i, i ^ k) for i in range(size)])  28.6 us
    another operation x4, other arithmetic, lower_inverse(): lax.linalg.triangular_solve(factor, eye, left_side=True, lower=True, tran...  16.6 us
    ppermute x11, starting transfers between devices, swap(): return lax.ppermute(x, axis, [(i, i ^ k) for i in range(size)])  16.4 us
    another operation x3, other arithmetic, block_cholesky(): l11 = lax.linalg.cholesky(a11, symmetrize_input=False)  12.4 us
    another operation x3, other arithmetic, block_cholesky(): lax.linalg.cholesky(a22 - jnp.dot(l21, l21.T, precision=precision), symme...  7.25 us
    all_to_all x1, starting transfers between devices, shards(): lax.all_to_all(copies, 'tile', 0, 0, tiled=False)  5.06 us
    dot_general x1, matrix products, shards(): jnp.einsum('vnc,mn->vmc', state_anom, space_t, precision=highest)  2.73 us
  transfers between devices with their start and end apart: 12, of which 10 were waited for; matrix products, arithmetic and copies ran while one was open for 39% of the time, Pallas kernels for 0%

profile of v7, /device:TPU:0, one launch (start us, length us, event | category | flops | bytes accessed | tf_op | source)
XLA Modules:
  0.0 106.1 jit_solution(2658386240268635412)
XLA Ops:
  0.0 0.9 reduce_sum.18
  0.9 0.7 broadcast_multiply_fusion.1
  1.6 1.0 subtract_multiply_fusion
  2.6 1.2 %fusion.31 = f32[200,200]{0,1:T(8,128)S(1)} fusion(f32[128,200]{0,1:T(8,128)S(1)} %get-tuple-element.20, f32[128,200]{0,1:T(8,128)} %param.7, f32[128]{0:T(128)S(1)} %get-tuple-element.17, f32[128]{0:T(128)S(1)} %get-tuple-element.23), kind=kOutput, calls=%fused_computation.51 | convolution fusion | flops 61491200 | bytes 365824 | tf_op jit(solution)/shard_map/dot_general | solution.py:96
  3.8 1.3 %broadcast_select_fusion = (f32[200,200]{0,1:T(8,128)S(1)}, f32[200,200]{0,1:T(8,128)S(1)}) fusion(f32[200,200]{0,1:T(8,128)S(1)} %fusion.31, pred[]{:T(512)S(6)} %eq.37, f32[128,200]{0,1:T(8,128)} %param.7, f32[128]{0:T(128)S(1)} %get-tuple-element.17, f32[128]{0:T(128)S(1)} %get-tuple-element.23), kind=kOutput, calls=%fused_computation.41 | convolution fusion | flops 61582400 | bytes 583425 | tf_op jit(solution)/shard_map/dot_general | solution.py:95
  5.7 1.1 %collective-permute-done = f32[200,200]{0,1:T(8,128)S(1)} collective-permute-done((f32[200,200]{0,1:T(8,128)S(1)}, f32[200,200]{0,1:T(8,128)S(1)}, u32[]{:S(2)}, u32[]{:S(2)}) %collective-permute-start) | collective-permute-done | bytes 160032 | tf_op jit(solution)/shard_map/ppermute | solution.py:54
  6.9 2.9 %collective-permute-start.1 = (f32[100,200]{0,1:T(8,128)S(1)}, f32[100,200]{0,1:T(8,128)S(1)}, u32[]{:S(2)}, u32[]{:S(2)}) collective-permute-start(f32[100,200]{0,1:T(8,128)S(1)} %slice_select_fusion.4), channel_id=1, source_target_pairs={{0,8},{8,0},{16,24},{24,16},{1,9},{9,1},{17,25},{25,17},{2,10},{10... | collective-permute-start | bytes 240008 | tf_op jit(solution)/shard_map/ppermute | solution.py:54
  9.8 3.2 %collective-permute-done.1 = f32[100,200]{0,1:T(8,128)S(1)} collective-permute-done((f32[100,200]{0,1:T(8,128)S(1)}, f32[100,200]{0,1:T(8,128)S(1)}, u32[]{:S(2)}, u32[]{:S(2)}) %collective-permute-start.1) | collective-permute-done | bytes 80032 | tf_op jit(solution)/shard_map/ppermute | solution.py:54
  13.2 1.8 %collective-permute-start.2 = (f32[50,200]{0,1:T(8,128)S(1)}, f32[50,200]{0,1:T(8,128)S(1)}, u32[]{:S(2)}, u32[]{:S(2)}) collective-permute-start(f32[50,200]{0,1:T(8,128)S(1)} %slice_select_fusion.3), channel_id=1, source_target_pairs={{0,16},{8,24},{16,0},{24,8},{1,17},{9,25},{17,1},{25,9},{2,18},{10... | collective-permute-start | bytes 120008 | tf_op jit(solution)/shard_map/ppermute | solution.py:54
  15.0 2.9 %collective-permute-done.2 = f32[50,200]{0,1:T(8,128)S(1)} collective-permute-done((f32[50,200]{0,1:T(8,128)S(1)}, f32[50,200]{0,1:T(8,128)S(1)}, u32[]{:S(2)}, u32[]{:S(2)}) %collective-permute-start.2) | collective-permute-done | bytes 40032 | tf_op jit(solution)/shard_map/ppermute | solution.py:54
  18.1 1.9 %collective-permute-start.3 = (f32[25,200]{0,1:T(8,128)S(1)}, f32[25,200]{0,1:T(8,128)S(1)}, u32[]{:S(2)}, u32[]{:S(2)}) collective-permute-start(f32[25,200]{0,1:T(8,128)S(1)} %slice_select_fusion.2), channel_id=1, source_target_pairs={{0,2},{1,3},{2,0},{3,1},{4,6},{5,7},{6,4},{7,5},{8,10},{9,11},{10,... | collective-permute-start | bytes 60008 | tf_op jit(solution)/shard_map/ppermute | solution.py:54
  20.0 2.8 %collective-permute-done.3 = f32[25,200]{0,1:T(8,128)S(1)} collective-permute-done((f32[25,200]{0,1:T(8,128)S(1)}, f32[25,200]{0,1:T(8,128)S(1)}, u32[]{:S(2)}, u32[]{:S(2)}) %collective-permute-start.3) | collective-permute-done | bytes 20032 | tf_op jit(solution)/shard_map/ppermute | solution.py:54
  23.0 3.3 %collective-permute-start.4 = (f32[25,200]{0,1:T(8,128)S(1)}, f32[25,200]{0,1:T(8,128)S(1)}, u32[]{:S(2)}, u32[]{:S(2)}) collective-permute-start(f32[25,200]{0,1:T(8,128)S(1)} %select_add_fusion.2), channel_id=1, source_target_pairs={{0,4},{1,5},{2,6},{3,7},{4,0},{5,1},{6,2},{7,3},{8,12},{9,13},{10,... | collective-permute-start | bytes 60008 | tf_op jit(solution)/shard_map/ppermute | solution.py:54
  26.3 3.7 %collective-permute-done.4 = f32[25,200]{0,1:T(8,128)S(1)} collective-permute-done((f32[25,200]{0,1:T(8,128)S(1)}, f32[25,200]{0,1:T(8,128)S(1)}, u32[]{:S(2)}, u32[]{:S(2)}) %collective-permute-start.4) | collective-permute-done | bytes 20032 | tf_op jit(solution)/shard_map/ppermute | solution.py:54
  30.6 4.1 %collective-permute-done.5 = f32[25,200]{0,1:T(8,128)S(1)} collective-permute-done((f32[25,200]{0,1:T(8,128)S(1)}, f32[25,200]{0,1:T(8,128)S(1)}, u32[]{:S(2)}, u32[]{:S(2)}) %collective-permute-start.5) | collective-permute-done | bytes 20032 | tf_op jit(solution)/shard_map/ppermute | solution.py:54
  34.8 1.6 %collective-permute-start.6 = (f32[50,200]{0,1:T(8,128)S(1)}, f32[50,200]{0,1:T(8,128)S(1)}, u32[]{:S(2)}, u32[]{:S(2)}) collective-permute-start(f32[50,200]{0,1:T(8,128)S(1)} %maximum_select_fusion.2), channel_id=1, source_target_pairs={{0,16},{8,24},{16,0},{24,8},{1,17},{9,25},{17,1},{25,9},{2,18},{10... | collective-permute-start | bytes 120008 | tf_op jit(solution)/shard_map/ppermute | solution.py:54
  36.4 1.3 %broadcast_in_dim.7 = f32[8,128,401]{1,2,0:T(8,128)} broadcast(f32[128,401]{0,1:T(8,128)S(1)} %pad_maximum_fusion), dimensions={1,2} | broadcast | bytes 1847808 | tf_op jit(solution)/shard_map/broadcast_in_dim | solution.py:109
  37.7 5.1 %all-to-all-start = ((f32[8,128,401]{1,2,0:T(8,128)}), f32[8,128,401]{1,2,0:T(8,128)S(1)}, u32[]{:S(2)}, u32[]{:S(2)}) async-start(f32[8,128,401]{1,2,0:T(8,128)} %broadcast_in_dim.7), calls=%async_computation | async-start | bytes 3342336 | tf_op jit(solution)/shard_map/all_to_all | solution.py:110
  42.9 1.5 %collective-permute-start.7 = (f32[100,200]{0,1:T(8,128)S(1)}, f32[100,200]{0,1:T(8,128)S(1)}, u32[]{:S(2)}, u32[]{:S(2)}) collective-permute-start(f32[100,200]{0,1:T(8,128)S(1)} %maximum_select_fusion.3), channel_id=1, source_target_pairs={{0,8},{8,0},{16,24},{24,16},{1,9},{9,1},{17,25},{25,17},{2,10},{10... | collective-permute-start | bytes 240008 | tf_op jit(solution)/shard_map/ppermute | solution.py:54
  44.5 3.8 %collective-permute-done.7 = f32[100,200]{0,1:T(8,128)S(1)} collective-permute-done((f32[100,200]{0,1:T(8,128)S(1)}, f32[100,200]{0,1:T(8,128)S(1)}, u32[]{:S(2)}, u32[]{:S(2)}) %collective-permute-start.7) | collective-permute-done | bytes 80032 | tf_op jit(solution)/shard_map/ppermute | solution.py:54
  48.6 1.4 %collective-permute-done.8 = f32[200,200]{0,1:T(8,128)S(1)} collective-permute-done((f32[200,200]{0,1:T(8,128)S(1)}, f32[200,200]{0,1:T(8,128)S(1)}, u32[]{:S(2)}, u32[]{:S(2)}) %collective-permute-start.8) | collective-permute-done | bytes 160032 | tf_op jit(solution)/shard_map/ppermute | solution.py:54
  50.4 11.7 %cholesky.35 = f32[128,128]{1,0:T(8,128)S(1)} custom-call(f32[128,128]{1,0:T(8,128)S(1)} %cholesky.77), custom_call_target="Cholesky" | custom-call | tf_op jit(solution)/shard_map/cholesky | solution.py:17
  62.8 0.7 fusion.35
  63.5 9.8 %custom-call.10 = f32[1,128,128]{1,2,0:T(8,128)S(1)} custom-call(f32[1,128,128]{2,1,0:T(8,128)S(1)} %fusion.35), custom_call_target="InvertDiagBlocksLowerTriangular" | custom-call | tf_op jit(solution)/shard_map/triangular_solve | solution.py:11
  74.0 6.6 %cholesky.68 = f32[72,72]{1,0:T(8,128)S(1)} custom-call(f32[72,72]{1,0:T(8,128)S(1)} %convolution_subtract_fusion.2), custom_call_target="Cholesky" | custom-call | tf_op jit(solution)/shard_map/cholesky | solution.py:20
  82.0 5.5 %custom-call.11 = f32[1,72,72]{1,2,0:T(8,128)S(1)} custom-call(f32[1,72,72]{2,1,0:T(8,128)S(1)} %fusion.43), custom_call_target="InvertDiagBlocksLowerTriangular" | custom-call | tf_op jit(solution)/shard_map/triangular_solve | solution.py:11
  90.8 1.9 %fusion.3 = f32[400,200]{0,1:T(8,128)S(1)} fusion(f32[1024,401]{0,1:T(8,128)S(1)} %bitcast.48, f32[1024]{0:T(1024)S(1)} %bitcast.51), kind=kOutput, calls=%fused_computation.4 | convolution fusion | flops 983244800 | bytes 2781696 | tf_op jit(solution)/shard_map/dot_general | solution.py:120
  94.0 2.0 %reduce_sum.19 = f32[3,1024]{1,0:T(4,128)S(1)} reduce(f32[3,200,1024]{2,1,0:T(8,128)} %param.6, f32[]{:T(128)} %constant.155.clone.1), dimensions={1}, to_apply=%region_5.6 | reduce | flops 611328 | bytes 2469892 | tf_op jit(solution)/shard_map/reduce_sum | solution.py:138
  96.0 2.4 %collective-permute-done.9 = f32[100,200]{0,1:T(8,128)S(1)} collective-permute-done((f32[100,200]{0,1:T(8,128)S(1)}, f32[100,200]{0,1:T(8,128)S(1)}, u32[]{:S(2)}, u32[]{:S(2)}) %collective-permute-start.9) | collective-permute-done | bytes 80032 | tf_op jit(solution)/shard_map/ppermute | solution.py:54
  98.6 1.5 %collective-permute-start.10 = (f32[50,200]{0,1:T(8,128)S(1)}, f32[50,200]{0,1:T(8,128)S(1)}, u32[]{:S(2)}, u32[]{:S(2)}) collective-permute-start(f32[50,200]{0,1:T(8,128)S(1)} %slice_select_fusion), channel_id=1, source_target_pairs={{0,8},{8,0},{16,24},{24,16},{1,9},{9,1},{17,25},{25,17},{2,10},{10... | collective-permute-start | bytes 120008 | tf_op jit(solution)/shard_map/ppermute | solution.py:54
  100.2 3.2 %collective-permute-done.10 = f32[50,200]{0,1:T(8,128)S(1)} collective-permute-done((f32[50,200]{0,1:T(8,128)S(1)}, f32[50,200]{0,1:T(8,128)S(1)}, u32[]{:S(2)}, u32[]{:S(2)}) %collective-permute-start.10) | collective-permute-done | bytes 40032 | tf_op jit(solution)/shard_map/ppermute | solution.py:54
  103.3 2.7 %fusion.8 = f32[3,50,1024]{2,1,0:T(8,128)} fusion(f32[3,200,1024]{2,1,0:T(8,128)S(1)} %copy-done, f32[3,1024]{1,0:T(4,128)S(1)} %broadcast_multiply_fusion, s32[]{:T(128)S(6)} %select_n.147, f32[50,200]{0,1:T(8,128)S(1)} %collective-permute-done.10, f32[100,200]{0,1:T(8,128)S(1)} %select_add_fusion.1, pred[]{:T(512)S(6)} %eq.34), kind=kOutput, calls=%fused_computation.7 | convolution fusion | flops 370042400 | bytes 4083717 | tf_op jit(solution)/shard_map/vnc,mn->vmc/dot_general | solution.py:139
  (56 shorter events, 10.0 us)
Async XLA Ops:
  5.2 1.6 %collective-permute-start = (f32[200,200]{0,1:T(8,128)S(1)}, f32[200,200]{0,1:T(8,128)S(1)}, u32[]{:S(2)}, u32[]{:S(2)}) collective-permute-start(f32[200,200]{0,1:T(8,128)S(1)} %get-tuple-element.21), channel_id=1, source_target_pairs={{0,1},{1,0},{2,3},{3,2},{4,5},{5,4},{6,7},{7,6},{8,9},{9,8},{10,11... | collective-permute-start | bytes 480008 | tf_op jit(solution)/shard_map/ppermute | solution.py:54
  6.9 6.1 %collective-permute-start.1 = (f32[100,200]{0,1:T(8,128)S(1)}, f32[100,200]{0,1:T(8,128)S(1)}, u32[]{:S(2)}, u32[]{:S(2)}) collective-permute-start(f32[100,200]{0,1:T(8,128)S(1)} %slice_select_fusion.4), channel_id=1, source_target_pairs={{0,8},{8,0},{16,24},{24,16},{1,9},{9,1},{17,25},{25,17},{2,10},{10... | collective-permute-start | bytes 240008 | tf_op jit(solution)/shard_map/ppermute | solution.py:54
  13.2 4.7 %collective-permute-start.2 = (f32[50,200]{0,1:T(8,128)S(1)}, f32[50,200]{0,1:T(8,128)S(1)}, u32[]{:S(2)}, u32[]{:S(2)}) collective-permute-start(f32[50,200]{0,1:T(8,128)S(1)} %slice_select_fusion.3), channel_id=1, source_target_pairs={{0,16},{8,24},{16,0},{24,8},{1,17},{9,25},{17,1},{25,9},{2,18},{10... | collective-permute-start | bytes 120008 | tf_op jit(solution)/shard_map/ppermute | solution.py:54
  18.1 4.7 %collective-permute-start.3 = (f32[25,200]{0,1:T(8,128)S(1)}, f32[25,200]{0,1:T(8,128)S(1)}, u32[]{:S(2)}, u32[]{:S(2)}) collective-permute-start(f32[25,200]{0,1:T(8,128)S(1)} %slice_select_fusion.2), channel_id=1, source_target_pairs={{0,2},{1,3},{2,0},{3,1},{4,6},{5,7},{6,4},{7,5},{8,10},{9,11},{10,... | collective-permute-start | bytes 60008 | tf_op jit(solution)/shard_map/ppermute | solution.py:54
  23.0 7.0 %collective-permute-start.4 = (f32[25,200]{0,1:T(8,128)S(1)}, f32[25,200]{0,1:T(8,128)S(1)}, u32[]{:S(2)}, u32[]{:S(2)}) collective-permute-start(f32[25,200]{0,1:T(8,128)S(1)} %select_add_fusion.2), channel_id=1, source_target_pairs={{0,4},{1,5},{2,6},{3,7},{4,0},{5,1},{6,2},{7,3},{8,12},{9,13},{10,... | collective-permute-start | bytes 60008 | tf_op jit(solution)/shard_map/ppermute | solution.py:54
  30.0 4.7 %collective-permute-start.5 = (f32[25,200]{0,1:T(8,128)S(1)}, f32[25,200]{0,1:T(8,128)S(1)}, u32[]{:S(2)}, u32[]{:S(2)}) collective-permute-start(f32[25,200]{0,1:T(8,128)S(1)} %add.77), channel_id=1, source_target_pairs={{0,2},{1,3},{2,0},{3,1},{4,6},{5,7},{6,4},{7,5},{8,10},{9,11},{10,... | collective-permute-start | bytes 60008 | tf_op jit(solution)/shard_map/ppermute | solution.py:54
  34.8 7.9 %collective-permute-start.6 = (f32[50,200]{0,1:T(8,128)S(1)}, f32[50,200]{0,1:T(8,128)S(1)}, u32[]{:S(2)}, u32[]{:S(2)}) collective-permute-start(f32[50,200]{0,1:T(8,128)S(1)} %maximum_select_fusion.2), channel_id=1, source_target_pairs={{0,16},{8,24},{16,0},{24,8},{1,17},{9,25},{17,1},{25,9},{2,18},{10... | collective-permute-start | bytes 120008 | tf_op jit(solution)/shard_map/ppermute | solution.py:54
  37.7 10.8 %copy-start.1 = (s32[1,8]{1,0:T(1,128)S(1)}, s32[1,8]{1,0:T(1,128)}, u32[]{:S(2)}) copy-start(s32[1,8]{1,0:T(1,128)} %param.11) | copy-start | bytes 100
  37.7 10.8 %copy-start.2 = (s32[1,8]{1,0:T(1,128)S(1)}, s32[1,8]{1,0:T(1,128)}, u32[]{:S(2)}) copy-start(s32[1,8]{1,0:T(1,128)} %param.10) | copy-start | bytes 100
  37.7 50.0 %all-to-all-start = ((f32[8,128,401]{1,2,0:T(8,128)}), f32[8,128,401]{1,2,0:T(8,128)S(1)}, u32[]{:S(2)}, u32[]{:S(2)}) async-start(f32[8,128,401]{1,2,0:T(8,128)} %broadcast_in_dim.7), calls=%async_computation | async-start | bytes 3342336 | tf_op jit(solution)/shard_map/all_to_all | solution.py:110
  42.9 5.4 %collective-permute-start.7 = (f32[100,200]{0,1:T(8,128)S(1)}, f32[100,200]{0,1:T(8,128)S(1)}, u32[]{:S(2)}, u32[]{:S(2)}) collective-permute-start(f32[100,200]{0,1:T(8,128)S(1)} %maximum_select_fusion.3), channel_id=1, source_target_pairs={{0,8},{8,0},{16,24},{24,16},{1,9},{9,1},{17,25},{25,17},{2,10},{10... | collective-permute-start | bytes 240008 | tf_op jit(solution)/shard_map/ppermute | solution.py:54
  48.5 1.5 %collective-permute-start.8 = (f32[200,200]{0,1:T(8,128)S(1)}, f32[200,200]{0,1:T(8,128)S(1)}, u32[]{:S(2)}, u32[]{:S(2)}) collective-permute-start(f32[200,200]{0,1:T(8,128)S(1)} %maximum_select_fusion.1), channel_id=1, source_target_pairs={{0,1},{1,0},{2,3},{3,2},{4,5},{5,4},{6,7},{7,6},{8,9},{9,8},{10,11... | collective-permute-start | bytes 480008 | tf_op jit(solution)/shard_map/ppermute | solution.py:54
  93.4 9.9 %copy-start = (f32[3,200,1024]{2,1,0:T(8,128)S(1)}, f32[3,200,1024]{2,1,0:T(8,128)}, u32[]{:S(2)}) copy-start(f32[3,200,1024]{2,1,0:T(8,128)} %param.6) | copy-start | bytes 7372804
  93.4 5.0 %collective-permute-start.9 = (f32[100,200]{0,1:T(8,128)S(1)}, f32[100,200]{0,1:T(8,128)S(1)}, u32[]{:S(2)}, u32[]{:S(2)}) collective-permute-start(f32[100,200]{0,1:T(8,128)S(1)} %slice_select_fusion.1), channel_id=1, source_target_pairs={{0,16},{8,24},{16,0},{24,8},{1,17},{9,25},{17,1},{25,9},{2,18},{10... | collective-permute-start | bytes 240008 | tf_op jit(solution)/shard_map/ppermute | solution.py:54
  98.6 4.7 %collective-permute-start.10 = (f32[50,200]{0,1:T(8,128)S(1)}, f32[50,200]{0,1:T(8,128)S(1)}, u32[]{:S(2)}, u32[]{:S(2)}) collective-permute-start(f32[50,200]{0,1:T(8,128)S(1)} %slice_select_fusion), channel_id=1, source_target_pairs={{0,8},{8,0},{16,24},{24,16},{1,9},{9,1},{17,25},{25,17},{2,10},{10... | collective-permute-start | bytes 120008 | tf_op jit(solution)/shard_map/ppermute | solution.py:54

commit v8 on v7

--- a/solution.py
+++ b/solution.py
@@ -63,21 +63,17 @@
     return out
 
 
-def all_sum(x, steps, tie):
-    halved = []
-    for axis, k in steps:
-        rows = x.shape[0]
-        if rows % 2 == 0:
-            half = rows // 2
-            hi = bit_of(axis, k) == 1
-            keep = jnp.where(hi, x[half:], x[:half])
-            send = jnp.where(hi, x[:half], x[half:])
-            x = keep + swap(send, axis, k)
-            halved.append((axis, k))
-        else:
-            x = x + swap(x, axis, k)
+def all_sum(x, steps, halvings, tie):
+    for axis, k in steps[:halvings]:
+        half = x.shape[0] // 2
+        hi = bit_of(axis, k) == 1
+        keep = jnp.where(hi, x[half:], x[:half])
+        send = jnp.where(hi, x[:half], x[half:])
+        x = keep + swap(send, axis, k)
+    for axis, k in steps[halvings:]:
+        x = x + swap(x, axis, k)
     x, tie = lax.optimization_barrier((x, tie))
-    for axis, k in reversed(halved):
+    for axis, k in reversed(steps[:halvings]):
         other = swap(x, axis, k)
         hi = bit_of(axis, k) == 1
         x = jnp.where(hi, jnp.concatenate([other, x], 0), jnp.concatenate([x, other], 0))
@@ -99,7 +95,7 @@
     )
     packed = jnp.concatenate([data_anom, innov, row_weight[:, None]], 1)
     order = axis_bits("tile")[:1] + axis_bits("well") + axis_bits("tile")[1:]
-    stacked, packed = all_sum(stacked, order, packed)
+    stacked, packed = all_sum(stacked, order, 2, packed)
     gram_matrix, cross_matrix = stacked[:members], stacked[members:]
     own_count = members // lax.axis_size("well")
     own_start = lax.axis_index("well") * own_count

time: 106 us -> 99.3 us (0.937)
  waiting for transfers between devices: 28.7 us -> 23.7 us
  starting transfers between devices: 21.4 us -> 20.1 us
    ppermute x11 -> x9, waiting for transfers between devices: 28.6 us -> 23.7 us  [swap(): return lax.ppermute(x, axis, [(i, i ^ k) for i in range(size)])]
    ppermute x11 -> x9, starting transfers between devices: 16.4 us -> 15.2 us  [swap(): return lax.ppermute(x, axis, [(i, i ^ k) for i in range(size)])]
  transfers between devices with their start and end apart: 12 -> 10, of which waited for: 10 -> 9; matrix products, arithmetic and copies ran while one was open for 39% -> 40% of each run, Pallas kernels for 0% -> 0%
where the time goes in v8:
time: 99.3 us; the launch traced here: 99 us
  other arithmetic  41.7 us (42%)
  waiting for transfers between devices  23.7 us (24%)
  starting transfers between devices  20.1 us (20%)
  matrix products  10.8 us (11%)
  local copies, waits for them, and re-layouts  2.38 us (2%)
    ppermute x9, waiting for transfers between devices, swap(): return lax.ppermute(x, axis, [(i, i ^ k) for i in range(size)])  23.7 us
    another operation x4, other arithmetic, lower_inverse(): lax.linalg.triangular_solve(factor, eye, left_side=True, lower=True, tran...  16.6 us
    ppermute x9, starting transfers between devices, swap(): return lax.ppermute(x, axis, [(i, i ^ k) for i in range(size)])  15.2 us
    another operation x3, other arithmetic, block_cholesky(): l11 = lax.linalg.cholesky(a11, symmetrize_input=False)  12.4 us
    another operation x3, other arithmetic, block_cholesky(): lax.linalg.cholesky(a22 - jnp.dot(l21, l21.T, precision=precision), symme...  7.25 us
    all_to_all x1, starting transfers between devices, shards(): lax.all_to_all(copies, 'tile', 0, 0, tiled=False)  4.85 us
    dot_general x1, matrix products, shards(): jnp.einsum('vnc,mn->vmc', state_anom, space_t, precision=highest)  2.73 us
  transfers between devices with their start and end apart: 10, of which 9 were waited for; matrix products, arithmetic and copies ran while one was open for 40% of the time, Pallas kernels for 0%

profile of v8, /device:TPU:0, one launch (start us, length us, event | category | flops | bytes accessed | tf_op | source)
XLA Modules:
  0.0 99.0 jit_solution(17038854523841809878)
XLA Ops:
  0.0 0.9 reduce_sum.18
  0.9 0.7 broadcast_multiply_fusion.1
  1.6 1.0 subtract_multiply_fusion
  2.6 1.2 %fusion.31 = f32[200,200]{0,1:T(8,128)S(1)} fusion(f32[128,200]{0,1:T(8,128)S(1)} %get-tuple-element.20, f32[128,200]{0,1:T(8,128)} %param.7, f32[128]{0:T(128)S(1)} %get-tuple-element.17, f32[128]{0:T(128)S(1)} %get-tuple-element.23), kind=kOutput, calls=%fused_computation.45 | convolution fusion | flops 61491200 | bytes 365824 | tf_op jit(solution)/shard_map/dot_general | solution.py:92
  3.8 1.3 %broadcast_select_fusion = (f32[200,200]{0,1:T(8,128)S(1)}, f32[200,200]{0,1:T(8,128)S(1)}) fusion(f32[200,200]{0,1:T(8,128)S(1)} %fusion.31, pred[]{:T(512)S(6)} %eq.27, f32[128,200]{0,1:T(8,128)} %param.7, f32[128]{0:T(128)S(1)} %get-tuple-element.17, f32[128]{0:T(128)S(1)} %get-tuple-element.23), kind=kOutput, calls=%fused_computation.37 | convolution fusion | flops 61582400 | bytes 583425 | tf_op jit(solution)/shard_map/dot_general | solution.py:91
  5.7 1.1 %collective-permute-done = f32[200,200]{0,1:T(8,128)S(1)} collective-permute-done((f32[200,200]{0,1:T(8,128)S(1)}, f32[200,200]{0,1:T(8,128)S(1)}, u32[]{:S(2)}, u32[]{:S(2)}) %collective-permute-start) | collective-permute-done | bytes 160032 | tf_op jit(solution)/shard_map/ppermute | solution.py:54
  6.9 2.9 %collective-permute-start.1 = (f32[100,200]{0,1:T(8,128)S(1)}, f32[100,200]{0,1:T(8,128)S(1)}, u32[]{:S(2)}, u32[]{:S(2)}) collective-permute-start(f32[100,200]{0,1:T(8,128)S(1)} %slice_select_fusion.2), channel_id=1, source_target_pairs={{0,8},{8,0},{16,24},{24,16},{1,9},{9,1},{17,25},{25,17},{2,10},{10... | collective-permute-start | bytes 240008 | tf_op jit(solution)/shard_map/ppermute | solution.py:54
  9.8 3.2 %collective-permute-done.1 = f32[100,200]{0,1:T(8,128)S(1)} collective-permute-done((f32[100,200]{0,1:T(8,128)S(1)}, f32[100,200]{0,1:T(8,128)S(1)}, u32[]{:S(2)}, u32[]{:S(2)}) %collective-permute-start.1) | collective-permute-done | bytes 80032 | tf_op jit(solution)/shard_map/ppermute | solution.py:54
  13.1 1.8 %collective-permute-start.2 = (f32[100,200]{0,1:T(8,128)S(1)}, f32[100,200]{0,1:T(8,128)S(1)}, u32[]{:S(2)}, u32[]{:S(2)}) collective-permute-start(f32[100,200]{0,1:T(8,128)S(1)} %select_add_fusion.2), channel_id=1, source_target_pairs={{0,16},{8,24},{16,0},{24,8},{1,17},{9,25},{17,1},{25,9},{2,18},{10... | collective-permute-start | bytes 240008 | tf_op jit(solution)/shard_map/ppermute | solution.py:54
  14.9 2.9 %collective-permute-done.2 = f32[100,200]{0,1:T(8,128)S(1)} collective-permute-done((f32[100,200]{0,1:T(8,128)S(1)}, f32[100,200]{0,1:T(8,128)S(1)}, u32[]{:S(2)}, u32[]{:S(2)}) %collective-permute-start.2) | collective-permute-done | bytes 80032 | tf_op jit(solution)/shard_map/ppermute | solution.py:54
  17.9 1.9 %collective-permute-start.3 = (f32[100,200]{0,1:T(8,128)S(1)}, f32[100,200]{0,1:T(8,128)S(1)}, u32[]{:S(2)}, u32[]{:S(2)}) collective-permute-start(f32[100,200]{0,1:T(8,128)S(1)} %add.67), channel_id=1, source_target_pairs={{0,2},{1,3},{2,0},{3,1},{4,6},{5,7},{6,4},{7,5},{8,10},{9,11},{10,... | collective-permute-start | bytes 240008 | tf_op jit(solution)/shard_map/ppermute | solution.py:54
  19.7 2.8 %collective-permute-done.3 = f32[100,200]{0,1:T(8,128)S(1)} collective-permute-done((f32[100,200]{0,1:T(8,128)S(1)}, f32[100,200]{0,1:T(8,128)S(1)}, u32[]{:S(2)}, u32[]{:S(2)}) %collective-permute-start.3) | collective-permute-done | bytes 80032 | tf_op jit(solution)/shard_map/ppermute | solution.py:54
  22.6 3.4 %collective-permute-start.4 = (f32[100,200]{0,1:T(8,128)S(1)}, f32[100,200]{0,1:T(8,128)S(1)}, u32[]{:S(2)}, u32[]{:S(2)}) collective-permute-start(f32[100,200]{0,1:T(8,128)S(1)} %add.68), channel_id=1, source_target_pairs={{0,4},{1,5},{2,6},{3,7},{4,0},{5,1},{6,2},{7,3},{8,12},{9,13},{10,... | collective-permute-start | bytes 240008 | tf_op jit(solution)/shard_map/ppermute | solution.py:54
  26.0 3.7 %collective-permute-done.4 = f32[100,200]{0,1:T(8,128)S(1)} collective-permute-done((f32[100,200]{0,1:T(8,128)S(1)}, f32[100,200]{0,1:T(8,128)S(1)}, u32[]{:S(2)}, u32[]{:S(2)}) %collective-permute-start.4) | collective-permute-done | bytes 80032 | tf_op jit(solution)/shard_map/ppermute | solution.py:54
  29.7 1.3 %broadcast_in_dim.7 = f32[8,128,401]{1,2,0:T(8,128)} broadcast(f32[128,401]{0,1:T(8,128)S(1)} %pad_maximum_fusion), dimensions={1,2} | broadcast | bytes 1847808 | tf_op jit(solution)/shard_map/broadcast_in_dim | solution.py:105
  31.0 4.9 %all-to-all-start = ((f32[8,128,401]{1,2,0:T(8,128)}), f32[8,128,401]{1,2,0:T(8,128)S(1)}, u32[]{:S(2)}, u32[]{:S(2)}) async-start(f32[8,128,401]{1,2,0:T(8,128)} %broadcast_in_dim.7), calls=%async_computation | async-start | bytes 3342336 | tf_op jit(solution)/shard_map/all_to_all | solution.py:106
  35.9 1.5 %collective-permute-start.5 = (f32[100,200]{0,1:T(8,128)S(1)}, f32[100,200]{0,1:T(8,128)S(1)}, u32[]{:S(2)}, u32[]{:S(2)}) collective-permute-start(f32[100,200]{0,1:T(8,128)S(1)} %add.69), channel_id=1, source_target_pairs={{0,8},{8,0},{16,24},{24,16},{1,9},{9,1},{17,25},{25,17},{2,10},{10... | collective-permute-start | bytes 240008 | tf_op jit(solution)/shard_map/ppermute | solution.py:54
  37.4 3.8 %collective-permute-done.5 = f32[100,200]{0,1:T(8,128)S(1)} collective-permute-done((f32[100,200]{0,1:T(8,128)S(1)}, f32[100,200]{0,1:T(8,128)S(1)}, u32[]{:S(2)}, u32[]{:S(2)}) %collective-permute-start.5) | collective-permute-done | bytes 80032 | tf_op jit(solution)/shard_map/ppermute | solution.py:54
  41.5 1.4 %collective-permute-done.6 = f32[200,200]{0,1:T(8,128)S(1)} collective-permute-done((f32[200,200]{0,1:T(8,128)S(1)}, f32[200,200]{0,1:T(8,128)S(1)}, u32[]{:S(2)}, u32[]{:S(2)}) %collective-permute-start.6) | collective-permute-done | bytes 160032 | tf_op jit(solution)/shard_map/ppermute | solution.py:54
  43.3 11.7 %cholesky.35 = f32[128,128]{1,0:T(8,128)S(1)} custom-call(f32[128,128]{1,0:T(8,128)S(1)} %cholesky.77), custom_call_target="Cholesky" | custom-call | tf_op jit(solution)/shard_map/cholesky | solution.py:17
  55.7 0.7 fusion.35
  56.4 9.8 %custom-call.10 = f32[1,128,128]{1,2,0:T(8,128)S(1)} custom-call(f32[1,128,128]{2,1,0:T(8,128)S(1)} %fusion.35), custom_call_target="InvertDiagBlocksLowerTriangular" | custom-call | tf_op jit(solution)/shard_map/triangular_solve | solution.py:11
  66.9 6.6 %cholesky.68 = f32[72,72]{1,0:T(8,128)S(1)} custom-call(f32[72,72]{1,0:T(8,128)S(1)} %convolution_subtract_fusion.2), custom_call_target="Cholesky" | custom-call | tf_op jit(solution)/shard_map/cholesky | solution.py:20
  74.2 0.7 fusion.43
  74.9 5.5 %custom-call.11 = f32[1,72,72]{1,2,0:T(8,128)S(1)} custom-call(f32[1,72,72]{2,1,0:T(8,128)S(1)} %fusion.43), custom_call_target="InvertDiagBlocksLowerTriangular" | custom-call | tf_op jit(solution)/shard_map/triangular_solve | solution.py:11
  83.7 1.9 %fusion.3 = f32[400,200]{0,1:T(8,128)S(1)} fusion(f32[1024,401]{0,1:T(8,128)S(1)} %bitcast.48, f32[1024]{0:T(1024)S(1)} %bitcast.51), kind=kOutput, calls=%fused_computation.4 | convolution fusion | flops 983244800 | bytes 2781696 | tf_op jit(solution)/shard_map/dot_general | solution.py:116
  86.3 1.6 %collective-permute-start.7 = (f32[100,200]{0,1:T(8,128)S(1)}, f32[100,200]{0,1:T(8,128)S(1)}, u32[]{:S(2)}, u32[]{:S(2)}) collective-permute-start(f32[100,200]{0,1:T(8,128)S(1)} %slice_select_fusion.1), channel_id=1, source_target_pairs={{0,16},{8,24},{16,0},{24,8},{1,17},{9,25},{17,1},{25,9},{2,18},{10... | collective-permute-start | bytes 240008 | tf_op jit(solution)/shard_map/ppermute | solution.py:54
  87.9 1.8 %reduce_sum.19 = f32[3,1024]{1,0:T(4,128)S(1)} reduce(f32[3,200,1024]{2,1,0:T(8,128)} %param.6, f32[]{:T(128)} %constant.132.clone.1), dimensions={1}, to_apply=%region_5.6 | reduce | flops 611328 | bytes 2469892 | tf_op jit(solution)/shard_map/reduce_sum | solution.py:134
  89.8 1.6 %collective-permute-done.7 = f32[100,200]{0,1:T(8,128)S(1)} collective-permute-done((f32[100,200]{0,1:T(8,128)S(1)}, f32[100,200]{0,1:T(8,128)S(1)}, u32[]{:S(2)}, u32[]{:S(2)}) %collective-permute-start.7) | collective-permute-done | bytes 80032 | tf_op jit(solution)/shard_map/ppermute | solution.py:54
  91.5 1.5 %collective-permute-start.8 = (f32[50,200]{0,1:T(8,128)S(1)}, f32[50,200]{0,1:T(8,128)S(1)}, u32[]{:S(2)}, u32[]{:S(2)}) collective-permute-start(f32[50,200]{0,1:T(8,128)S(1)} %slice_select_fusion), channel_id=1, source_target_pairs={{0,8},{8,0},{16,24},{24,16},{1,9},{9,1},{17,25},{25,17},{2,10},{10... | collective-permute-start | bytes 120008 | tf_op jit(solution)/shard_map/ppermute | solution.py:54
  93.1 3.2 %collective-permute-done.8 = f32[50,200]{0,1:T(8,128)S(1)} collective-permute-done((f32[50,200]{0,1:T(8,128)S(1)}, f32[50,200]{0,1:T(8,128)S(1)}, u32[]{:S(2)}, u32[]{:S(2)}) %collective-permute-start.8) | collective-permute-done | bytes 40032 | tf_op jit(solution)/shard_map/ppermute | solution.py:54
  96.2 2.7 %fusion.8 = f32[3,50,1024]{2,1,0:T(8,128)} fusion(f32[3,200,1024]{2,1,0:T(8,128)S(1)} %copy-done, f32[3,1024]{1,0:T(4,128)S(1)} %broadcast_multiply_fusion, s32[]{:T(128)S(6)} %select_n.99, f32[50,200]{0,1:T(8,128)S(1)} %collective-permute-done.8, f32[100,200]{0,1:T(8,128)S(1)} %select_add_fusion.1, pred[]{:T(512)S(6)} %eq.24), kind=kOutput, calls=%fused_computation.7 | convolution fusion | flops 370042400 | bytes 4083717 | tf_op jit(solution)/shard_map/vnc,mn->vmc/dot_general | solution.py:135
  (48 shorter events, 7.6 us)
Async XLA Ops:
  5.2 1.6 %collective-permute-start = (f32[200,200]{0,1:T(8,128)S(1)}, f32[200,200]{0,1:T(8,128)S(1)}, u32[]{:S(2)}, u32[]{:S(2)}) collective-permute-start(f32[200,200]{0,1:T(8,128)S(1)} %get-tuple-element.21), channel_id=1, source_target_pairs={{0,1},{1,0},{2,3},{3,2},{4,5},{5,4},{6,7},{7,6},{8,9},{9,8},{10,11... | collective-permute-start | bytes 480008 | tf_op jit(solution)/shard_map/ppermute | solution.py:54
  6.9 6.1 %collective-permute-start.1 = (f32[100,200]{0,1:T(8,128)S(1)}, f32[100,200]{0,1:T(8,128)S(1)}, u32[]{:S(2)}, u32[]{:S(2)}) collective-permute-start(f32[100,200]{0,1:T(8,128)S(1)} %slice_select_fusion.2), channel_id=1, source_target_pairs={{0,8},{8,0},{16,24},{24,16},{1,9},{9,1},{17,25},{25,17},{2,10},{10... | collective-permute-start | bytes 240008 | tf_op jit(solution)/shard_map/ppermute | solution.py:54
  13.1 4.7 %collective-permute-start.2 = (f32[100,200]{0,1:T(8,128)S(1)}, f32[100,200]{0,1:T(8,128)S(1)}, u32[]{:S(2)}, u32[]{:S(2)}) collective-permute-start(f32[100,200]{0,1:T(8,128)S(1)} %select_add_fusion.2), channel_id=1, source_target_pairs={{0,16},{8,24},{16,0},{24,8},{1,17},{9,25},{17,1},{25,9},{2,18},{10... | collective-permute-start | bytes 240008 | tf_op jit(solution)/shard_map/ppermute | solution.py:54
  17.9 4.7 %collective-permute-start.3 = (f32[100,200]{0,1:T(8,128)S(1)}, f32[100,200]{0,1:T(8,128)S(1)}, u32[]{:S(2)}, u32[]{:S(2)}) collective-permute-start(f32[100,200]{0,1:T(8,128)S(1)} %add.67), channel_id=1, source_target_pairs={{0,2},{1,3},{2,0},{3,1},{4,6},{5,7},{6,4},{7,5},{8,10},{9,11},{10,... | collective-permute-start | bytes 240008 | tf_op jit(solution)/shard_map/ppermute | solution.py:54
  22.6 7.1 %collective-permute-start.4 = (f32[100,200]{0,1:T(8,128)S(1)}, f32[100,200]{0,1:T(8,128)S(1)}, u32[]{:S(2)}, u32[]{:S(2)}) collective-permute-start(f32[100,200]{0,1:T(8,128)S(1)} %add.68), channel_id=1, source_target_pairs={{0,4},{1,5},{2,6},{3,7},{4,0},{5,1},{6,2},{7,3},{8,12},{9,13},{10,... | collective-permute-start | bytes 240008 | tf_op jit(solution)/shard_map/ppermute | solution.py:54
  31.0 10.4 %copy-start.1 = (s32[1,8]{1,0:T(1,128)S(1)}, s32[1,8]{1,0:T(1,128)}, u32[]{:S(2)}) copy-start(s32[1,8]{1,0:T(1,128)} %param.11) | copy-start | bytes 100
  31.0 10.4 %copy-start.2 = (s32[1,8]{1,0:T(1,128)S(1)}, s32[1,8]{1,0:T(1,128)}, u32[]{:S(2)}) copy-start(s32[1,8]{1,0:T(1,128)} %param.10) | copy-start | bytes 100
  31.0 49.6 %all-to-all-start = ((f32[8,128,401]{1,2,0:T(8,128)}), f32[8,128,401]{1,2,0:T(8,128)S(1)}, u32[]{:S(2)}, u32[]{:S(2)}) async-start(f32[8,128,401]{1,2,0:T(8,128)} %broadcast_in_dim.7), calls=%async_computation | async-start | bytes 3342336 | tf_op jit(solution)/shard_map/all_to_all | solution.py:106
  35.9 5.3 %collective-permute-start.5 = (f32[100,200]{0,1:T(8,128)S(1)}, f32[100,200]{0,1:T(8,128)S(1)}, u32[]{:S(2)}, u32[]{:S(2)}) collective-permute-start(f32[100,200]{0,1:T(8,128)S(1)} %add.69), channel_id=1, source_target_pairs={{0,8},{8,0},{16,24},{24,16},{1,9},{9,1},{17,25},{25,17},{2,10},{10... | collective-permute-start | bytes 240008 | tf_op jit(solution)/shard_map/ppermute | solution.py:54
  41.4 1.5 %collective-permute-start.6 = (f32[200,200]{0,1:T(8,128)S(1)}, f32[200,200]{0,1:T(8,128)S(1)}, u32[]{:S(2)}, u32[]{:S(2)}) collective-permute-start(f32[200,200]{0,1:T(8,128)S(1)} %maximum_select_fusion.1), channel_id=1, source_target_pairs={{0,1},{1,0},{2,3},{3,2},{4,5},{5,4},{6,7},{7,6},{8,9},{9,8},{10,11... | collective-permute-start | bytes 480008 | tf_op jit(solution)/shard_map/ppermute | solution.py:54
  86.3 9.9 %copy-start = (f32[3,200,1024]{2,1,0:T(8,128)S(1)}, f32[3,200,1024]{2,1,0:T(8,128)}, u32[]{:S(2)}) copy-start(f32[3,200,1024]{2,1,0:T(8,128)} %param.6) | copy-start | bytes 7372804
  86.3 5.0 %collective-permute-start.7 = (f32[100,200]{0,1:T(8,128)S(1)}, f32[100,200]{0,1:T(8,128)S(1)}, u32[]{:S(2)}, u32[]{:S(2)}) collective-permute-start(f32[100,200]{0,1:T(8,128)S(1)} %slice_select_fusion.1), channel_id=1, source_target_pairs={{0,16},{8,24},{16,0},{24,8},{1,17},{9,25},{17,1},{25,9},{2,18},{10... | collective-permute-start | bytes 240008 | tf_op jit(solution)/shard_map/ppermute | solution.py:54
  91.5 4.7 %collective-permute-start.8 = (f32[50,200]{0,1:T(8,128)S(1)}, f32[50,200]{0,1:T(8,128)S(1)}, u32[]{:S(2)}, u32[]{:S(2)}) collective-permute-start(f32[50,200]{0,1:T(8,128)S(1)} %slice_select_fusion), channel_id=1, source_target_pairs={{0,8},{8,0},{16,24},{24,16},{1,9},{9,1},{17,25},{25,17},{2,10},{10... | collective-permute-start | bytes 120008 | tf_op jit(solution)/shard_map/ppermute | solution.py:54

commit v9 on v8

--- a/solution.py
+++ b/solution.py
@@ -18,8 +18,7 @@
     inv11 = lower_inverse(l11, precision)
     l21 = jnp.dot(a21, inv11.T, precision=precision)
     l22 = lax.linalg.cholesky(a22 - jnp.dot(l21, l21.T, precision=precision), symmetrize_input=False)
-    inv22 = lower_inverse(l22, precision)
-    return inv11, l21, inv22
+    return inv11, l21, l22
 
 
 def forward(parts, right, precision):
@@ -100,11 +99,11 @@
     own_count = members // lax.axis_size("well")
     own_start = lax.axis_index("well") * own_count
     system = jnp.eye(members, dtype=jnp.float32) + gram_matrix
-    factor = block_cholesky(system, min(BLOCK, members - 8), highest)
+    head = block_cholesky(system, min(BLOCK, members - 8), highest)
 
     copies = jnp.broadcast_to(packed[None], (lax.axis_size("tile"),) + packed.shape)
     group = lax.all_to_all(copies, "tile", 0, 0, tiled=False).reshape((-1, packed.shape[1]))
-    factor, group = lax.optimization_barrier((factor, group))
+    head, group = lax.optimization_barrier((head, group))
     group_anom, group_innov, group_weight = (
         group[:, :members],
         group[:, members : 2 * members],
@@ -121,6 +120,9 @@
     )
     taper_gram, taper_cross_t = both[:members], both[members:]
 
+    head, taper_gram, taper_cross_t = lax.optimization_barrier((head, taper_gram, taper_cross_t))
+    inv11, l21, l22 = head
+    factor = (inv11, l21, lower_inverse(l22, highest))
     solved = backward(factor, *forward(factor, cross_matrix, highest), highest)
     space_t = taper_cross_t - lax.dot_general(
         solved, taper_gram, (((0,), (1,)), ((), ())), precision=highest

time: 99.3 us -> 98.7 us (level)
  other arithmetic: 41.7 us -> 39.8 us
  waiting for transfers between devices: 23.7 us -> 25.6 us
    reduce_sum x1, other arithmetic: 1.85 us -> 0.16 us  [shards(): jnp.mean(prior_state, axis=1, keepdims=True)]
  transfers between devices with their start and end apart: 10 -> 10, of which waited for: 9 -> 10; matrix products, arithmetic and copies ran while one was open for 40% -> 33% of each run, Pallas kernels for 0% -> 0%
where the time goes in v9:
time: 98.7 us; the launch traced here: 98.4 us
  other arithmetic  39.8 us (40%)
  waiting for transfers between devices  25.6 us (26%)
  starting transfers between devices  20.1 us (20%)
  matrix products  10.2 us (10%)
  local copies, waits for them, and re-layouts  2.41 us (2%)
    ppermute x9, waiting for transfers between devices, swap(): return lax.ppermute(x, axis, [(i, i ^ k) for i in range(size)])  24.7 us
    another operation x4, other arithmetic, lower_inverse(): lax.linalg.triangular_solve(factor, eye, left_side=True, lower=True, tran...  16 us
    ppermute x9, starting transfers between devices, swap(): return lax.ppermute(x, axis, [(i, i ^ k) for i in range(size)])  15.2 us
    another operation x3, other arithmetic, block_cholesky(): l11 = lax.linalg.cholesky(a11, symmetrize_input=False)  12.4 us
    another operation x3, other arithmetic, block_cholesky(): lax.linalg.cholesky(a22 - jnp.dot(l21, l21.T, precision=precision), symme...  7.25 us
    all_to_all x1, starting transfers between devices, shards(): lax.all_to_all(copies, 'tile', 0, 0, tiled=False)  4.85 us
    dot_general x1, matrix products, shards(): jnp.einsum('vnc,mn->vmc', state_anom, space_t, precision=highest)  2.64 us
  transfers between devices with their start and end apart: 10, of which 10 were waited for; matrix products, arithmetic and copies ran while one was open for 33% of the time, Pallas kernels for 0%

profile of v9, /device:TPU:0, one launch (start us, length us, event | category | flops | bytes accessed | tf_op | source)
XLA Modules:
  0.0 98.4 jit_solution(9485443740408435395)
XLA Ops:
  0.0 0.9 reduce_sum.18
  0.9 0.7 broadcast_multiply_fusion.1
  1.6 1.0 subtract_multiply_fusion
  2.6 1.2 %fusion.25 = f32[200,200]{0,1:T(8,128)S(1)} fusion(f32[128,200]{0,1:T(8,128)S(1)} %get-tuple-element.32, f32[128,200]{0,1:T(8,128)} %param.7, f32[128]{0:T(128)S(1)} %get-tuple-element.27, f32[128]{0:T(128)S(1)} %get-tuple-element.35), kind=kOutput, calls=%fused_computation.38 | convolution fusion | flops 61491200 | bytes 365824 | tf_op jit(solution)/shard_map/dot_general | solution.py:91
  3.8 1.3 %broadcast_select_fusion = (f32[200,200]{0,1:T(8,128)S(1)}, f32[200,200]{0,1:T(8,128)S(1)}) fusion(f32[200,200]{0,1:T(8,128)S(1)} %fusion.25, pred[]{:T(512)S(6)} %eq.27, f32[128,200]{0,1:T(8,128)} %param.7, f32[128]{0:T(128)S(1)} %get-tuple-element.27, f32[128]{0:T(128)S(1)} %get-tuple-element.35), kind=kOutput, calls=%fused_computation.33 | convolution fusion | flops 61582400 | bytes 583425 | tf_op jit(solution)/shard_map/dot_general | solution.py:90
  5.7 1.1 %collective-permute-done = f32[200,200]{0,1:T(8,128)S(1)} collective-permute-done((f32[200,200]{0,1:T(8,128)S(1)}, f32[200,200]{0,1:T(8,128)S(1)}, u32[]{:S(2)}, u32[]{:S(2)}) %collective-permute-start) | collective-permute-done | bytes 160032 | tf_op jit(solution)/shard_map/ppermute | solution.py:53
  6.9 2.9 %collective-permute-start.1 = (f32[100,200]{0,1:T(8,128)S(1)}, f32[100,200]{0,1:T(8,128)S(1)}, u32[]{:S(2)}, u32[]{:S(2)}) collective-permute-start(f32[100,200]{0,1:T(8,128)S(1)} %slice_select_fusion.1), channel_id=1, source_target_pairs={{0,8},{8,0},{16,24},{24,16},{1,9},{9,1},{17,25},{25,17},{2,10},{10... | collective-permute-start | bytes 240008 | tf_op jit(solution)/shard_map/ppermute | solution.py:53
  9.8 3.2 %collective-permute-done.1 = f32[100,200]{0,1:T(8,128)S(1)} collective-permute-done((f32[100,200]{0,1:T(8,128)S(1)}, f32[100,200]{0,1:T(8,128)S(1)}, u32[]{:S(2)}, u32[]{:S(2)}) %collective-permute-start.1) | collective-permute-done | bytes 80032 | tf_op jit(solution)/shard_map/ppermute | solution.py:53
  13.1 1.8 %collective-permute-start.2 = (f32[100,200]{0,1:T(8,128)S(1)}, f32[100,200]{0,1:T(8,128)S(1)}, u32[]{:S(2)}, u32[]{:S(2)}) collective-permute-start(f32[100,200]{0,1:T(8,128)S(1)} %select_add_fusion.2), channel_id=1, source_target_pairs={{0,16},{8,24},{16,0},{24,8},{1,17},{9,25},{17,1},{25,9},{2,18},{10... | collective-permute-start | bytes 240008 | tf_op jit(solution)/shard_map/ppermute | solution.py:53
  14.9 2.9 %collective-permute-done.2 = f32[100,200]{0,1:T(8,128)S(1)} collective-permute-done((f32[100,200]{0,1:T(8,128)S(1)}, f32[100,200]{0,1:T(8,128)S(1)}, u32[]{:S(2)}, u32[]{:S(2)}) %collective-permute-start.2) | collective-permute-done | bytes 80032 | tf_op jit(solution)/shard_map/ppermute | solution.py:53
  17.9 1.9 %collective-permute-start.3 = (f32[100,200]{0,1:T(8,128)S(1)}, f32[100,200]{0,1:T(8,128)S(1)}, u32[]{:S(2)}, u32[]{:S(2)}) collective-permute-start(f32[100,200]{0,1:T(8,128)S(1)} %add.67), channel_id=1, source_target_pairs={{0,2},{1,3},{2,0},{3,1},{4,6},{5,7},{6,4},{7,5},{8,10},{9,11},{10,... | collective-permute-start | bytes 240008 | tf_op jit(solution)/shard_map/ppermute | solution.py:53
  19.7 2.8 %collective-permute-done.3 = f32[100,200]{0,1:T(8,128)S(1)} collective-permute-done((f32[100,200]{0,1:T(8,128)S(1)}, f32[100,200]{0,1:T(8,128)S(1)}, u32[]{:S(2)}, u32[]{:S(2)}) %collective-permute-start.3) | collective-permute-done | bytes 80032 | tf_op jit(solution)/shard_map/ppermute | solution.py:53
  22.6 3.4 %collective-permute-start.4 = (f32[100,200]{0,1:T(8,128)S(1)}, f32[100,200]{0,1:T(8,128)S(1)}, u32[]{:S(2)}, u32[]{:S(2)}) collective-permute-start(f32[100,200]{0,1:T(8,128)S(1)} %add.68), channel_id=1, source_target_pairs={{0,4},{1,5},{2,6},{3,7},{4,0},{5,1},{6,2},{7,3},{8,12},{9,13},{10,... | collective-permute-start | bytes 240008 | tf_op jit(solution)/shard_map/ppermute | solution.py:53
  26.0 3.7 %collective-permute-done.4 = f32[100,200]{0,1:T(8,128)S(1)} collective-permute-done((f32[100,200]{0,1:T(8,128)S(1)}, f32[100,200]{0,1:T(8,128)S(1)}, u32[]{:S(2)}, u32[]{:S(2)}) %collective-permute-start.4) | collective-permute-done | bytes 80032 | tf_op jit(solution)/shard_map/ppermute | solution.py:53
  29.7 1.3 %broadcast_in_dim.7 = f32[8,128,401]{1,2,0:T(8,128)} broadcast(f32[128,401]{0,1:T(8,128)S(1)} %pad_maximum_fusion), dimensions={1,2} | broadcast | bytes 1847808 | tf_op jit(solution)/shard_map/broadcast_in_dim | solution.py:104
  31.0 4.9 %all-to-all-start = ((f32[8,128,401]{1,2,0:T(8,128)}), f32[8,128,401]{1,2,0:T(8,128)S(1)}, u32[]{:S(2)}, u32[]{:S(2)}) async-start(f32[8,128,401]{1,2,0:T(8,128)} %broadcast_in_dim.7), calls=%async_computation | async-start | bytes 3342336 | tf_op jit(solution)/shard_map/all_to_all | solution.py:105
  35.9 1.5 %collective-permute-start.5 = (f32[100,200]{0,1:T(8,128)S(1)}, f32[100,200]{0,1:T(8,128)S(1)}, u32[]{:S(2)}, u32[]{:S(2)}) collective-permute-start(f32[100,200]{0,1:T(8,128)S(1)} %add.69), channel_id=1, source_target_pairs={{0,8},{8,0},{16,24},{24,16},{1,9},{9,1},{17,25},{25,17},{2,10},{10... | collective-permute-start | bytes 240008 | tf_op jit(solution)/shard_map/ppermute | solution.py:53
  37.4 3.8 %collective-permute-done.5 = f32[100,200]{0,1:T(8,128)S(1)} collective-permute-done((f32[100,200]{0,1:T(8,128)S(1)}, f32[100,200]{0,1:T(8,128)S(1)}, u32[]{:S(2)}, u32[]{:S(2)}) %collective-permute-start.5) | collective-permute-done | bytes 80032 | tf_op jit(solution)/shard_map/ppermute | solution.py:53
  41.5 1.4 %collective-permute-done.6 = f32[200,200]{0,1:T(8,128)S(1)} collective-permute-done((f32[200,200]{0,1:T(8,128)S(1)}, f32[200,200]{0,1:T(8,128)S(1)}, u32[]{:S(2)}, u32[]{:S(2)}) %collective-permute-start.6) | collective-permute-done | bytes 160032 | tf_op jit(solution)/shard_map/ppermute | solution.py:53
  43.3 11.7 %cholesky.37 = f32[128,128]{1,0:T(8,128)S(1)} custom-call(f32[128,128]{1,0:T(8,128)S(1)} %cholesky.82), custom_call_target="Cholesky" | custom-call | tf_op jit(solution)/shard_map/cholesky | solution.py:17
  55.7 0.7 fusion.29
  56.4 9.8 %custom-call.10 = f32[1,128,128]{1,2,0:T(8,128)S(1)} custom-call(f32[1,128,128]{2,1,0:T(8,128)S(1)} %fusion.29), custom_call_target="InvertDiagBlocksLowerTriangular" | custom-call | tf_op jit(solution)/shard_map/triangular_solve | solution.py:11
  66.9 6.6 %cholesky.73 = f32[72,72]{1,0:T(8,128)S(1)} custom-call(f32[72,72]{1,0:T(8,128)S(1)} %convolution_subtract_fusion.2), custom_call_target="Cholesky" | custom-call | tf_op jit(solution)/shard_map/cholesky | solution.py:20
  74.2 0.7 select_select_fusion.1
  74.9 1.0 all-to-all-done
  76.7 1.5 %fusion.3 = f32[400,200]{1,0:T(8,128)S(1)} fusion(f32[1024,401]{0,1:T(8,128)S(1)} %bitcast.49, f32[1024]{0:T(1024)S(1)} %bitcast.52), kind=kOutput, calls=%fused_computation.4 | convolution fusion | flops 983244800 | bytes 2781696 | tf_op jit(solution)/shard_map/dot_general | solution.py:115
  78.6 5.5 %custom-call.11 = f32[1,72,72]{1,2,0:T(8,128)S(1)} custom-call(f32[1,72,72]{2,1,0:T(8,128)S(1)} %select_bitcast_fusion), custom_call_target="InvertDiagBlocksLowerTriangular" | custom-call | tf_op jit(solution)/shard_map/triangular_solve | solution.py:11
  86.7 1.6 %collective-permute-start.7 = (f32[100,200]{1,0:T(8,128)S(1)}, f32[100,200]{1,0:T(8,128)S(1)}, u32[]{:S(2)}, u32[]{:S(2)}) collective-permute-start(f32[100,200]{1,0:T(8,128)S(1)} %slice_select_fusion), channel_id=1, source_target_pairs={{0,16},{8,24},{16,0},{24,8},{1,17},{9,25},{17,1},{25,9},{2,18},{10... | collective-permute-start | bytes 240008 | tf_op jit(solution)/shard_map/ppermute | solution.py:53
  88.4 3.0 %collective-permute-done.7 = f32[100,200]{1,0:T(8,128)S(1)} collective-permute-done((f32[100,200]{1,0:T(8,128)S(1)}, f32[100,200]{1,0:T(8,128)S(1)}, u32[]{:S(2)}, u32[]{:S(2)}) %collective-permute-start.7) | collective-permute-done | bytes 80032 | tf_op jit(solution)/shard_map/ppermute | solution.py:53
  91.5 1.5 %collective-permute-start.8 = (f32[50,200]{1,0:T(8,128)S(1)}, f32[50,200]{1,0:T(8,128)S(1)}, u32[]{:S(2)}, u32[]{:S(2)}) collective-permute-start(f32[50,200]{1,0:T(8,128)S(1)} %slice_select_fusion.2), channel_id=1, source_target_pairs={{0,8},{8,0},{16,24},{24,16},{1,9},{9,1},{17,25},{25,17},{2,10},{10... | collective-permute-start | bytes 120008 | tf_op jit(solution)/shard_map/ppermute | solution.py:53
  93.0 2.7 %collective-permute-done.8 = f32[50,200]{1,0:T(8,128)S(1)} collective-permute-done((f32[50,200]{1,0:T(8,128)S(1)}, f32[50,200]{1,0:T(8,128)S(1)}, u32[]{:S(2)}, u32[]{:S(2)}) %collective-permute-start.8) | collective-permute-done | bytes 40032 | tf_op jit(solution)/shard_map/ppermute | solution.py:53
  95.7 2.6 %fusion.8 = f32[3,50,1024]{2,1,0:T(8,128)} fusion(f32[3,200,1024]{2,1,0:T(8,128)S(1)} %copy-done, f32[3,1024]{1,0:T(4,128)S(1)} %broadcast_multiply_fusion, s32[]{:T(128)S(6)} %select_n.99, f32[50,200]{1,0:T(8,128)S(1)} %collective-permute-done.8, f32[100,200]{1,0:T(8,128)S(1)} %select_add_fusion.1, pred[]{:T(512)S(6)} %eq.24), kind=kOutput, calls=%fused_computation.7 | convolution fusion | flops 370042400 | bytes 3948549 | tf_op jit(solution)/shard_map/vnc,mn->vmc/dot_general | solution.py:137
  (50 shorter events, 7.5 us)
Async XLA Ops:
  5.2 1.6 %collective-permute-start = (f32[200,200]{0,1:T(8,128)S(1)}, f32[200,200]{0,1:T(8,128)S(1)}, u32[]{:S(2)}, u32[]{:S(2)}) collective-permute-start(f32[200,200]{0,1:T(8,128)S(1)} %get-tuple-element.33), channel_id=1, source_target_pairs={{0,1},{1,0},{2,3},{3,2},{4,5},{5,4},{6,7},{7,6},{8,9},{9,8},{10,11... | collective-permute-start | bytes 480008 | tf_op jit(solution)/shard_map/ppermute | solution.py:53
  6.9 6.1 %collective-permute-start.1 = (f32[100,200]{0,1:T(8,128)S(1)}, f32[100,200]{0,1:T(8,128)S(1)}, u32[]{:S(2)}, u32[]{:S(2)}) collective-permute-start(f32[100,200]{0,1:T(8,128)S(1)} %slice_select_fusion.1), channel_id=1, source_target_pairs={{0,8},{8,0},{16,24},{24,16},{1,9},{9,1},{17,25},{25,17},{2,10},{10... | collective-permute-start | bytes 240008 | tf_op jit(solution)/shard_map/ppermute | solution.py:53
  13.1 4.7 %collective-permute-start.2 = (f32[100,200]{0,1:T(8,128)S(1)}, f32[100,200]{0,1:T(8,128)S(1)}, u32[]{:S(2)}, u32[]{:S(2)}) collective-permute-start(f32[100,200]{0,1:T(8,128)S(1)} %select_add_fusion.2), channel_id=1, source_target_pairs={{0,16},{8,24},{16,0},{24,8},{1,17},{9,25},{17,1},{25,9},{2,18},{10... | collective-permute-start | bytes 240008 | tf_op jit(solution)/shard_map/ppermute | solution.py:53
  17.9 4.7 %collective-permute-start.3 = (f32[100,200]{0,1:T(8,128)S(1)}, f32[100,200]{0,1:T(8,128)S(1)}, u32[]{:S(2)}, u32[]{:S(2)}) collective-permute-start(f32[100,200]{0,1:T(8,128)S(1)} %add.67), channel_id=1, source_target_pairs={{0,2},{1,3},{2,0},{3,1},{4,6},{5,7},{6,4},{7,5},{8,10},{9,11},{10,... | collective-permute-start | bytes 240008 | tf_op jit(solution)/shard_map/ppermute | solution.py:53
  22.6 7.1 %collective-permute-start.4 = (f32[100,200]{0,1:T(8,128)S(1)}, f32[100,200]{0,1:T(8,128)S(1)}, u32[]{:S(2)}, u32[]{:S(2)}) collective-permute-start(f32[100,200]{0,1:T(8,128)S(1)} %add.68), channel_id=1, source_target_pairs={{0,4},{1,5},{2,6},{3,7},{4,0},{5,1},{6,2},{7,3},{8,12},{9,13},{10,... | collective-permute-start | bytes 240008 | tf_op jit(solution)/shard_map/ppermute | solution.py:53
  31.0 10.4 %copy-start.1 = (s32[1,8]{1,0:T(1,128)S(1)}, s32[1,8]{1,0:T(1,128)}, u32[]{:S(2)}) copy-start(s32[1,8]{1,0:T(1,128)} %param.11) | copy-start | bytes 100
  31.0 10.4 %copy-start.2 = (s32[1,8]{1,0:T(1,128)S(1)}, s32[1,8]{1,0:T(1,128)}, u32[]{:S(2)}) copy-start(s32[1,8]{1,0:T(1,128)} %param.10) | copy-start | bytes 100
  31.0 44.8 %all-to-all-start = ((f32[8,128,401]{1,2,0:T(8,128)}), f32[8,128,401]{1,2,0:T(8,128)S(1)}, u32[]{:S(2)}, u32[]{:S(2)}) async-start(f32[8,128,401]{1,2,0:T(8,128)} %broadcast_in_dim.7), calls=%async_computation | async-start | bytes 3342336 | tf_op jit(solution)/shard_map/all_to_all | solution.py:105
  35.9 5.3 %collective-permute-start.5 = (f32[100,200]{0,1:T(8,128)S(1)}, f32[100,200]{0,1:T(8,128)S(1)}, u32[]{:S(2)}, u32[]{:S(2)}) collective-permute-start(f32[100,200]{0,1:T(8,128)S(1)} %add.69), channel_id=1, source_target_pairs={{0,8},{8,0},{16,24},{24,16},{1,9},{9,1},{17,25},{25,17},{2,10},{10... | collective-permute-start | bytes 240008 | tf_op jit(solution)/shard_map/ppermute | solution.py:53
  41.4 1.5 %collective-permute-start.6 = (f32[200,200]{0,1:T(8,128)S(1)}, f32[200,200]{0,1:T(8,128)S(1)}, u32[]{:S(2)}, u32[]{:S(2)}) collective-permute-start(f32[200,200]{0,1:T(8,128)S(1)} %maximum_select_fusion.1), channel_id=1, source_target_pairs={{0,1},{1,0},{2,3},{3,2},{4,5},{5,4},{6,7},{7,6},{8,9},{9,8},{10,11... | collective-permute-start | bytes 480008 | tf_op jit(solution)/shard_map/ppermute | solution.py:53
  78.2 10.0 %copy-start = (f32[3,200,1024]{2,1,0:T(8,128)S(1)}, f32[3,200,1024]{2,1,0:T(8,128)}, u32[]{:S(2)}) copy-start(f32[3,200,1024]{2,1,0:T(8,128)} %param.6) | copy-start | bytes 7372804
  86.7 4.8 %collective-permute-start.7 = (f32[100,200]{1,0:T(8,128)S(1)}, f32[100,200]{1,0:T(8,128)S(1)}, u32[]{:S(2)}, u32[]{:S(2)}) collective-permute-start(f32[100,200]{1,0:T(8,128)S(1)} %slice_select_fusion), channel_id=1, source_target_pairs={{0,16},{8,24},{16,0},{24,8},{1,17},{9,25},{17,1},{25,9},{2,18},{10... | collective-permute-start | bytes 240008 | tf_op jit(solution)/shard_map/ppermute | solution.py:53
  91.5 4.2 %collective-permute-start.8 = (f32[50,200]{1,0:T(8,128)S(1)}, f32[50,200]{1,0:T(8,128)S(1)}, u32[]{:S(2)}, u32[]{:S(2)}) collective-permute-start(f32[50,200]{1,0:T(8,128)S(1)} %slice_select_fusion.2), channel_id=1, source_target_pairs={{0,8},{8,0},{16,24},{24,16},{1,9},{9,1},{17,25},{25,17},{2,10},{10... | collective-permute-start | bytes 120008 | tf_op jit(solution)/shard_map/ppermute | solution.py:53

commit v10 on v9

--- a/solution.py
+++ b/solution.py
@@ -127,12 +127,9 @@
     space_t = taper_cross_t - lax.dot_general(
         solved, taper_gram, (((0,), (1,)), ((), ())), precision=highest
     )
-    for axis, k in reversed(axis_bits("well")):
-        half = space_t.shape[0] // 2
-        hi = bit_of(axis, k) == 1
-        keep = jnp.where(hi, space_t[half:], space_t[:half])
-        send = jnp.where(hi, space_t[:half], space_t[half:])
-        space_t = keep + swap(send, axis, k)
+    wells = lax.axis_size("well")
+    blocks = space_t.reshape((wells, space_t.shape[0] // wells, space_t.shape[1]))
+    space_t = jnp.sum(lax.all_to_all(blocks, "well", 0, 0, tiled=False), axis=0)
     state_anom = (prior_state - jnp.mean(prior_state, axis=1, keepdims=True)) * norm_factor
     increment = jnp.einsum("vnc,mn->vmc", state_anom, space_t, precision=highest)
     prior_mine = lax.dynamic_slice_in_dim(prior_state, own_start, own_count, 1)

time: 98.7 us -> 104 us (1.054)
  local copies, waits for them, and re-layouts: 2.41 us -> 4.56 us
  other arithmetic: 39.8 us -> 41.9 us
    ppermute x9 -> x7, waiting for transfers between devices: 24.7 us -> 18.7 us  [swap(): return lax.ppermute(x, axis, [(i, i ^ k) for i in range(size)])]
    all_to_all x0 -> x1, waiting for transfers between devices: none -> 5.28 us  [shards(): space_t = jnp.sum(lax.all_to_all(blocks, 'well', 0, 0, tiled=False), axis=0)]
    all_to_all x0 -> x1, starting transfers between devices: none -> 3.71 us  [shards(): space_t = jnp.sum(lax.all_to_all(blocks, 'well', 0, 0, tiled=False), axis=0)]
    ppermute x9 -> x7, starting transfers between devices: 15.2 us -> 12.2 us  [swap(): return lax.ppermute(x, axis, [(i, i ^ k) for i in range(size)])]
    another operation x4, other arithmetic: 16 us -> 18.1 us  [lower_inverse(): lax.linalg.triangular_solve(factor, eye, left_side=True, lower=True, tran...]
    all_to_all x1, local copies, waits for them, and re-layouts: 0.32 us -> 1.76 us  [shards(): lax.all_to_all(copies, 'tile', 0, 0, tiled=False)]
  transfers between devices with their start and end apart: 10 -> 9, of which waited for: 10 -> 9; matrix products, arithmetic and copies ran while one was open for 33% -> 31% of each run, Pallas kernels for 0% -> 0%
where the time goes in v10:
time: 104 us; the launch traced here: 103 us
  other arithmetic  41.9 us (40%)
  waiting for transfers between devices  25 us (24%)
  starting transfers between devices  20.8 us (20%)
  matrix products  10.8 us (10%)
  local copies, waits for them, and re-layouts  4.56 us (4%)
    ppermute x7, waiting for transfers between devices, swap(): return lax.ppermute(x, axis, [(i, i ^ k) for i in range(size)])  18.7 us
    another operation x4, other arithmetic, lower_inverse(): lax.linalg.triangular_solve(factor, eye, left_side=True, lower=True, tran...  18.1 us
    another operation x3, other arithmetic, block_cholesky(): l11 = lax.linalg.cholesky(a11, symmetrize_input=False)  12.4 us
    ppermute x7, starting transfers between devices, swap(): return lax.ppermute(x, axis, [(i, i ^ k) for i in range(size)])  12.2 us
    another operation x3, other arithmetic, block_cholesky(): lax.linalg.cholesky(a22 - jnp.dot(l21, l21.T, precision=precision), symme...  7.25 us
    all_to_all x1, waiting for transfers between devices, shards(): space_t = jnp.sum(lax.all_to_all(blocks, 'well', 0, 0, tiled=False), axis=0)  5.28 us
    all_to_all x1, starting transfers between devices, shards(): lax.all_to_all(copies, 'tile', 0, 0, tiled=False)  4.87 us
    all_to_all x1, starting transfers between devices, shards(): space_t = jnp.sum(lax.all_to_all(blocks, 'well', 0, 0, tiled=False), axis=0)  3.71 us
  transfers between devices with their start and end apart: 9, of which 9 were waited for; matrix products, arithmetic and copies ran while one was open for 31% of the time, Pallas kernels for 0%

profile of v10, /device:TPU:0, one launch (start us, length us, event | category | flops | bytes accessed | tf_op | source)
XLA Modules:
  0.0 103.3 jit_solution(8035920621314899681)
XLA Ops:
  0.0 0.9 reduce_sum.27
  0.9 0.7 broadcast_multiply_fusion.1
  1.6 1.0 subtract_multiply_fusion
  2.6 1.2 %fusion.25 = f32[200,200]{0,1:T(8,128)S(1)} fusion(f32[128,200]{0,1:T(8,128)S(1)} %get-tuple-element.32, f32[128,200]{0,1:T(8,128)} %param.7, f32[128]{0:T(128)S(1)} %get-tuple-element.27, f32[128]{0:T(128)S(1)} %get-tuple-element.35), kind=kOutput, calls=%fused_computation.36 | convolution fusion | flops 61491200 | bytes 365824 | tf_op jit(solution)/shard_map/dot_general | solution.py:91
  3.8 1.3 %broadcast_select_fusion = (f32[200,200]{0,1:T(8,128)S(1)}, f32[200,200]{0,1:T(8,128)S(1)}) fusion(f32[200,200]{0,1:T(8,128)S(1)} %fusion.25, pred[]{:T(512)S(6)} %eq.19, f32[128,200]{0,1:T(8,128)} %param.7, f32[128]{0:T(128)S(1)} %get-tuple-element.27, f32[128]{0:T(128)S(1)} %get-tuple-element.35), kind=kOutput, calls=%fused_computation.32 | convolution fusion | flops 61582400 | bytes 583425 | tf_op jit(solution)/shard_map/dot_general | solution.py:90
  5.7 1.1 %collective-permute-done = f32[200,200]{0,1:T(8,128)S(1)} collective-permute-done((f32[200,200]{0,1:T(8,128)S(1)}, f32[200,200]{0,1:T(8,128)S(1)}, u32[]{:S(2)}, u32[]{:S(2)}) %collective-permute-start) | collective-permute-done | bytes 160032 | tf_op jit(solution)/shard_map/ppermute | solution.py:53
  6.9 2.9 %collective-permute-start.1 = (f32[100,200]{0,1:T(8,128)S(1)}, f32[100,200]{0,1:T(8,128)S(1)}, u32[]{:S(2)}, u32[]{:S(2)}) collective-permute-start(f32[100,200]{0,1:T(8,128)S(1)} %slice_select_fusion), channel_id=1, source_target_pairs={{0,8},{8,0},{16,24},{24,16},{1,9},{9,1},{17,25},{25,17},{2,10},{10... | collective-permute-start | bytes 240008 | tf_op jit(solution)/shard_map/ppermute | solution.py:53
  9.8 3.2 %collective-permute-done.1 = f32[100,200]{0,1:T(8,128)S(1)} collective-permute-done((f32[100,200]{0,1:T(8,128)S(1)}, f32[100,200]{0,1:T(8,128)S(1)}, u32[]{:S(2)}, u32[]{:S(2)}) %collective-permute-start.1) | collective-permute-done | bytes 80032 | tf_op jit(solution)/shard_map/ppermute | solution.py:53
  13.1 1.8 %collective-permute-start.2 = (f32[100,200]{0,1:T(8,128)S(1)}, f32[100,200]{0,1:T(8,128)S(1)}, u32[]{:S(2)}, u32[]{:S(2)}) collective-permute-start(f32[100,200]{0,1:T(8,128)S(1)} %select_add_fusion.1), channel_id=1, source_target_pairs={{0,16},{8,24},{16,0},{24,8},{1,17},{9,25},{17,1},{25,9},{2,18},{10... | collective-permute-start | bytes 240008 | tf_op jit(solution)/shard_map/ppermute | solution.py:53
  14.9 2.9 %collective-permute-done.2 = f32[100,200]{0,1:T(8,128)S(1)} collective-permute-done((f32[100,200]{0,1:T(8,128)S(1)}, f32[100,200]{0,1:T(8,128)S(1)}, u32[]{:S(2)}, u32[]{:S(2)}) %collective-permute-start.2) | collective-permute-done | bytes 80032 | tf_op jit(solution)/shard_map/ppermute | solution.py:53
  17.8 1.9 %collective-permute-start.3 = (f32[100,200]{0,1:T(8,128)S(1)}, f32[100,200]{0,1:T(8,128)S(1)}, u32[]{:S(2)}, u32[]{:S(2)}) collective-permute-start(f32[100,200]{0,1:T(8,128)S(1)} %add.55), channel_id=1, source_target_pairs={{0,2},{1,3},{2,0},{3,1},{4,6},{5,7},{6,4},{7,5},{8,10},{9,11},{10,... | collective-permute-start | bytes 240008 | tf_op jit(solution)/shard_map/ppermute | solution.py:53
  19.7 2.8 %collective-permute-done.3 = f32[100,200]{0,1:T(8,128)S(1)} collective-permute-done((f32[100,200]{0,1:T(8,128)S(1)}, f32[100,200]{0,1:T(8,128)S(1)}, u32[]{:S(2)}, u32[]{:S(2)}) %collective-permute-start.3) | collective-permute-done | bytes 80032 | tf_op jit(solution)/shard_map/ppermute | solution.py:53
  22.6 3.4 %collective-permute-start.4 = (f32[100,200]{0,1:T(8,128)S(1)}, f32[100,200]{0,1:T(8,128)S(1)}, u32[]{:S(2)}, u32[]{:S(2)}) collective-permute-start(f32[100,200]{0,1:T(8,128)S(1)} %add.56), channel_id=1, source_target_pairs={{0,4},{1,5},{2,6},{3,7},{4,0},{5,1},{6,2},{7,3},{8,12},{9,13},{10,... | collective-permute-start | bytes 240008 | tf_op jit(solution)/shard_map/ppermute | solution.py:53
  26.0 3.7 %collective-permute-done.4 = f32[100,200]{0,1:T(8,128)S(1)} collective-permute-done((f32[100,200]{0,1:T(8,128)S(1)}, f32[100,200]{0,1:T(8,128)S(1)}, u32[]{:S(2)}, u32[]{:S(2)}) %collective-permute-start.4) | collective-permute-done | bytes 80032 | tf_op jit(solution)/shard_map/ppermute | solution.py:53
  29.7 1.3 %broadcast_in_dim.7 = f32[8,128,401]{1,2,0:T(8,128)} broadcast(f32[128,401]{0,1:T(8,128)S(1)} %pad_maximum_fusion), dimensions={1,2} | broadcast | bytes 1847808 | tf_op jit(solution)/shard_map/broadcast_in_dim | solution.py:104
  31.0 4.9 %all-to-all-start = ((f32[8,128,401]{1,2,0:T(8,128)}), f32[8,128,401]{1,2,0:T(8,128)}, u32[]{:S(2)}, u32[]{:S(2)}) async-start(f32[8,128,401]{1,2,0:T(8,128)} %broadcast_in_dim.7), calls=%async_computation | async-start | bytes 3342336 | tf_op jit(solution)/shard_map/all_to_all | solution.py:105
  35.9 1.6 %collective-permute-start.5 = (f32[100,200]{0,1:T(8,128)S(1)}, f32[100,200]{0,1:T(8,128)S(1)}, u32[]{:S(2)}, u32[]{:S(2)}) collective-permute-start(f32[100,200]{0,1:T(8,128)S(1)} %add.57), channel_id=1, source_target_pairs={{0,8},{8,0},{16,24},{24,16},{1,9},{9,1},{17,25},{25,17},{2,10},{10... | collective-permute-start | bytes 240008 | tf_op jit(solution)/shard_map/ppermute | solution.py:53
  37.6 3.6 %collective-permute-done.5 = f32[100,200]{0,1:T(8,128)S(1)} collective-permute-done((f32[100,200]{0,1:T(8,128)S(1)}, f32[100,200]{0,1:T(8,128)S(1)}, u32[]{:S(2)}, u32[]{:S(2)}) %collective-permute-start.5) | collective-permute-done | bytes 80032 | tf_op jit(solution)/shard_map/ppermute | solution.py:53
  41.5 1.4 %collective-permute-done.6 = f32[200,200]{0,1:T(8,128)S(1)} collective-permute-done((f32[200,200]{0,1:T(8,128)S(1)}, f32[200,200]{0,1:T(8,128)S(1)}, u32[]{:S(2)}, u32[]{:S(2)}) %collective-permute-start.6) | collective-permute-done | bytes 160032 | tf_op jit(solution)/shard_map/ppermute | solution.py:53
  43.3 11.7 %cholesky.37 = f32[128,128]{1,0:T(8,128)S(1)} custom-call(f32[128,128]{1,0:T(8,128)S(1)} %cholesky.82), custom_call_target="Cholesky" | custom-call | tf_op jit(solution)/shard_map/cholesky | solution.py:17
  55.7 0.7 fusion.29
  56.4 9.8 %custom-call.10 = f32[1,128,128]{1,2,0:T(8,128)S(1)} custom-call(f32[1,128,128]{2,1,0:T(8,128)S(1)} %fusion.29), custom_call_target="InvertDiagBlocksLowerTriangular" | custom-call | tf_op jit(solution)/shard_map/triangular_solve | solution.py:11
  66.9 6.6 %cholesky.73 = f32[72,72]{1,0:T(8,128)S(1)} custom-call(f32[72,72]{1,0:T(8,128)S(1)} %convolution_subtract_fusion.2), custom_call_target="Cholesky" | custom-call | tf_op jit(solution)/shard_map/cholesky | solution.py:20
  74.9 1.1 %all-to-all-done = f32[8,128,401]{1,2,0:T(8,128)} async-done(((f32[8,128,401]{1,2,0:T(8,128)}), f32[8,128,401]{1,2,0:T(8,128)}, u32[]{:S(2)}, u32[]{:S(2)}) %all-to-all-start) | async-done | bytes 1642528 | tf_op jit(solution)/shard_map/all_to_all | solution.py:105
  75.9 1.8 %copy.17 = f32[8,128,401]{1,0,2:T(8,128)S(1)} copy(f32[8,128,401]{1,2,0:T(8,128)} %all-to-all-done) | data formatting | bytes 3284992 | tf_op jit(solution)/shard_map/all_to_all | solution.py:105
  78.3 1.5 %fusion.3 = f32[400,200]{1,0:T(8,128)S(1)} fusion(f32[1024,401]{0,1:T(8,128)S(1)} %bitcast.49, f32[1024]{0:T(1024)S(1)} %bitcast.52), kind=kOutput, calls=%fused_computation.4 | convolution fusion | flops 983244800 | bytes 2781696 | tf_op jit(solution)/shard_map/dot_general | solution.py:115
  80.8 7.0 %custom-call.11 = f32[1,72,72]{1,2,0:T(8,128)} custom-call(f32[1,72,72]{2,1,0:T(8,128)} %select_bitcast_fusion), custom_call_target="InvertDiagBlocksLowerTriangular" | custom-call | tf_op jit(solution)/shard_map/triangular_solve | solution.py:11
  87.8 1.0 fusion.39
  91.0 0.7 reshape.42
  91.7 3.7 %all-to-all-start.1 = ((f32[4,50,200]{2,1,0:T(8,128)}), f32[4,50,200]{2,1,0:T(8,128)S(1)}, u32[]{:S(2)}, u32[]{:S(2)}) async-start(f32[4,50,200]{2,1,0:T(8,128)} %reshape.42), calls=%async_computation.1 | async-start | bytes 458752 | tf_op jit(solution)/shard_map/all_to_all | solution.py:132
  95.4 5.3 %all-to-all-done.1 = f32[4,50,200]{2,1,0:T(8,128)S(1)} async-done(((f32[4,50,200]{2,1,0:T(8,128)}), f32[4,50,200]{2,1,0:T(8,128)S(1)}, u32[]{:S(2)}, u32[]{:S(2)}) %all-to-all-start.1) | async-done | bytes 160032 | tf_op jit(solution)/shard_map/all_to_all | solution.py:132
  100.7 2.6 %fusion.8 = f32[3,50,1024]{2,1,0:T(8,128)} fusion(f32[3,200,1024]{2,1,0:T(8,128)S(1)} %copy-done, f32[3,1024]{1,0:T(4,128)S(1)} %broadcast_multiply_fusion, s32[]{:T(128)S(6)} %select_n.67, f32[50,200]{1,0:T(8,128)S(1)} %reduce_sum.28), kind=kOutput, calls=%fused_computation.7 | convolution fusion | flops 370022400 | bytes 3833860 | tf_op jit(solution)/shard_map/vnc,mn->vmc/dot_general | solution.py:134
  (47 shorter events, 8.1 us)
Async XLA Ops:
  5.2 1.6 %collective-permute-start = (f32[200,200]{0,1:T(8,128)S(1)}, f32[200,200]{0,1:T(8,128)S(1)}, u32[]{:S(2)}, u32[]{:S(2)}) collective-permute-start(f32[200,200]{0,1:T(8,128)S(1)} %get-tuple-element.33), channel_id=1, source_target_pairs={{0,1},{1,0},{2,3},{3,2},{4,5},{5,4},{6,7},{7,6},{8,9},{9,8},{10,11... | collective-permute-start | bytes 480008 | tf_op jit(solution)/shard_map/ppermute | solution.py:53
  6.9 6.1 %collective-permute-start.1 = (f32[100,200]{0,1:T(8,128)S(1)}, f32[100,200]{0,1:T(8,128)S(1)}, u32[]{:S(2)}, u32[]{:S(2)}) collective-permute-start(f32[100,200]{0,1:T(8,128)S(1)} %slice_select_fusion), channel_id=1, source_target_pairs={{0,8},{8,0},{16,24},{24,16},{1,9},{9,1},{17,25},{25,17},{2,10},{10... | collective-permute-start | bytes 240008 | tf_op jit(solution)/shard_map/ppermute | solution.py:53
  13.1 4.7 %collective-permute-start.2 = (f32[100,200]{0,1:T(8,128)S(1)}, f32[100,200]{0,1:T(8,128)S(1)}, u32[]{:S(2)}, u32[]{:S(2)}) collective-permute-start(f32[100,200]{0,1:T(8,128)S(1)} %select_add_fusion.1), channel_id=1, source_target_pairs={{0,16},{8,24},{16,0},{24,8},{1,17},{9,25},{17,1},{25,9},{2,18},{10... | collective-permute-start | bytes 240008 | tf_op jit(solution)/shard_map/ppermute | solution.py:53
  17.8 4.7 %collective-permute-start.3 = (f32[100,200]{0,1:T(8,128)S(1)}, f32[100,200]{0,1:T(8,128)S(1)}, u32[]{:S(2)}, u32[]{:S(2)}) collective-permute-start(f32[100,200]{0,1:T(8,128)S(1)} %add.55), channel_id=1, source_target_pairs={{0,2},{1,3},{2,0},{3,1},{4,6},{5,7},{6,4},{7,5},{8,10},{9,11},{10,... | collective-permute-start | bytes 240008 | tf_op jit(solution)/shard_map/ppermute | solution.py:53
  22.6 7.1 %collective-permute-start.4 = (f32[100,200]{0,1:T(8,128)S(1)}, f32[100,200]{0,1:T(8,128)S(1)}, u32[]{:S(2)}, u32[]{:S(2)}) collective-permute-start(f32[100,200]{0,1:T(8,128)S(1)} %add.56), channel_id=1, source_target_pairs={{0,4},{1,5},{2,6},{3,7},{4,0},{5,1},{6,2},{7,3},{8,12},{9,13},{10,... | collective-permute-start | bytes 240008 | tf_op jit(solution)/shard_map/ppermute | solution.py:53
  31.0 6.4 %copy-start = (f32[3,200,1024]{2,1,0:T(8,128)S(1)}, f32[3,200,1024]{2,1,0:T(8,128)}, u32[]{:S(2)}) copy-start(f32[3,200,1024]{2,1,0:T(8,128)} %param.6) | copy-start | bytes 7372804
  31.0 44.9 %all-to-all-start = ((f32[8,128,401]{1,2,0:T(8,128)}), f32[8,128,401]{1,2,0:T(8,128)}, u32[]{:S(2)}, u32[]{:S(2)}) async-start(f32[8,128,401]{1,2,0:T(8,128)} %broadcast_in_dim.7), calls=%async_computation | async-start | bytes 3342336 | tf_op jit(solution)/shard_map/all_to_all | solution.py:105
  35.9 5.6 %copy-start.1 = (s32[1,8]{1,0:T(1,128)S(1)}, s32[1,8]{1,0:T(1,128)}, u32[]{:S(2)}) copy-start(s32[1,8]{1,0:T(1,128)} %param.11) | copy-start | bytes 100
  35.9 5.6 %copy-start.2 = (s32[1,8]{1,0:T(1,128)S(1)}, s32[1,8]{1,0:T(1,128)}, u32[]{:S(2)}) copy-start(s32[1,8]{1,0:T(1,128)} %param.10) | copy-start | bytes 100
  35.9 5.3 %collective-permute-start.5 = (f32[100,200]{0,1:T(8,128)S(1)}, f32[100,200]{0,1:T(8,128)S(1)}, u32[]{:S(2)}, u32[]{:S(2)}) collective-permute-start(f32[100,200]{0,1:T(8,128)S(1)} %add.57), channel_id=1, source_target_pairs={{0,8},{8,0},{16,24},{24,16},{1,9},{9,1},{17,25},{25,17},{2,10},{10... | collective-permute-start | bytes 240008 | tf_op jit(solution)/shard_map/ppermute | solution.py:53
  41.4 1.5 %collective-permute-start.6 = (f32[200,200]{0,1:T(8,128)S(1)}, f32[200,200]{0,1:T(8,128)S(1)}, u32[]{:S(2)}, u32[]{:S(2)}) collective-permute-start(f32[200,200]{0,1:T(8,128)S(1)} %maximum_select_fusion.1), channel_id=1, source_target_pairs={{0,1},{1,0},{2,3},{3,2},{4,5},{5,4},{6,7},{7,6},{8,9},{9,8},{10,11... | collective-permute-start | bytes 480008 | tf_op jit(solution)/shard_map/ppermute | solution.py:53
  91.7 9.0 %all-to-all-start.1 = ((f32[4,50,200]{2,1,0:T(8,128)}), f32[4,50,200]{2,1,0:T(8,128)S(1)}, u32[]{:S(2)}, u32[]{:S(2)}) async-start(f32[4,50,200]{2,1,0:T(8,128)} %reshape.42), calls=%async_computation.1 | async-start | bytes 458752 | tf_op jit(solution)/shard_map/all_to_all | solution.py:132

commit v11 on v9

--- a/solution.py
+++ b/solution.py
@@ -19,14 +19,6 @@
     l21 = jnp.dot(a21, inv11.T, precision=precision)
     l22 = lax.linalg.cholesky(a22 - jnp.dot(l21, l21.T, precision=precision), symmetrize_input=False)
     return inv11, l21, l22
-
-
-def forward(parts, right, precision):
-    inv11, l21, inv22 = parts
-    split = inv11.shape[0]
-    y1 = jnp.dot(inv11, right[:split], precision=precision)
-    y2 = jnp.dot(inv22, right[split:] - jnp.dot(l21, y1, precision=precision), precision=precision)
-    return y1, y2
 
 
 def backward(parts, y1, y2, precision):
@@ -93,16 +85,16 @@
         0,
     )
     packed = jnp.concatenate([data_anom, innov, row_weight[:, None]], 1)
+    copies = jnp.broadcast_to(packed[None], (lax.axis_size("tile"),) + packed.shape)
     order = axis_bits("tile")[:1] + axis_bits("well") + axis_bits("tile")[1:]
-    stacked, packed = all_sum(stacked, order, 2, packed)
+    stacked, copies = all_sum(stacked, order, 2, copies)
     gram_matrix, cross_matrix = stacked[:members], stacked[members:]
     own_count = members // lax.axis_size("well")
     own_start = lax.axis_index("well") * own_count
     system = jnp.eye(members, dtype=jnp.float32) + gram_matrix
     head = block_cholesky(system, min(BLOCK, members - 8), highest)
 
-    copies = jnp.broadcast_to(packed[None], (lax.axis_size("tile"),) + packed.shape)
-    group = lax.all_to_all(copies, "tile", 0, 0, tiled=False).reshape((-1, packed.shape[1]))
+    group = lax.all_to_all(copies, "tile", 0, 0, tiled=False).reshape((-1, copies.shape[2]))
     head, group = lax.optimization_barrier((head, group))
     group_anom, group_innov, group_weight = (
         group[:, :members],
@@ -120,10 +112,16 @@
     )
     taper_gram, taper_cross_t = both[:members], both[members:]
 
-    head, taper_gram, taper_cross_t = lax.optimization_barrier((head, taper_gram, taper_cross_t))
+    inv11, l21, l22 = head
+    split = inv11.shape[0]
+    y1 = jnp.dot(inv11, cross_matrix[:split], precision=highest)
+    rest = cross_matrix[split:] - jnp.dot(l21, y1, precision=highest)
+    head, y1, rest, taper_gram, taper_cross_t = lax.optimization_barrier(
+        (head, y1, rest, taper_gram, taper_cross_t)
+    )
     inv11, l21, l22 = head
     factor = (inv11, l21, lower_inverse(l22, highest))
-    solved = backward(factor, *forward(factor, cross_matrix, highest), highest)
+    solved = backward(factor, y1, jnp.dot(factor[2], rest, precision=highest), highest)
     space_t = taper_cross_t - lax.dot_general(
         solved, taper_gram, (((0,), (1,)), ((), ())), precision=highest
     )
@@ -134,7 +132,7 @@
         send = jnp.where(hi, space_t[:half], space_t[half:])
         space_t = keep + swap(send, axis, k)
     state_anom = (prior_state - jnp.mean(prior_state, axis=1, keepdims=True)) * norm_factor
-    increment = jnp.einsum("vnc,mn->vmc", state_anom, space_t, precision=highest)
+    increment = jnp.einsum("vnc,mn->vmc", state_anom, space_t, precision=lax.Precision.HIGH)
     prior_mine = lax.dynamic_slice_in_dim(prior_state, own_start, own_count, 1)
     return prior_mine + increment
 

time: 98.7 us -> 99.4 us (level)
  no operation moved by 1% of the time
where the time goes in v11:
time: 99.4 us; the launch traced here: 99 us
  other arithmetic  39.9 us (40%)
  waiting for transfers between devices  25.6 us (26%)
  starting transfers between devices  20.1 us (20%)
  matrix products  10.7 us (11%)
  local copies, waits for them, and re-layouts  2.41 us (2%)
    ppermute x9, waiting for transfers between devices, swap(): return lax.ppermute(x, axis, [(i, i ^ k) for i in range(size)])  24.6 us
    another operation x4, other arithmetic, lower_inverse(): lax.linalg.triangular_solve(factor, eye, left_side=True, lower=True, tran...  16.1 us
    ppermute x9, starting transfers between devices, swap(): return lax.ppermute(x, axis, [(i, i ^ k) for i in range(size)])  15.2 us
    another operation x3, other arithmetic, block_cholesky(): l11 = lax.linalg.cholesky(a11, symmetrize_input=False)  12.4 us
    another operation x3, other arithmetic, block_cholesky(): lax.linalg.cholesky(a22 - jnp.dot(l21, l21.T, precision=precision), symme...  7.25 us
    all_to_all x1, starting transfers between devices, shards(): lax.all_to_all(copies, 'tile', 0, 0, tiled=False)  4.85 us
  transfers between devices with their start and end apart: 10, of which 10 were waited for; matrix products, arithmetic and copies ran while one was open for 33% of the time, Pallas kernels for 0%

profile of v11, /device:TPU:0, one launch (start us, length us, event | category | flops | bytes accessed | tf_op | source)
XLA Modules:
  0.0 99.0 jit_solution(9433018598374176880)
XLA Ops:
  0.0 0.9 reduce_sum.18
  0.9 0.7 broadcast_multiply_fusion.1
  1.6 1.0 subtract_multiply_fusion
  2.6 1.2 %fusion.24 = f32[200,200]{0,1:T(8,128)S(1)} fusion(f32[128,200]{0,1:T(8,128)S(1)} %get-tuple-element.36, f32[128,200]{0,1:T(8,128)} %param.7, f32[128]{0:T(128)S(1)} %get-tuple-element.31, f32[128]{0:T(128)S(1)} %get-tuple-element.39), kind=kOutput, calls=%fused_computation.37 | convolution fusion | flops 61491200 | bytes 365824 | tf_op jit(solution)/shard_map/dot_general | solution.py:83
  3.8 1.3 %broadcast_select_fusion = (f32[200,200]{0,1:T(8,128)S(1)}, f32[200,200]{0,1:T(8,128)S(1)}) fusion(f32[200,200]{0,1:T(8,128)S(1)} %fusion.24, pred[]{:T(512)S(6)} %eq.27, f32[128,200]{0,1:T(8,128)} %param.7, f32[128]{0:T(128)S(1)} %get-tuple-element.31, f32[128]{0:T(128)S(1)} %get-tuple-element.39), kind=kOutput, calls=%fused_computation.32 | convolution fusion | flops 61582400 | bytes 583425 | tf_op jit(solution)/shard_map/dot_general | solution.py:82
  5.7 1.1 %collective-permute-done = f32[200,200]{0,1:T(8,128)S(1)} collective-permute-done((f32[200,200]{0,1:T(8,128)S(1)}, f32[200,200]{0,1:T(8,128)S(1)}, u32[]{:S(2)}, u32[]{:S(2)}) %collective-permute-start) | collective-permute-done | bytes 160032 | tf_op jit(solution)/shard_map/ppermute | solution.py:45
  6.9 2.9 %collective-permute-start.1 = (f32[100,200]{0,1:T(8,128)S(1)}, f32[100,200]{0,1:T(8,128)S(1)}, u32[]{:S(2)}, u32[]{:S(2)}) collective-permute-start(f32[100,200]{0,1:T(8,128)S(1)} %slice_select_fusion.1), channel_id=1, source_target_pairs={{0,8},{8,0},{16,24},{24,16},{1,9},{9,1},{17,25},{25,17},{2,10},{10... | collective-permute-start | bytes 240008 | tf_op jit(solution)/shard_map/ppermute | solution.py:45
  9.8 3.2 %collective-permute-done.1 = f32[100,200]{0,1:T(8,128)S(1)} collective-permute-done((f32[100,200]{0,1:T(8,128)S(1)}, f32[100,200]{0,1:T(8,128)S(1)}, u32[]{:S(2)}, u32[]{:S(2)}) %collective-permute-start.1) | collective-permute-done | bytes 80032 | tf_op jit(solution)/shard_map/ppermute | solution.py:45
  13.1 1.8 %collective-permute-start.2 = (f32[100,200]{0,1:T(8,128)S(1)}, f32[100,200]{0,1:T(8,128)S(1)}, u32[]{:S(2)}, u32[]{:S(2)}) collective-permute-start(f32[100,200]{0,1:T(8,128)S(1)} %select_add_fusion.2), channel_id=1, source_target_pairs={{0,16},{8,24},{16,0},{24,8},{1,17},{9,25},{17,1},{25,9},{2,18},{10... | collective-permute-start | bytes 240008 | tf_op jit(solution)/shard_map/ppermute | solution.py:45
  14.9 2.9 %collective-permute-done.2 = f32[100,200]{0,1:T(8,128)S(1)} collective-permute-done((f32[100,200]{0,1:T(8,128)S(1)}, f32[100,200]{0,1:T(8,128)S(1)}, u32[]{:S(2)}, u32[]{:S(2)}) %collective-permute-start.2) | collective-permute-done | bytes 80032 | tf_op jit(solution)/shard_map/ppermute | solution.py:45
  17.9 1.9 %collective-permute-start.3 = (f32[100,200]{0,1:T(8,128)S(1)}, f32[100,200]{0,1:T(8,128)S(1)}, u32[]{:S(2)}, u32[]{:S(2)}) collective-permute-start(f32[100,200]{0,1:T(8,128)S(1)} %add.67), channel_id=1, source_target_pairs={{0,2},{1,3},{2,0},{3,1},{4,6},{5,7},{6,4},{7,5},{8,10},{9,11},{10,... | collective-permute-start | bytes 240008 | tf_op jit(solution)/shard_map/ppermute | solution.py:45
  19.7 2.8 %collective-permute-done.3 = f32[100,200]{0,1:T(8,128)S(1)} collective-permute-done((f32[100,200]{0,1:T(8,128)S(1)}, f32[100,200]{0,1:T(8,128)S(1)}, u32[]{:S(2)}, u32[]{:S(2)}) %collective-permute-start.3) | collective-permute-done | bytes 80032 | tf_op jit(solution)/shard_map/ppermute | solution.py:45
  22.6 3.4 %collective-permute-start.4 = (f32[100,200]{0,1:T(8,128)S(1)}, f32[100,200]{0,1:T(8,128)S(1)}, u32[]{:S(2)}, u32[]{:S(2)}) collective-permute-start(f32[100,200]{0,1:T(8,128)S(1)} %add.68), channel_id=1, source_target_pairs={{0,4},{1,5},{2,6},{3,7},{4,0},{5,1},{6,2},{7,3},{8,12},{9,13},{10,... | collective-permute-start | bytes 240008 | tf_op jit(solution)/shard_map/ppermute | solution.py:45
  26.0 3.7 %collective-permute-done.4 = f32[100,200]{0,1:T(8,128)S(1)} collective-permute-done((f32[100,200]{0,1:T(8,128)S(1)}, f32[100,200]{0,1:T(8,128)S(1)}, u32[]{:S(2)}, u32[]{:S(2)}) %collective-permute-start.4) | collective-permute-done | bytes 80032 | tf_op jit(solution)/shard_map/ppermute | solution.py:45
  29.7 1.3 %broadcast_in_dim.7 = f32[8,128,401]{1,2,0:T(8,128)} broadcast(f32[128,401]{0,1:T(8,128)S(1)} %pad_maximum_fusion), dimensions={1,2} | broadcast | bytes 1847808 | tf_op jit(solution)/shard_map/broadcast_in_dim | solution.py:88
  31.0 4.9 %all-to-all-start = ((f32[8,128,401]{1,2,0:T(8,128)}), f32[8,128,401]{1,2,0:T(8,128)S(1)}, u32[]{:S(2)}, u32[]{:S(2)}) async-start(f32[8,128,401]{1,2,0:T(8,128)} %broadcast_in_dim.7), calls=%async_computation | async-start | bytes 3342336 | tf_op jit(solution)/shard_map/all_to_all | solution.py:97
  35.9 1.5 %collective-permute-start.5 = (f32[100,200]{0,1:T(8,128)S(1)}, f32[100,200]{0,1:T(8,128)S(1)}, u32[]{:S(2)}, u32[]{:S(2)}) collective-permute-start(f32[100,200]{0,1:T(8,128)S(1)} %add.69), channel_id=1, source_target_pairs={{0,8},{8,0},{16,24},{24,16},{1,9},{9,1},{17,25},{25,17},{2,10},{10... | collective-permute-start | bytes 240008 | tf_op jit(solution)/shard_map/ppermute | solution.py:45
  37.4 3.8 %collective-permute-done.5 = f32[100,200]{0,1:T(8,128)S(1)} collective-permute-done((f32[100,200]{0,1:T(8,128)S(1)}, f32[100,200]{0,1:T(8,128)S(1)}, u32[]{:S(2)}, u32[]{:S(2)}) %collective-permute-start.5) | collective-permute-done | bytes 80032 | tf_op jit(solution)/shard_map/ppermute | solution.py:45
  41.5 1.4 %collective-permute-done.6 = f32[200,200]{0,1:T(8,128)S(1)} collective-permute-done((f32[200,200]{0,1:T(8,128)S(1)}, f32[200,200]{0,1:T(8,128)S(1)}, u32[]{:S(2)}, u32[]{:S(2)}) %collective-permute-start.6) | collective-permute-done | bytes 160032 | tf_op jit(solution)/shard_map/ppermute | solution.py:45
  43.3 11.7 %cholesky.37 = f32[128,128]{1,0:T(8,128)S(1)} custom-call(f32[128,128]{1,0:T(8,128)S(1)} %cholesky.82), custom_call_target="Cholesky" | custom-call | tf_op jit(solution)/shard_map/cholesky | solution.py:17
  56.4 9.8 %custom-call.10 = f32[1,128,128]{1,2,0:T(8,128)S(1)} custom-call(f32[1,128,128]{2,1,0:T(8,128)S(1)} %fusion.28), custom_call_target="InvertDiagBlocksLowerTriangular" | custom-call | tf_op jit(solution)/shard_map/triangular_solve | solution.py:11
  66.9 6.6 %cholesky.73 = f32[72,72]{1,0:T(8,128)S(1)} custom-call(f32[72,72]{1,0:T(8,128)S(1)} %convolution_subtract_fusion.2), custom_call_target="Cholesky" | custom-call | tf_op jit(solution)/shard_map/cholesky | solution.py:20
  74.9 1.0 all-to-all-done
  76.7 1.5 %fusion.3 = f32[400,200]{1,0:T(8,128)S(1)} fusion(f32[1024,401]{0,1:T(8,128)S(1)} %bitcast.50, f32[1024]{0:T(1024)S(1)} %bitcast.53), kind=kOutput, calls=%fused_computation.4 | convolution fusion | flops 983244800 | bytes 2781696 | tf_op jit(solution)/shard_map/dot_general | solution.py:107
  78.6 1.0 slice_subtract_fusion
  79.6 5.6 %custom-call.11 = f32[1,72,72]{1,2,0:T(8,128)S(1)} custom-call(f32[1,72,72]{2,1,0:T(8,128)S(1)} %select_bitcast_fusion), custom_call_target="InvertDiagBlocksLowerTriangular" | custom-call | tf_op jit(solution)/shard_map/triangular_solve | solution.py:11
  85.5 1.2 %fusion.51 = f32[72,200]{1,0:T(8,128)S(1)} fusion(f32[72,72]{1,0:T(8,128)S(1)} %fusion.42, f32[72,200]{0,1:T(8,128)} %slice_subtract_fusion), kind=kOutput, calls=%fused_computation.82 | convolution fusion | flops 12441600 | bytes 135936 | tf_op jit(solution)/shard_map/dot_general | solution.py:124
  88.2 1.6 %collective-permute-start.7 = (f32[100,200]{1,0:T(8,128)S(1)}, f32[100,200]{1,0:T(8,128)S(1)}, u32[]{:S(2)}, u32[]{:S(2)}) collective-permute-start(f32[100,200]{1,0:T(8,128)S(1)} %slice_select_fusion), channel_id=1, source_target_pairs={{0,16},{8,24},{16,0},{24,8},{1,17},{9,25},{17,1},{25,9},{2,18},{10... | collective-permute-start | bytes 240008 | tf_op jit(solution)/shard_map/ppermute | solution.py:45
  89.9 3.0 %collective-permute-done.7 = f32[100,200]{1,0:T(8,128)S(1)} collective-permute-done((f32[100,200]{1,0:T(8,128)S(1)}, f32[100,200]{1,0:T(8,128)S(1)}, u32[]{:S(2)}, u32[]{:S(2)}) %collective-permute-start.7) | collective-permute-done | bytes 80032 | tf_op jit(solution)/shard_map/ppermute | solution.py:45
  93.0 1.5 %collective-permute-start.8 = (f32[50,200]{1,0:T(8,128)S(1)}, f32[50,200]{1,0:T(8,128)S(1)}, u32[]{:S(2)}, u32[]{:S(2)}) collective-permute-start(f32[50,200]{1,0:T(8,128)S(1)} %slice_select_fusion.2), channel_id=1, source_target_pairs={{0,8},{8,0},{16,24},{24,16},{1,9},{9,1},{17,25},{25,17},{2,10},{10... | collective-permute-start | bytes 120008 | tf_op jit(solution)/shard_map/ppermute | solution.py:45
  94.5 2.7 %collective-permute-done.8 = f32[50,200]{1,0:T(8,128)S(1)} collective-permute-done((f32[50,200]{1,0:T(8,128)S(1)}, f32[50,200]{1,0:T(8,128)S(1)}, u32[]{:S(2)}, u32[]{:S(2)}) %collective-permute-start.8) | collective-permute-done | bytes 40032 | tf_op jit(solution)/shard_map/ppermute | solution.py:45
  97.2 1.8 %fusion.8 = f32[3,50,1024]{2,1,0:T(8,128)} fusion(f32[3,200,1024]{2,1,0:T(8,128)S(1)} %copy-done, f32[3,1024]{1,0:T(4,128)S(1)} %broadcast_multiply_fusion, s32[]{:T(128)S(6)} %select_n.99, f32[50,200]{1,0:T(8,128)S(1)} %collective-permute-done.8, f32[100,200]{1,0:T(8,128)S(1)} %select_add_fusion.1, pred[]{:T(512)S(6)} %eq.24), kind=kOutput, calls=%fused_computation.7 | convolution fusion | flops 185722400 | bytes 3948549 | tf_op jit(solution)/shard_map/vnc,mn->vmc/dot_general | solution.py:135
  (50 shorter events, 8.0 us)
Async XLA Ops:
  5.2 1.6 %collective-permute-start = (f32[200,200]{0,1:T(8,128)S(1)}, f32[200,200]{0,1:T(8,128)S(1)}, u32[]{:S(2)}, u32[]{:S(2)}) collective-permute-start(f32[200,200]{0,1:T(8,128)S(1)} %get-tuple-element.37), channel_id=1, source_target_pairs={{0,1},{1,0},{2,3},{3,2},{4,5},{5,4},{6,7},{7,6},{8,9},{9,8},{10,11... | collective-permute-start | bytes 480008 | tf_op jit(solution)/shard_map/ppermute | solution.py:45
  6.9 6.1 %collective-permute-start.1 = (f32[100,200]{0,1:T(8,128)S(1)}, f32[100,200]{0,1:T(8,128)S(1)}, u32[]{:S(2)}, u32[]{:S(2)}) collective-permute-start(f32[100,200]{0,1:T(8,128)S(1)} %slice_select_fusion.1), channel_id=1, source_target_pairs={{0,8},{8,0},{16,24},{24,16},{1,9},{9,1},{17,25},{25,17},{2,10},{10... | collective-permute-start | bytes 240008 | tf_op jit(solution)/shard_map/ppermute | solution.py:45
  13.1 4.7 %collective-permute-start.2 = (f32[100,200]{0,1:T(8,128)S(1)}, f32[100,200]{0,1:T(8,128)S(1)}, u32[]{:S(2)}, u32[]{:S(2)}) collective-permute-start(f32[100,200]{0,1:T(8,128)S(1)} %select_add_fusion.2), channel_id=1, source_target_pairs={{0,16},{8,24},{16,0},{24,8},{1,17},{9,25},{17,1},{25,9},{2,18},{10... | collective-permute-start | bytes 240008 | tf_op jit(solution)/shard_map/ppermute | solution.py:45
  17.9 4.7 %collective-permute-start.3 = (f32[100,200]{0,1:T(8,128)S(1)}, f32[100,200]{0,1:T(8,128)S(1)}, u32[]{:S(2)}, u32[]{:S(2)}) collective-permute-start(f32[100,200]{0,1:T(8,128)S(1)} %add.67), channel_id=1, source_target_pairs={{0,2},{1,3},{2,0},{3,1},{4,6},{5,7},{6,4},{7,5},{8,10},{9,11},{10,... | collective-permute-start | bytes 240008 | tf_op jit(solution)/shard_map/ppermute | solution.py:45
  22.6 7.1 %collective-permute-start.4 = (f32[100,200]{0,1:T(8,128)S(1)}, f32[100,200]{0,1:T(8,128)S(1)}, u32[]{:S(2)}, u32[]{:S(2)}) collective-permute-start(f32[100,200]{0,1:T(8,128)S(1)} %add.68), channel_id=1, source_target_pairs={{0,4},{1,5},{2,6},{3,7},{4,0},{5,1},{6,2},{7,3},{8,12},{9,13},{10,... | collective-permute-start | bytes 240008 | tf_op jit(solution)/shard_map/ppermute | solution.py:45
  31.0 10.4 %copy-start.1 = (s32[1,8]{1,0:T(1,128)S(1)}, s32[1,8]{1,0:T(1,128)}, u32[]{:S(2)}) copy-start(s32[1,8]{1,0:T(1,128)} %param.11) | copy-start | bytes 100
  31.0 10.4 %copy-start.2 = (s32[1,8]{1,0:T(1,128)S(1)}, s32[1,8]{1,0:T(1,128)}, u32[]{:S(2)}) copy-start(s32[1,8]{1,0:T(1,128)} %param.10) | copy-start | bytes 100
  31.0 44.8 %all-to-all-start = ((f32[8,128,401]{1,2,0:T(8,128)}), f32[8,128,401]{1,2,0:T(8,128)S(1)}, u32[]{:S(2)}, u32[]{:S(2)}) async-start(f32[8,128,401]{1,2,0:T(8,128)} %broadcast_in_dim.7), calls=%async_computation | async-start | bytes 3342336 | tf_op jit(solution)/shard_map/all_to_all | solution.py:97
  35.9 5.3 %collective-permute-start.5 = (f32[100,200]{0,1:T(8,128)S(1)}, f32[100,200]{0,1:T(8,128)S(1)}, u32[]{:S(2)}, u32[]{:S(2)}) collective-permute-start(f32[100,200]{0,1:T(8,128)S(1)} %add.69), channel_id=1, source_target_pairs={{0,8},{8,0},{16,24},{24,16},{1,9},{9,1},{17,25},{25,17},{2,10},{10... | collective-permute-start | bytes 240008 | tf_op jit(solution)/shard_map/ppermute | solution.py:45
  41.4 1.5 %collective-permute-start.6 = (f32[200,200]{0,1:T(8,128)S(1)}, f32[200,200]{0,1:T(8,128)S(1)}, u32[]{:S(2)}, u32[]{:S(2)}) collective-permute-start(f32[200,200]{0,1:T(8,128)S(1)} %maximum_select_fusion.1), channel_id=1, source_target_pairs={{0,1},{1,0},{2,3},{3,2},{4,5},{5,4},{6,7},{7,6},{8,9},{9,8},{10,11... | collective-permute-start | bytes 480008 | tf_op jit(solution)/shard_map/ppermute | solution.py:45
  78.2 11.5 %copy-start = (f32[3,200,1024]{2,1,0:T(8,128)S(1)}, f32[3,200,1024]{2,1,0:T(8,128)}, u32[]{:S(2)}) copy-start(f32[3,200,1024]{2,1,0:T(8,128)} %param.6) | copy-start | bytes 7372804
  88.2 4.8 %collective-permute-start.7 = (f32[100,200]{1,0:T(8,128)S(1)}, f32[100,200]{1,0:T(8,128)S(1)}, u32[]{:S(2)}, u32[]{:S(2)}) collective-permute-start(f32[100,200]{1,0:T(8,128)S(1)} %slice_select_fusion), channel_id=1, source_target_pairs={{0,16},{8,24},{16,0},{24,8},{1,17},{9,25},{17,1},{25,9},{2,18},{10... | collective-permute-start | bytes 240008 | tf_op jit(solution)/shard_map/ppermute | solution.py:45
  93.0 4.2 %collective-permute-start.8 = (f32[50,200]{1,0:T(8,128)S(1)}, f32[50,200]{1,0:T(8,128)S(1)}, u32[]{:S(2)}, u32[]{:S(2)}) collective-permute-start(f32[50,200]{1,0:T(8,128)S(1)} %slice_select_fusion.2), channel_id=1, source_target_pairs={{0,8},{8,0},{16,24},{24,16},{1,9},{9,1},{17,25},{25,17},{2,10},{10... | collective-permute-start | bytes 120008 | tf_op jit(solution)/shard_map/ppermute | solution.py:45

commit v12 on v9

--- a/solution.py
+++ b/solution.py
@@ -94,7 +94,7 @@
     )
     packed = jnp.concatenate([data_anom, innov, row_weight[:, None]], 1)
     order = axis_bits("tile")[:1] + axis_bits("well") + axis_bits("tile")[1:]
-    stacked, packed = all_sum(stacked, order, 2, packed)
+    stacked, packed = all_sum(stacked, order, 1, packed)
     gram_matrix, cross_matrix = stacked[:members], stacked[members:]
     own_count = members // lax.axis_size("well")
     own_start = lax.axis_index("well") * own_count

time: 98.7 us -> 106 us (1.074)
  waiting for transfers between devices: 25.6 us -> 35.9 us
  starting transfers between devices: 20.1 us -> 17.7 us
    all_to_all x1, waiting for transfers between devices: 0.98 us -> 6.22 us  [shards(): lax.all_to_all(copies, 'tile', 0, 0, tiled=False)]
    ppermute x9 -> x8, waiting for transfers between devices: 24.7 us -> 29.7 us  [swap(): return lax.ppermute(x, axis, [(i, i ^ k) for i in range(size)])]
    ppermute x9 -> x8, starting transfers between devices: 15.2 us -> 13.2 us  [swap(): return lax.ppermute(x, axis, [(i, i ^ k) for i in range(size)])]
  transfers between devices with their start and end apart: 10 -> 9, of which waited for: 10 -> 9; matrix products, arithmetic and copies ran while one was open for 33% -> 30% of each run, Pallas kernels for 0% -> 0%
where the time goes in v12:
time: 106 us
  other arithmetic  39.5 us (37%)
  waiting for transfers between devices  35.9 us (34%)
  starting transfers between devices  17.7 us (17%)
  matrix products  10.2 us (10%)
  local copies, waits for them, and re-layouts  2.41 us (2%)
    ppermute x8, waiting for transfers between devices, swap(): return lax.ppermute(x, axis, [(i, i ^ k) for i in range(size)])  29.7 us
    another operation x4, other arithmetic, lower_inverse(): lax.linalg.triangular_solve(factor, eye, left_side=True, lower=True, tran...  16 us
    ppermute x8, starting transfers between devices, swap(): return lax.ppermute(x, axis, [(i, i ^ k) for i in range(size)])  13.2 us
    another operation x3, other arithmetic, block_cholesky(): l11 = lax.linalg.cholesky(a11, symmetrize_input=False)  12.4 us
    another operation x3, other arithmetic, block_cholesky(): lax.linalg.cholesky(a22 - jnp.dot(l21, l21.T, precision=precision), symme...  7.25 us
    all_to_all x1, waiting for transfers between devices, shards(): lax.all_to_all(copies, 'tile', 0, 0, tiled=False)  6.22 us
    all_to_all x1, starting transfers between devices, shards(): lax.all_to_all(copies, 'tile', 0, 0, tiled=False)  4.49 us
    dot_general x1, matrix products, shards(): jnp.einsum('vnc,mn->vmc', state_anom, space_t, precision=highest)  2.64 us
  transfers between devices with their start and end apart: 9, of which 9 were waited for; matrix products, arithmetic and copies ran while one was open for 30% of the time, Pallas kernels for 0%

profile of v12, /device:TPU:0, one launch (start us, length us, event | category | flops | bytes accessed | tf_op | source)
XLA Modules:
  0.0 106.0 jit_solution(8804878257592455229)
XLA Ops:
  0.0 0.9 reduce_sum.18
  0.9 0.7 broadcast_multiply_fusion.1
  1.6 1.0 subtract_multiply_fusion
  2.6 1.2 %fusion.25 = f32[200,200]{0,1:T(8,128)S(1)} fusion(f32[128,200]{0,1:T(8,128)S(1)} %get-tuple-element.32, f32[128,200]{0,1:T(8,128)} %param.7, f32[128]{0:T(128)S(1)} %get-tuple-element.27, f32[128]{0:T(128)S(1)} %get-tuple-element.35), kind=kOutput, calls=%fused_computation.35 | convolution fusion | flops 61491200 | bytes 365824 | tf_op jit(solution)/shard_map/dot_general | solution.py:91
  3.8 1.3 %broadcast_select_fusion = (f32[200,200]{0,1:T(8,128)S(1)}, f32[200,200]{0,1:T(8,128)S(1)}) fusion(f32[200,200]{0,1:T(8,128)S(1)} %fusion.25, pred[]{:T(512)S(6)} %eq.23, f32[128,200]{0,1:T(8,128)} %param.7, f32[128]{0:T(128)S(1)} %get-tuple-element.27, f32[128]{0:T(128)S(1)} %get-tuple-element.35), kind=kOutput, calls=%fused_computation.31 | convolution fusion | flops 61582400 | bytes 583425 | tf_op jit(solution)/shard_map/dot_general | solution.py:90
  5.7 1.1 %collective-permute-done = f32[200,200]{0,1:T(8,128)S(1)} collective-permute-done((f32[200,200]{0,1:T(8,128)S(1)}, f32[200,200]{0,1:T(8,128)S(1)}, u32[]{:S(2)}, u32[]{:S(2)}) %collective-permute-start) | collective-permute-done | bytes 160032 | tf_op jit(solution)/shard_map/ppermute | solution.py:53
  6.8 2.9 %collective-permute-start.1 = (f32[200,200]{0,1:T(8,128)S(1)}, f32[200,200]{0,1:T(8,128)S(1)}, u32[]{:S(2)}, u32[]{:S(2)}) collective-permute-start(f32[200,200]{0,1:T(8,128)S(1)} %select_add_fusion), channel_id=1, source_target_pairs={{0,8},{8,0},{16,24},{24,16},{1,9},{9,1},{17,25},{25,17},{2,10},{10... | collective-permute-start | bytes 480008 | tf_op jit(solution)/shard_map/ppermute | solution.py:53
  9.7 5.4 %collective-permute-done.1 = f32[200,200]{0,1:T(8,128)S(1)} collective-permute-done((f32[200,200]{0,1:T(8,128)S(1)}, f32[200,200]{0,1:T(8,128)S(1)}, u32[]{:S(2)}, u32[]{:S(2)}) %collective-permute-start.1) | collective-permute-done | bytes 160032 | tf_op jit(solution)/shard_map/ppermute | solution.py:53
  15.1 1.8 %collective-permute-start.2 = (f32[200,200]{0,1:T(8,128)S(1)}, f32[200,200]{0,1:T(8,128)S(1)}, u32[]{:S(2)}, u32[]{:S(2)}) collective-permute-start(f32[200,200]{0,1:T(8,128)S(1)} %add.64), channel_id=1, source_target_pairs={{0,16},{8,24},{16,0},{24,8},{1,17},{9,25},{17,1},{25,9},{2,18},{10... | collective-permute-start | bytes 480008 | tf_op jit(solution)/shard_map/ppermute | solution.py:53
  17.0 4.8 %collective-permute-done.2 = f32[200,200]{0,1:T(8,128)S(1)} collective-permute-done((f32[200,200]{0,1:T(8,128)S(1)}, f32[200,200]{0,1:T(8,128)S(1)}, u32[]{:S(2)}, u32[]{:S(2)}) %collective-permute-start.2) | collective-permute-done | bytes 160032 | tf_op jit(solution)/shard_map/ppermute | solution.py:53
  21.8 1.6 %collective-permute-start.3 = (f32[200,200]{0,1:T(8,128)S(1)}, f32[200,200]{0,1:T(8,128)S(1)}, u32[]{:S(2)}, u32[]{:S(2)}) collective-permute-start(f32[200,200]{0,1:T(8,128)S(1)} %add.65), channel_id=1, source_target_pairs={{0,2},{1,3},{2,0},{3,1},{4,6},{5,7},{6,4},{7,5},{8,10},{9,11},{10,... | collective-permute-start | bytes 480008 | tf_op jit(solution)/shard_map/ppermute | solution.py:53
  23.4 4.2 %collective-permute-done.3 = f32[200,200]{0,1:T(8,128)S(1)} collective-permute-done((f32[200,200]{0,1:T(8,128)S(1)}, f32[200,200]{0,1:T(8,128)S(1)}, u32[]{:S(2)}, u32[]{:S(2)}) %collective-permute-start.3) | collective-permute-done | bytes 160032 | tf_op jit(solution)/shard_map/ppermute | solution.py:53
  27.7 2.7 %collective-permute-start.4 = (f32[200,200]{0,1:T(8,128)S(1)}, f32[200,200]{0,1:T(8,128)S(1)}, u32[]{:S(2)}, u32[]{:S(2)}) collective-permute-start(f32[200,200]{0,1:T(8,128)S(1)} %add.66), channel_id=1, source_target_pairs={{0,4},{1,5},{2,6},{3,7},{4,0},{5,1},{6,2},{7,3},{8,12},{9,13},{10,... | collective-permute-start | bytes 480008 | tf_op jit(solution)/shard_map/ppermute | solution.py:53
  30.4 7.2 %collective-permute-done.4 = f32[200,200]{0,1:T(8,128)S(1)} collective-permute-done((f32[200,200]{0,1:T(8,128)S(1)}, f32[200,200]{0,1:T(8,128)S(1)}, u32[]{:S(2)}, u32[]{:S(2)}) %collective-permute-start.4) | collective-permute-done | bytes 160032 | tf_op jit(solution)/shard_map/ppermute | solution.py:53
  37.6 1.3 %broadcast_in_dim.7 = f32[8,128,401]{1,2,0:T(8,128)} broadcast(f32[128,401]{0,1:T(8,128)S(1)} %pad_maximum_fusion), dimensions={1,2} | broadcast | bytes 1847808 | tf_op jit(solution)/shard_map/broadcast_in_dim | solution.py:104
  38.9 4.5 %all-to-all-start = ((f32[8,128,401]{1,2,0:T(8,128)}), f32[8,128,401]{1,2,0:T(8,128)S(1)}, u32[]{:S(2)}, u32[]{:S(2)}) async-start(f32[8,128,401]{1,2,0:T(8,128)} %broadcast_in_dim.7), calls=%async_computation | async-start | bytes 3342336 | tf_op jit(solution)/shard_map/all_to_all | solution.py:105
  44.0 1.2 %collective-permute-done.5 = f32[200,200]{0,1:T(8,128)S(1)} collective-permute-done((f32[200,200]{0,1:T(8,128)S(1)}, f32[200,200]{0,1:T(8,128)S(1)}, u32[]{:S(2)}, u32[]{:S(2)}) %collective-permute-start.5) | collective-permute-done | bytes 160032 | tf_op jit(solution)/shard_map/ppermute | solution.py:53
  45.6 11.7 %cholesky.37 = f32[128,128]{1,0:T(8,128)S(1)} custom-call(f32[128,128]{1,0:T(8,128)S(1)} %cholesky.82), custom_call_target="Cholesky" | custom-call | tf_op jit(solution)/shard_map/cholesky | solution.py:17
  57.4 0.6 compare_reduce_fusion.1
  58.0 0.7 fusion.29
  58.7 9.8 %custom-call.10 = f32[1,128,128]{1,2,0:T(8,128)S(1)} custom-call(f32[1,128,128]{2,1,0:T(8,128)S(1)} %fusion.29), custom_call_target="InvertDiagBlocksLowerTriangular" | custom-call | tf_op jit(solution)/shard_map/triangular_solve | solution.py:11
  69.2 6.6 %cholesky.73 = f32[72,72]{1,0:T(8,128)S(1)} custom-call(f32[72,72]{1,0:T(8,128)S(1)} %convolution_subtract_fusion.2), custom_call_target="Cholesky" | custom-call | tf_op jit(solution)/shard_map/cholesky | solution.py:20
  75.9 0.6 compare_reduce_fusion
  76.5 0.7 select_select_fusion.1
  77.2 6.2 %all-to-all-done = f32[8,128,401]{1,2,0:T(8,128)S(1)} async-done(((f32[8,128,401]{1,2,0:T(8,128)}), f32[8,128,401]{1,2,0:T(8,128)S(1)}, u32[]{:S(2)}, u32[]{:S(2)}) %all-to-all-start) | async-done | bytes 1642528 | tf_op jit(solution)/shard_map/all_to_all | solution.py:105
  84.3 1.5 %fusion.3 = f32[400,200]{1,0:T(8,128)S(1)} fusion(f32[1024,401]{0,1:T(8,128)S(1)} %bitcast.49, f32[1024]{0:T(1024)S(1)} %bitcast.52), kind=kOutput, calls=%fused_computation.4 | convolution fusion | flops 983244800 | bytes 2781696 | tf_op jit(solution)/shard_map/dot_general | solution.py:115
  86.2 5.5 %custom-call.11 = f32[1,72,72]{1,2,0:T(8,128)S(1)} custom-call(f32[1,72,72]{2,1,0:T(8,128)S(1)} %select_bitcast_fusion), custom_call_target="InvertDiagBlocksLowerTriangular" | custom-call | tf_op jit(solution)/shard_map/triangular_solve | solution.py:11
  94.3 1.6 %collective-permute-start.6 = (f32[100,200]{1,0:T(8,128)S(1)}, f32[100,200]{1,0:T(8,128)S(1)}, u32[]{:S(2)}, u32[]{:S(2)}) collective-permute-start(f32[100,200]{1,0:T(8,128)S(1)} %slice_select_fusion), channel_id=1, source_target_pairs={{0,16},{8,24},{16,0},{24,8},{1,17},{9,25},{17,1},{25,9},{2,18},{10... | collective-permute-start | bytes 240008 | tf_op jit(solution)/shard_map/ppermute | solution.py:53
  96.1 3.0 %collective-permute-done.6 = f32[100,200]{1,0:T(8,128)S(1)} collective-permute-done((f32[100,200]{1,0:T(8,128)S(1)}, f32[100,200]{1,0:T(8,128)S(1)}, u32[]{:S(2)}, u32[]{:S(2)}) %collective-permute-start.6) | collective-permute-done | bytes 80032 | tf_op jit(solution)/shard_map/ppermute | solution.py:53
  99.1 1.6 %collective-permute-start.7 = (f32[50,200]{1,0:T(8,128)S(1)}, f32[50,200]{1,0:T(8,128)S(1)}, u32[]{:S(2)}, u32[]{:S(2)}) collective-permute-start(f32[50,200]{1,0:T(8,128)S(1)} %slice_select_fusion.1), channel_id=1, source_target_pairs={{0,8},{8,0},{16,24},{24,16},{1,9},{9,1},{17,25},{25,17},{2,10},{10... | collective-permute-start | bytes 120008 | tf_op jit(solution)/shard_map/ppermute | solution.py:53
  100.7 2.7 %collective-permute-done.7 = f32[50,200]{1,0:T(8,128)S(1)} collective-permute-done((f32[50,200]{1,0:T(8,128)S(1)}, f32[50,200]{1,0:T(8,128)S(1)}, u32[]{:S(2)}, u32[]{:S(2)}) %collective-permute-start.7) | collective-permute-done | bytes 40032 | tf_op jit(solution)/shard_map/ppermute | solution.py:53
  103.4 2.6 %fusion.8 = f32[3,50,1024]{2,1,0:T(8,128)} fusion(f32[3,200,1024]{2,1,0:T(8,128)S(1)} %copy-done, f32[3,1024]{1,0:T(4,128)S(1)} %broadcast_multiply_fusion, s32[]{:T(128)S(6)} %select_n.77, f32[50,200]{1,0:T(8,128)S(1)} %collective-permute-done.7, f32[100,200]{1,0:T(8,128)S(1)} %select_add_fusion.1, pred[]{:T(512)S(6)} %eq.20), kind=kOutput, calls=%fused_computation.7 | convolution fusion | flops 370042400 | bytes 3948549 | tf_op jit(solution)/shard_map/vnc,mn->vmc/dot_general | solution.py:137
  (46 shorter events, 6.5 us)
Async XLA Ops:
  5.2 1.6 %collective-permute-start = (f32[200,200]{0,1:T(8,128)S(1)}, f32[200,200]{0,1:T(8,128)S(1)}, u32[]{:S(2)}, u32[]{:S(2)}) collective-permute-start(f32[200,200]{0,1:T(8,128)S(1)} %get-tuple-element.33), channel_id=1, source_target_pairs={{0,1},{1,0},{2,3},{3,2},{4,5},{5,4},{6,7},{7,6},{8,9},{9,8},{10,11... | collective-permute-start | bytes 480008 | tf_op jit(solution)/shard_map/ppermute | solution.py:53
  6.8 8.3 %collective-permute-start.1 = (f32[200,200]{0,1:T(8,128)S(1)}, f32[200,200]{0,1:T(8,128)S(1)}, u32[]{:S(2)}, u32[]{:S(2)}) collective-permute-start(f32[200,200]{0,1:T(8,128)S(1)} %select_add_fusion), channel_id=1, source_target_pairs={{0,8},{8,0},{16,24},{24,16},{1,9},{9,1},{17,25},{25,17},{2,10},{10... | collective-permute-start | bytes 480008 | tf_op jit(solution)/shard_map/ppermute | solution.py:53
  15.1 6.7 %collective-permute-start.2 = (f32[200,200]{0,1:T(8,128)S(1)}, f32[200,200]{0,1:T(8,128)S(1)}, u32[]{:S(2)}, u32[]{:S(2)}) collective-permute-start(f32[200,200]{0,1:T(8,128)S(1)} %add.64), channel_id=1, source_target_pairs={{0,16},{8,24},{16,0},{24,8},{1,17},{9,25},{17,1},{25,9},{2,18},{10... | collective-permute-start | bytes 480008 | tf_op jit(solution)/shard_map/ppermute | solution.py:53
  21.8 5.8 %collective-permute-start.3 = (f32[200,200]{0,1:T(8,128)S(1)}, f32[200,200]{0,1:T(8,128)S(1)}, u32[]{:S(2)}, u32[]{:S(2)}) collective-permute-start(f32[200,200]{0,1:T(8,128)S(1)} %add.65), channel_id=1, source_target_pairs={{0,2},{1,3},{2,0},{3,1},{4,6},{5,7},{6,4},{7,5},{8,10},{9,11},{10,... | collective-permute-start | bytes 480008 | tf_op jit(solution)/shard_map/ppermute | solution.py:53
  27.7 9.9 %collective-permute-start.4 = (f32[200,200]{0,1:T(8,128)S(1)}, f32[200,200]{0,1:T(8,128)S(1)}, u32[]{:S(2)}, u32[]{:S(2)}) collective-permute-start(f32[200,200]{0,1:T(8,128)S(1)} %add.66), channel_id=1, source_target_pairs={{0,4},{1,5},{2,6},{3,7},{4,0},{5,1},{6,2},{7,3},{8,12},{9,13},{10,... | collective-permute-start | bytes 480008 | tf_op jit(solution)/shard_map/ppermute | solution.py:53
  38.9 5.0 %copy-start.1 = (s32[1,8]{1,0:T(1,128)S(1)}, s32[1,8]{1,0:T(1,128)}, u32[]{:S(2)}) copy-start(s32[1,8]{1,0:T(1,128)} %param.11) | copy-start | bytes 100
  38.9 5.0 %copy-start.2 = (s32[1,8]{1,0:T(1,128)S(1)}, s32[1,8]{1,0:T(1,128)}, u32[]{:S(2)}) copy-start(s32[1,8]{1,0:T(1,128)} %param.10) | copy-start | bytes 100
  38.9 44.4 %all-to-all-start = ((f32[8,128,401]{1,2,0:T(8,128)}), f32[8,128,401]{1,2,0:T(8,128)S(1)}, u32[]{:S(2)}, u32[]{:S(2)}) async-start(f32[8,128,401]{1,2,0:T(8,128)} %broadcast_in_dim.7), calls=%async_computation | async-start | bytes 3342336 | tf_op jit(solution)/shard_map/all_to_all | solution.py:105
  43.4 1.7 %collective-permute-start.5 = (f32[200,200]{0,1:T(8,128)S(1)}, f32[200,200]{0,1:T(8,128)S(1)}, u32[]{:S(2)}, u32[]{:S(2)}) collective-permute-start(f32[200,200]{0,1:T(8,128)S(1)} %add.67), channel_id=1, source_target_pairs={{0,1},{1,0},{2,3},{3,2},{4,5},{5,4},{6,7},{7,6},{8,9},{9,8},{10,11... | collective-permute-start | bytes 480008 | tf_op jit(solution)/shard_map/ppermute | solution.py:53
  85.8 10.1 %copy-start = (f32[3,200,1024]{2,1,0:T(8,128)S(1)}, f32[3,200,1024]{2,1,0:T(8,128)}, u32[]{:S(2)}) copy-start(f32[3,200,1024]{2,1,0:T(8,128)} %param.6) | copy-start | bytes 7372804
  94.3 4.8 %collective-permute-start.6 = (f32[100,200]{1,0:T(8,128)S(1)}, f32[100,200]{1,0:T(8,128)S(1)}, u32[]{:S(2)}, u32[]{:S(2)}) collective-permute-start(f32[100,200]{1,0:T(8,128)S(1)} %slice_select_fusion), channel_id=1, source_target_pairs={{0,16},{8,24},{16,0},{24,8},{1,17},{9,25},{17,1},{25,9},{2,18},{10... | collective-permute-start | bytes 240008 | tf_op jit(solution)/shard_map/ppermute | solution.py:53
  99.1 4.2 %collective-permute-start.7 = (f32[50,200]{1,0:T(8,128)S(1)}, f32[50,200]{1,0:T(8,128)S(1)}, u32[]{:S(2)}, u32[]{:S(2)}) collective-permute-start(f32[50,200]{1,0:T(8,128)S(1)} %slice_select_fusion.1), channel_id=1, source_target_pairs={{0,8},{8,0},{16,24},{24,16},{1,9},{9,1},{17,25},{25,17},{2,10},{10... | collective-permute-start | bytes 120008 | tf_op jit(solution)/shard_map/ppermute | solution.py:53

commit v13 on v12

--- a/solution.py
+++ b/solution.py
@@ -62,8 +62,11 @@
     return out
 
 
-def all_sum(x, steps, halvings, tie):
-    for axis, k in steps[:halvings]:
+def all_sum(first, steps, halvings, tie):
+    keep, send = first
+    axis, k = steps[0]
+    x = keep + swap(send, axis, k)
+    for axis, k in steps[1:halvings]:
         half = x.shape[0] // 2
         hi = bit_of(axis, k) == 1
         keep = jnp.where(hi, x[half:], x[:half])
@@ -85,16 +88,14 @@
     norm_factor = 1.0 / jnp.sqrt(jnp.float32(members - 1))
     data_anom, innov, row_weight, scaled = prepare(pred_data, obs_pert, obs_std, norm_factor)
 
-    stacked = jnp.concatenate(
-        [
-            jnp.dot(data_anom.T, scaled, precision=highest),
-            jnp.dot(scaled.T, innov, precision=highest),
-        ],
-        0,
-    )
+    order = axis_bits("tile")[:1] + axis_bits("well") + axis_bits("tile")[1:]
+    hi = bit_of(*order[0]) == 1
+    halves = [
+        jnp.dot(jnp.where(a, scaled, data_anom).T, jnp.where(a, innov, scaled), precision=highest)
+        for a in (hi, jnp.logical_not(hi))
+    ]
     packed = jnp.concatenate([data_anom, innov, row_weight[:, None]], 1)
-    order = axis_bits("tile")[:1] + axis_bits("well") + axis_bits("tile")[1:]
-    stacked, packed = all_sum(stacked, order, 1, packed)
+    stacked, packed = all_sum(halves, order, 2, packed)
     gram_matrix, cross_matrix = stacked[:members], stacked[members:]
     own_count = members // lax.axis_size("well")
     own_start = lax.axis_index("well") * own_count

time: 106 us -> 98.7 us (0.931)
  waiting for transfers between devices: 35.9 us -> 25.6 us
  starting transfers between devices: 17.7 us -> 20.1 us
    all_to_all x1, waiting for transfers between devices: 6.22 us -> 0.98 us  [shards(): lax.all_to_all(copies, 'tile', 0, 0, tiled=False)]
    ppermute x8 -> x9, waiting for transfers between devices: 29.7 us -> 24.6 us  [swap(): return lax.ppermute(x, axis, [(i, i ^ k) for i in range(size)])]
    ppermute x8 -> x9, starting transfers between devices: 13.2 us -> 15.3 us  [swap(): return lax.ppermute(x, axis, [(i, i ^ k) for i in range(size)])]
  transfers between devices with their start and end apart: 9 -> 10, of which waited for: 9 -> 10; matrix products, arithmetic and copies ran while one was open for 30% -> 33% of each run, Pallas kernels for 0% -> 0%
where the time goes in v13:
time: 98.7 us; the launch traced here: 98.4 us
  other arithmetic  39.8 us (40%)
  waiting for transfers between devices  25.6 us (26%)
  starting transfers between devices  20.1 us (20%)
  matrix products  10.2 us (10%)
  local copies, waits for them, and re-layouts  2.41 us (2%)
    ppermute x9, waiting for transfers between devices, swap(): return lax.ppermute(x, axis, [(i, i ^ k) for i in range(size)])  24.6 us
    another operation x4, other arithmetic, lower_inverse(): lax.linalg.triangular_solve(factor, eye, left_side=True, lower=True, tran...  16 us
    ppermute x9, starting transfers between devices, swap(): return lax.ppermute(x, axis, [(i, i ^ k) for i in range(size)])  15.3 us
    another operation x3, other arithmetic, block_cholesky(): l11 = lax.linalg.cholesky(a11, symmetrize_input=False)  12.4 us
    another operation x3, other arithmetic, block_cholesky(): lax.linalg.cholesky(a22 - jnp.dot(l21, l21.T, precision=precision), symme...  7.25 us
    all_to_all x1, starting transfers between devices, shards(): lax.all_to_all(copies, 'tile', 0, 0, tiled=False)  4.86 us
    dot_general x2, matrix products, shards(): jnp.dot(jnp.where(a, scaled, data_anom).T, jnp.where(a, innov, scaled), p...  2.66 us
    dot_general x1, matrix products, shards(): jnp.einsum('vnc,mn->vmc', state_anom, space_t, precision=highest)  2.64 us
  transfers between devices with their start and end apart: 10, of which 10 were waited for; matrix products, arithmetic and copies ran while one was open for 33% of the time, Pallas kernels for 0%

profile of v13, /device:TPU:0, one launch (start us, length us, event | category | flops | bytes accessed | tf_op | source)
XLA Modules:
  0.0 98.4 jit_solution(16977969823524250627)
XLA Ops:
  0.0 0.9 reduce_sum.18
  0.9 0.7 broadcast_multiply_fusion.1
  1.6 1.0 subtract_multiply_fusion
  2.6 1.3 %fusion.23 = f32[200,200]{0,1:T(8,128)S(1)} fusion(f32[128,200]{0,1:T(8,128)S(1)} %get-tuple-element.32, f32[128,200]{0,1:T(8,128)} %param.7, f32[128]{0:T(128)S(1)} %get-tuple-element.27, f32[128]{0:T(128)S(1)} %get-tuple-element.33, pred[]{:T(512)S(6)} %not.3), kind=kOutput, calls=%fused_computation.33 | convolution fusion | flops 61619200 | bytes 365825 | tf_op jit(solution)/shard_map/dot_general | solution.py:94
  4.4 1.1 %collective-permute-done = f32[200,200]{0,1:T(8,128)S(1)} collective-permute-done((f32[200,200]{0,1:T(8,128)S(1)}, f32[200,200]{0,1:T(8,128)S(1)}, u32[]{:S(2)}, u32[]{:S(2)}) %collective-permute-start) | collective-permute-done | bytes 160032 | tf_op jit(solution)/shard_map/ppermute | solution.py:53
  5.5 1.3 %convolution_add_fusion = f32[200,200]{0,1:T(8,128)S(1)} fusion(f32[200,200]{0,1:T(8,128)S(1)} %collective-permute-done, f32[128,200]{0,1:T(8,128)S(1)} %get-tuple-element.32, f32[128,200]{0,1:T(8,128)} %param.7, f32[128]{0:T(128)S(1)} %get-tuple-element.27, f32[128]{0:T(128)S(1)} %get-tuple-element.33, pred[]{:T(512)S(6)} %eq.27), kind=kOutput, calls=%fused_computation.11 | convolution fusion | flops 61659200 | bytes 525825 | tf_op jit(solution)/shard_map/dot_general | solution.py:94
  6.9 2.9 %collective-permute-start.1 = (f32[100,200]{0,1:T(8,128)S(1)}, f32[100,200]{0,1:T(8,128)S(1)}, u32[]{:S(2)}, u32[]{:S(2)}) collective-permute-start(f32[100,200]{0,1:T(8,128)S(1)} %slice_select_fusion.1), channel_id=1, source_target_pairs={{0,8},{8,0},{16,24},{24,16},{1,9},{9,1},{17,25},{25,17},{2,10},{10... | collective-permute-start | bytes 240008 | tf_op jit(solution)/shard_map/ppermute | solution.py:53
  9.9 3.2 %collective-permute-done.1 = f32[100,200]{0,1:T(8,128)S(1)} collective-permute-done((f32[100,200]{0,1:T(8,128)S(1)}, f32[100,200]{0,1:T(8,128)S(1)}, u32[]{:S(2)}, u32[]{:S(2)}) %collective-permute-start.1) | collective-permute-done | bytes 80032 | tf_op jit(solution)/shard_map/ppermute | solution.py:53
  13.1 1.8 %collective-permute-start.2 = (f32[100,200]{0,1:T(8,128)S(1)}, f32[100,200]{0,1:T(8,128)S(1)}, u32[]{:S(2)}, u32[]{:S(2)}) collective-permute-start(f32[100,200]{0,1:T(8,128)S(1)} %select_add_fusion.1), channel_id=1, source_target_pairs={{0,16},{8,24},{16,0},{24,8},{1,17},{9,25},{17,1},{25,9},{2,18},{10... | collective-permute-start | bytes 240008 | tf_op jit(solution)/shard_map/ppermute | solution.py:53
  15.0 2.9 %collective-permute-done.2 = f32[100,200]{0,1:T(8,128)S(1)} collective-permute-done((f32[100,200]{0,1:T(8,128)S(1)}, f32[100,200]{0,1:T(8,128)S(1)}, u32[]{:S(2)}, u32[]{:S(2)}) %collective-permute-start.2) | collective-permute-done | bytes 80032 | tf_op jit(solution)/shard_map/ppermute | solution.py:53
  17.9 1.9 %collective-permute-start.3 = (f32[100,200]{0,1:T(8,128)S(1)}, f32[100,200]{0,1:T(8,128)S(1)}, u32[]{:S(2)}, u32[]{:S(2)}) collective-permute-start(f32[100,200]{0,1:T(8,128)S(1)} %add.67), channel_id=1, source_target_pairs={{0,2},{1,3},{2,0},{3,1},{4,6},{5,7},{6,4},{7,5},{8,10},{9,11},{10,... | collective-permute-start | bytes 240008 | tf_op jit(solution)/shard_map/ppermute | solution.py:53
  19.8 2.8 %collective-permute-done.3 = f32[100,200]{0,1:T(8,128)S(1)} collective-permute-done((f32[100,200]{0,1:T(8,128)S(1)}, f32[100,200]{0,1:T(8,128)S(1)}, u32[]{:S(2)}, u32[]{:S(2)}) %collective-permute-start.3) | collective-permute-done | bytes 80032 | tf_op jit(solution)/shard_map/ppermute | solution.py:53
  22.6 3.4 %collective-permute-start.4 = (f32[100,200]{0,1:T(8,128)S(1)}, f32[100,200]{0,1:T(8,128)S(1)}, u32[]{:S(2)}, u32[]{:S(2)}) collective-permute-start(f32[100,200]{0,1:T(8,128)S(1)} %add.68), channel_id=1, source_target_pairs={{0,4},{1,5},{2,6},{3,7},{4,0},{5,1},{6,2},{7,3},{8,12},{9,13},{10,... | collective-permute-start | bytes 240008 | tf_op jit(solution)/shard_map/ppermute | solution.py:53
  26.0 3.7 %collective-permute-done.4 = f32[100,200]{0,1:T(8,128)S(1)} collective-permute-done((f32[100,200]{0,1:T(8,128)S(1)}, f32[100,200]{0,1:T(8,128)S(1)}, u32[]{:S(2)}, u32[]{:S(2)}) %collective-permute-start.4) | collective-permute-done | bytes 80032 | tf_op jit(solution)/shard_map/ppermute | solution.py:53
  29.8 1.3 %broadcast_in_dim.7 = f32[8,128,401]{1,2,0:T(8,128)} broadcast(f32[128,401]{0,1:T(8,128)S(1)} %pad_maximum_fusion), dimensions={1,2} | broadcast | bytes 1847808 | tf_op jit(solution)/shard_map/broadcast_in_dim | solution.py:105
  31.1 4.9 %all-to-all-start = ((f32[8,128,401]{1,2,0:T(8,128)}), f32[8,128,401]{1,2,0:T(8,128)S(1)}, u32[]{:S(2)}, u32[]{:S(2)}) async-start(f32[8,128,401]{1,2,0:T(8,128)} %broadcast_in_dim.7), calls=%async_computation | async-start | bytes 3342336 | tf_op jit(solution)/shard_map/all_to_all | solution.py:106
  35.9 1.5 %collective-permute-start.5 = (f32[100,200]{0,1:T(8,128)S(1)}, f32[100,200]{0,1:T(8,128)S(1)}, u32[]{:S(2)}, u32[]{:S(2)}) collective-permute-start(f32[100,200]{0,1:T(8,128)S(1)} %add.69), channel_id=1, source_target_pairs={{0,8},{8,0},{16,24},{24,16},{1,9},{9,1},{17,25},{25,17},{2,10},{10... | collective-permute-start | bytes 240008 | tf_op jit(solution)/shard_map/ppermute | solution.py:53
  37.4 3.8 %collective-permute-done.5 = f32[100,200]{0,1:T(8,128)S(1)} collective-permute-done((f32[100,200]{0,1:T(8,128)S(1)}, f32[100,200]{0,1:T(8,128)S(1)}, u32[]{:S(2)}, u32[]{:S(2)}) %collective-permute-start.5) | collective-permute-done | bytes 80032 | tf_op jit(solution)/shard_map/ppermute | solution.py:53
  41.5 1.4 %collective-permute-done.6 = f32[200,200]{0,1:T(8,128)S(1)} collective-permute-done((f32[200,200]{0,1:T(8,128)S(1)}, f32[200,200]{0,1:T(8,128)S(1)}, u32[]{:S(2)}, u32[]{:S(2)}) %collective-permute-start.6) | collective-permute-done | bytes 160032 | tf_op jit(solution)/shard_map/ppermute | solution.py:53
  43.4 11.7 %cholesky.37 = f32[128,128]{1,0:T(8,128)S(1)} custom-call(f32[128,128]{1,0:T(8,128)S(1)} %cholesky.82), custom_call_target="Cholesky" | custom-call | tf_op jit(solution)/shard_map/cholesky | solution.py:17
  55.7 0.7 fusion.32
  56.4 9.8 %custom-call.10 = f32[1,128,128]{1,2,0:T(8,128)S(1)} custom-call(f32[1,128,128]{2,1,0:T(8,128)S(1)} %fusion.32), custom_call_target="InvertDiagBlocksLowerTriangular" | custom-call | tf_op jit(solution)/shard_map/triangular_solve | solution.py:11
  67.0 6.6 %cholesky.73 = f32[72,72]{1,0:T(8,128)S(1)} custom-call(f32[72,72]{1,0:T(8,128)S(1)} %convolution_subtract_fusion.2), custom_call_target="Cholesky" | custom-call | tf_op jit(solution)/shard_map/cholesky | solution.py:20
  74.2 0.7 select_select_fusion.1
  74.9 1.0 all-to-all-done
  76.7 1.5 %fusion.3 = f32[400,200]{1,0:T(8,128)S(1)} fusion(f32[1024,401]{0,1:T(8,128)S(1)} %bitcast.48, f32[1024]{0:T(1024)S(1)} %bitcast.51), kind=kOutput, calls=%fused_computation.4 | convolution fusion | flops 983244800 | bytes 2781696 | tf_op jit(solution)/shard_map/dot_general | solution.py:116
  78.7 5.5 %custom-call.11 = f32[1,72,72]{1,2,0:T(8,128)S(1)} custom-call(f32[1,72,72]{2,1,0:T(8,128)S(1)} %select_bitcast_fusion), custom_call_target="InvertDiagBlocksLowerTriangular" | custom-call | tf_op jit(solution)/shard_map/triangular_solve | solution.py:11
  86.7 1.6 %collective-permute-start.7 = (f32[100,200]{1,0:T(8,128)S(1)}, f32[100,200]{1,0:T(8,128)S(1)}, u32[]{:S(2)}, u32[]{:S(2)}) collective-permute-start(f32[100,200]{1,0:T(8,128)S(1)} %slice_select_fusion), channel_id=1, source_target_pairs={{0,16},{8,24},{16,0},{24,8},{1,17},{9,25},{17,1},{25,9},{2,18},{10... | collective-permute-start | bytes 240008 | tf_op jit(solution)/shard_map/ppermute | solution.py:53
  88.5 3.0 %collective-permute-done.7 = f32[100,200]{1,0:T(8,128)S(1)} collective-permute-done((f32[100,200]{1,0:T(8,128)S(1)}, f32[100,200]{1,0:T(8,128)S(1)}, u32[]{:S(2)}, u32[]{:S(2)}) %collective-permute-start.7) | collective-permute-done | bytes 80032 | tf_op jit(solution)/shard_map/ppermute | solution.py:53
  91.5 1.6 %collective-permute-start.8 = (f32[50,200]{1,0:T(8,128)S(1)}, f32[50,200]{1,0:T(8,128)S(1)}, u32[]{:S(2)}, u32[]{:S(2)}) collective-permute-start(f32[50,200]{1,0:T(8,128)S(1)} %slice_select_fusion.2), channel_id=1, source_target_pairs={{0,8},{8,0},{16,24},{24,16},{1,9},{9,1},{17,25},{25,17},{2,10},{10... | collective-permute-start | bytes 120008 | tf_op jit(solution)/shard_map/ppermute | solution.py:53
  93.1 2.7 %collective-permute-done.8 = f32[50,200]{1,0:T(8,128)S(1)} collective-permute-done((f32[50,200]{1,0:T(8,128)S(1)}, f32[50,200]{1,0:T(8,128)S(1)}, u32[]{:S(2)}, u32[]{:S(2)}) %collective-permute-start.8) | collective-permute-done | bytes 40032 | tf_op jit(solution)/shard_map/ppermute | solution.py:53
  95.8 2.6 %fusion.8 = f32[3,50,1024]{2,1,0:T(8,128)} fusion(f32[3,200,1024]{2,1,0:T(8,128)S(1)} %copy-done, f32[3,1024]{1,0:T(4,128)S(1)} %broadcast_multiply_fusion, s32[]{:T(128)S(6)} %select_n.111, f32[50,200]{1,0:T(8,128)S(1)} %collective-permute-done.8, f32[100,200]{1,0:T(8,128)S(1)} %select_add_fusion, pred[]{:T(512)S(6)} %eq.24), kind=kOutput, calls=%fused_computation.7 | convolution fusion | flops 370042400 | bytes 3948549 | tf_op jit(solution)/shard_map/vnc,mn->vmc/dot_general | solution.py:138
  (49 shorter events, 7.4 us)
Async XLA Ops:
  3.9 1.6 %collective-permute-start = (f32[200,200]{0,1:T(8,128)S(1)}, f32[200,200]{0,1:T(8,128)S(1)}, u32[]{:S(2)}, u32[]{:S(2)}) collective-permute-start(f32[200,200]{0,1:T(8,128)S(1)} %fusion.23), channel_id=1, source_target_pairs={{0,1},{1,0},{2,3},{3,2},{4,5},{5,4},{6,7},{7,6},{8,9},{9,8},{10,11... | collective-permute-start | bytes 480008 | tf_op jit(solution)/shard_map/ppermute | solution.py:53
  6.9 6.1 %collective-permute-start.1 = (f32[100,200]{0,1:T(8,128)S(1)}, f32[100,200]{0,1:T(8,128)S(1)}, u32[]{:S(2)}, u32[]{:S(2)}) collective-permute-start(f32[100,200]{0,1:T(8,128)S(1)} %slice_select_fusion.1), channel_id=1, source_target_pairs={{0,8},{8,0},{16,24},{24,16},{1,9},{9,1},{17,25},{25,17},{2,10},{10... | collective-permute-start | bytes 240008 | tf_op jit(solution)/shard_map/ppermute | solution.py:53
  13.1 4.7 %collective-permute-start.2 = (f32[100,200]{0,1:T(8,128)S(1)}, f32[100,200]{0,1:T(8,128)S(1)}, u32[]{:S(2)}, u32[]{:S(2)}) collective-permute-start(f32[100,200]{0,1:T(8,128)S(1)} %select_add_fusion.1), channel_id=1, source_target_pairs={{0,16},{8,24},{16,0},{24,8},{1,17},{9,25},{17,1},{25,9},{2,18},{10... | collective-permute-start | bytes 240008 | tf_op jit(solution)/shard_map/ppermute | solution.py:53
  17.9 4.7 %collective-permute-start.3 = (f32[100,200]{0,1:T(8,128)S(1)}, f32[100,200]{0,1:T(8,128)S(1)}, u32[]{:S(2)}, u32[]{:S(2)}) collective-permute-start(f32[100,200]{0,1:T(8,128)S(1)} %add.67), channel_id=1, source_target_pairs={{0,2},{1,3},{2,0},{3,1},{4,6},{5,7},{6,4},{7,5},{8,10},{9,11},{10,... | collective-permute-start | bytes 240008 | tf_op jit(solution)/shard_map/ppermute | solution.py:53
  22.6 7.1 %collective-permute-start.4 = (f32[100,200]{0,1:T(8,128)S(1)}, f32[100,200]{0,1:T(8,128)S(1)}, u32[]{:S(2)}, u32[]{:S(2)}) collective-permute-start(f32[100,200]{0,1:T(8,128)S(1)} %add.68), channel_id=1, source_target_pairs={{0,4},{1,5},{2,6},{3,7},{4,0},{5,1},{6,2},{7,3},{8,12},{9,13},{10,... | collective-permute-start | bytes 240008 | tf_op jit(solution)/shard_map/ppermute | solution.py:53
  31.1 10.4 %copy-start.1 = (s32[1,8]{1,0:T(1,128)S(1)}, s32[1,8]{1,0:T(1,128)}, u32[]{:S(2)}) copy-start(s32[1,8]{1,0:T(1,128)} %param.11) | copy-start | bytes 100
  31.1 10.4 %copy-start.2 = (s32[1,8]{1,0:T(1,128)S(1)}, s32[1,8]{1,0:T(1,128)}, u32[]{:S(2)}) copy-start(s32[1,8]{1,0:T(1,128)} %param.10) | copy-start | bytes 100
  31.1 44.8 %all-to-all-start = ((f32[8,128,401]{1,2,0:T(8,128)}), f32[8,128,401]{1,2,0:T(8,128)S(1)}, u32[]{:S(2)}, u32[]{:S(2)}) async-start(f32[8,128,401]{1,2,0:T(8,128)} %broadcast_in_dim.7), calls=%async_computation | async-start | bytes 3342336 | tf_op jit(solution)/shard_map/all_to_all | solution.py:106
  35.9 5.3 %collective-permute-start.5 = (f32[100,200]{0,1:T(8,128)S(1)}, f32[100,200]{0,1:T(8,128)S(1)}, u32[]{:S(2)}, u32[]{:S(2)}) collective-permute-start(f32[100,200]{0,1:T(8,128)S(1)} %add.69), channel_id=1, source_target_pairs={{0,8},{8,0},{16,24},{24,16},{1,9},{9,1},{17,25},{25,17},{2,10},{10... | collective-permute-start | bytes 240008 | tf_op jit(solution)/shard_map/ppermute | solution.py:53
  41.4 1.5 %collective-permute-start.6 = (f32[200,200]{0,1:T(8,128)S(1)}, f32[200,200]{0,1:T(8,128)S(1)}, u32[]{:S(2)}, u32[]{:S(2)}) collective-permute-start(f32[200,200]{0,1:T(8,128)S(1)} %maximum_select_fusion.1), channel_id=1, source_target_pairs={{0,1},{1,0},{2,3},{3,2},{4,5},{5,4},{6,7},{7,6},{8,9},{9,8},{10,11... | collective-permute-start | bytes 480008 | tf_op jit(solution)/shard_map/ppermute | solution.py:53
  78.3 10.0 %copy-start = (f32[3,200,1024]{2,1,0:T(8,128)S(1)}, f32[3,200,1024]{2,1,0:T(8,128)}, u32[]{:S(2)}) copy-start(f32[3,200,1024]{2,1,0:T(8,128)} %param.6) | copy-start | bytes 7372804
  86.7 4.8 %collective-permute-start.7 = (f32[100,200]{1,0:T(8,128)S(1)}, f32[100,200]{1,0:T(8,128)S(1)}, u32[]{:S(2)}, u32[]{:S(2)}) collective-permute-start(f32[100,200]{1,0:T(8,128)S(1)} %slice_select_fusion), channel_id=1, source_target_pairs={{0,16},{8,24},{16,0},{24,8},{1,17},{9,25},{17,1},{25,9},{2,18},{10... | collective-permute-start | bytes 240008 | tf_op jit(solution)/shard_map/ppermute | solution.py:53
  91.5 4.2 %collective-permute-start.8 = (f32[50,200]{1,0:T(8,128)S(1)}, f32[50,200]{1,0:T(8,128)S(1)}, u32[]{:S(2)}, u32[]{:S(2)}) collective-permute-start(f32[50,200]{1,0:T(8,128)S(1)} %slice_select_fusion.2), channel_id=1, source_target_pairs={{0,8},{8,0},{16,24},{24,16},{1,9},{9,1},{17,25},{25,17},{2,10},{10... | collective-permute-start | bytes 120008 | tf_op jit(solution)/shard_map/ppermute | solution.py:53

commit v14 on v10

--- a/solution.py
+++ b/solution.py
@@ -79,6 +79,15 @@
     return x, tie
 
 
+def well_step(full, split, axis, k):
+    half = split.shape[0] // 2
+    hi = bit_of(axis, k) == 1
+    keep = jnp.where(hi, split[half:], split[:half])
+    send = jnp.where(hi, split[:half], split[half:])
+    got = swap(jnp.concatenate([full, send], 0), axis, k)
+    return full + got[: full.shape[0]], keep + got[full.shape[0]:]
+
+
 def shards(prior_state, pred_data, obs_pert, obs_std, loc_mask, taper_level):
     highest = lax.Precision.HIGHEST
     members = pred_data.shape[1]
@@ -121,15 +130,15 @@
     taper_gram, taper_cross_t = both[:members], both[members:]
 
     head, taper_gram, taper_cross_t = lax.optimization_barrier((head, taper_gram, taper_cross_t))
+    for axis, k in reversed(axis_bits("well")):
+        taper_gram, taper_cross_t = well_step(taper_gram, taper_cross_t, axis, k)
     inv11, l21, l22 = head
     factor = (inv11, l21, lower_inverse(l22, highest))
     solved = backward(factor, *forward(factor, cross_matrix, highest), highest)
+    solved_mine = lax.dynamic_slice_in_dim(solved, own_start, own_count, 1)
     space_t = taper_cross_t - lax.dot_general(
-        solved, taper_gram, (((0,), (1,)), ((), ())), precision=highest
+        solved_mine, taper_gram, (((0,), (1,)), ((), ())), precision=highest
     )
-    wells = lax.axis_size("well")
-    blocks = space_t.reshape((wells, space_t.shape[0] // wells, space_t.shape[1]))
-    space_t = jnp.sum(lax.all_to_all(blocks, "well", 0, 0, tiled=False), axis=0)
     state_anom = (prior_state - jnp.mean(prior_state, axis=1, keepdims=True)) * norm_factor
     increment = jnp.einsum("vnc,mn->vmc", state_anom, space_t, precision=highest)
     prior_mine = lax.dynamic_slice_in_dim(prior_state, own_start, own_count, 1)

time: 104 us -> 111 us (1.067)
  waiting for transfers between devices: 25 us -> 31.1 us
  other arithmetic: 41.9 us -> 44.6 us
    ppermute x7 -> x9, waiting for transfers between devices: 18.7 us -> 30.2 us  [swap(): return lax.ppermute(x, axis, [(i, i ^ k) for i in range(size)])]
    all_to_all x1 -> x0, waiting for transfers between devices: 5.28 us -> none  [shards(): space_t = jnp.sum(lax.all_to_all(blocks, 'well', 0, 0, tiled=False), axis=0)]
    all_to_all x1 -> x0, starting transfers between devices: 3.71 us -> none  [shards(): space_t = jnp.sum(lax.all_to_all(blocks, 'well', 0, 0, tiled=False), axis=0)]
    ppermute x7 -> x9, starting transfers between devices: 12.2 us -> 15.3 us  [swap(): return lax.ppermute(x, axis, [(i, i ^ k) for i in range(size)])]
    add x0 -> x2, other arithmetic: none -> 1.88 us  [well_step(): return (full + got[:full.shape[0]], keep + got[full.shape[0]:])]
  transfers between devices with their start and end apart: 9 -> 10, of which waited for: 9 -> 10; matrix products, arithmetic and copies ran while one was open for 31% -> 31% of each run, Pallas kernels for 0% -> 0%
where the time goes in v14:
time: 111 us
  other arithmetic  44.6 us (40%)
  waiting for transfers between devices  31.1 us (28%)
  starting transfers between devices  20.1 us (18%)
  matrix products  10.8 us (10%)
  local copies, waits for them, and re-layouts  3.84 us (3%)
    ppermute x9, waiting for transfers between devices, swap(): return lax.ppermute(x, axis, [(i, i ^ k) for i in range(size)])  30.2 us
    another operation x4, other arithmetic, lower_inverse(): lax.linalg.triangular_solve(factor, eye, left_side=True, lower=True, tran...  18.1 us
    ppermute x9, starting transfers between devices, swap(): return lax.ppermute(x, axis, [(i, i ^ k) for i in range(size)])  15.3 us
    another operation x3, other arithmetic, block_cholesky(): l11 = lax.linalg.cholesky(a11, symmetrize_input=False)  12.4 us
    another operation x3, other arithmetic, block_cholesky(): lax.linalg.cholesky(a22 - jnp.dot(l21, l21.T, precision=precision), symme...  7.25 us
    all_to_all x1, starting transfers between devices, shards(): lax.all_to_all(copies, 'tile', 0, 0, tiled=False)  4.87 us
    dot_general x1, matrix products, shards(): jnp.einsum('vnc,mn->vmc', state_anom, space_t, precision=highest)  2.66 us
  transfers between devices with their start and end apart: 10, of which 10 were waited for; matrix products, arithmetic and copies ran while one was open for 31% of the time, Pallas kernels for 0%

profile of v14, /device:TPU:0, one launch (start us, length us, event | category | flops | bytes accessed | tf_op | source)
XLA Modules:
  0.0 110.7 jit_solution(17381340260186694908)
XLA Ops:
  0.0 0.9 reduce_sum.18
  1.6 1.0 subtract_multiply_fusion
  2.6 1.2 %fusion.23 = f32[200,200]{0,1:T(8,128)S(1)} fusion(f32[128,200]{0,1:T(8,128)S(1)} %get-tuple-element.32, f32[128,200]{0,1:T(8,128)} %param.7, f32[128]{0:T(128)S(1)} %get-tuple-element.27, f32[128]{0:T(128)S(1)} %get-tuple-element.35), kind=kOutput, calls=%fused_computation.41 | convolution fusion | flops 61491200 | bytes 365824 | tf_op jit(solution)/shard_map/dot_general | solution.py:100
  3.8 1.3 %broadcast_select_fusion = (f32[200,200]{0,1:T(8,128)S(1)}, f32[200,200]{0,1:T(8,128)S(1)}) fusion(f32[200,200]{0,1:T(8,128)S(1)} %fusion.23, pred[]{:T(512)S(6)} %eq.27, f32[128,200]{0,1:T(8,128)} %param.7, f32[128]{0:T(128)S(1)} %get-tuple-element.27, f32[128]{0:T(128)S(1)} %get-tuple-element.35), kind=kOutput, calls=%fused_computation.36 | convolution fusion | flops 61582400 | bytes 583425 | tf_op jit(solution)/shard_map/dot_general | solution.py:99
  5.7 1.1 collective-permute-done
  6.9 2.9 %collective-permute-start.1 = (f32[100,200]{0,1:T(8,128)S(1)}, f32[100,200]{0,1:T(8,128)S(1)}, u32[]{:S(2)}, u32[]{:S(2)}) collective-permute-start(f32[100,200]{0,1:T(8,128)S(1)} %slice_select_fusion.1), channel_id=1, source_target_pairs={{0,8},{8,0},{16,24},{24,16},{1,9},{9,1},{17,25},{25,17},{2,10},{10... | collective-permute-start | bytes 240008 | tf_op jit(solution)/shard_map/ppermute | solution.py:53
  9.8 3.2 %collective-permute-done.1 = f32[100,200]{0,1:T(8,128)S(1)} collective-permute-done((f32[100,200]{0,1:T(8,128)S(1)}, f32[100,200]{0,1:T(8,128)S(1)}, u32[]{:S(2)}, u32[]{:S(2)}) %collective-permute-start.1) | collective-permute-done | bytes 80032 | tf_op jit(solution)/shard_map/ppermute | solution.py:53
  13.1 1.8 %collective-permute-start.2 = (f32[100,200]{0,1:T(8,128)S(1)}, f32[100,200]{0,1:T(8,128)S(1)}, u32[]{:S(2)}, u32[]{:S(2)}) collective-permute-start(f32[100,200]{0,1:T(8,128)S(1)} %select_add_fusion.1), channel_id=1, source_target_pairs={{0,16},{8,24},{16,0},{24,8},{1,17},{9,25},{17,1},{25,9},{2,18},{10... | collective-permute-start | bytes 240008 | tf_op jit(solution)/shard_map/ppermute | solution.py:53
  14.9 2.9 %collective-permute-done.2 = f32[100,200]{0,1:T(8,128)S(1)} collective-permute-done((f32[100,200]{0,1:T(8,128)S(1)}, f32[100,200]{0,1:T(8,128)S(1)}, u32[]{:S(2)}, u32[]{:S(2)}) %collective-permute-start.2) | collective-permute-done | bytes 80032 | tf_op jit(solution)/shard_map/ppermute | solution.py:53
  17.8 1.9 %collective-permute-start.3 = (f32[100,200]{0,1:T(8,128)S(1)}, f32[100,200]{0,1:T(8,128)S(1)}, u32[]{:S(2)}, u32[]{:S(2)}) collective-permute-start(f32[100,200]{0,1:T(8,128)S(1)} %add.74), channel_id=1, source_target_pairs={{0,2},{1,3},{2,0},{3,1},{4,6},{5,7},{6,4},{7,5},{8,10},{9,11},{10,... | collective-permute-start | bytes 240008 | tf_op jit(solution)/shard_map/ppermute | solution.py:53
  19.7 2.8 %collective-permute-done.3 = f32[100,200]{0,1:T(8,128)S(1)} collective-permute-done((f32[100,200]{0,1:T(8,128)S(1)}, f32[100,200]{0,1:T(8,128)S(1)}, u32[]{:S(2)}, u32[]{:S(2)}) %collective-permute-start.3) | collective-permute-done | bytes 80032 | tf_op jit(solution)/shard_map/ppermute | solution.py:53
  22.6 3.4 %collective-permute-start.4 = (f32[100,200]{0,1:T(8,128)S(1)}, f32[100,200]{0,1:T(8,128)S(1)}, u32[]{:S(2)}, u32[]{:S(2)}) collective-permute-start(f32[100,200]{0,1:T(8,128)S(1)} %add.75), channel_id=1, source_target_pairs={{0,4},{1,5},{2,6},{3,7},{4,0},{5,1},{6,2},{7,3},{8,12},{9,13},{10,... | collective-permute-start | bytes 240008 | tf_op jit(solution)/shard_map/ppermute | solution.py:53
  26.0 3.7 %collective-permute-done.4 = f32[100,200]{0,1:T(8,128)S(1)} collective-permute-done((f32[100,200]{0,1:T(8,128)S(1)}, f32[100,200]{0,1:T(8,128)S(1)}, u32[]{:S(2)}, u32[]{:S(2)}) %collective-permute-start.4) | collective-permute-done | bytes 80032 | tf_op jit(solution)/shard_map/ppermute | solution.py:53
  29.7 1.3 %broadcast_in_dim.7 = f32[8,128,401]{1,2,0:T(8,128)} broadcast(f32[128,401]{0,1:T(8,128)S(1)} %pad_maximum_fusion.2), dimensions={1,2} | broadcast | bytes 1847808 | tf_op jit(solution)/shard_map/broadcast_in_dim | solution.py:113
  31.0 4.9 %all-to-all-start = ((f32[8,128,401]{1,2,0:T(8,128)}), f32[8,128,401]{1,2,0:T(8,128)}, u32[]{:S(2)}, u32[]{:S(2)}) async-start(f32[8,128,401]{1,2,0:T(8,128)} %broadcast_in_dim.7), calls=%async_computation | async-start | bytes 3342336 | tf_op jit(solution)/shard_map/all_to_all | solution.py:114
  36.1 1.6 %collective-permute-start.5 = (f32[100,200]{0,1:T(8,128)S(1)}, f32[100,200]{0,1:T(8,128)S(1)}, u32[]{:S(2)}, u32[]{:S(2)}) collective-permute-start(f32[100,200]{0,1:T(8,128)S(1)} %add.76), channel_id=1, source_target_pairs={{0,8},{8,0},{16,24},{24,16},{1,9},{9,1},{17,25},{25,17},{2,10},{10... | collective-permute-start | bytes 240008 | tf_op jit(solution)/shard_map/ppermute | solution.py:53
  37.6 3.8 %collective-permute-done.5 = f32[100,200]{0,1:T(8,128)S(1)} collective-permute-done((f32[100,200]{0,1:T(8,128)S(1)}, f32[100,200]{0,1:T(8,128)S(1)}, u32[]{:S(2)}, u32[]{:S(2)}) %collective-permute-start.5) | collective-permute-done | bytes 80032 | tf_op jit(solution)/shard_map/ppermute | solution.py:53
  41.7 1.4 %collective-permute-done.6 = f32[200,200]{0,1:T(8,128)S(1)} collective-permute-done((f32[200,200]{0,1:T(8,128)S(1)}, f32[200,200]{0,1:T(8,128)S(1)}, u32[]{:S(2)}, u32[]{:S(2)}) %collective-permute-start.6) | collective-permute-done | bytes 160032 | tf_op jit(solution)/shard_map/ppermute | solution.py:53
  43.5 11.7 %cholesky.37 = f32[128,128]{1,0:T(8,128)S(1)} custom-call(f32[128,128]{1,0:T(8,128)S(1)} %cholesky.82), custom_call_target="Cholesky" | custom-call | tf_op jit(solution)/shard_map/cholesky | solution.py:17
  56.6 9.8 %custom-call.10 = f32[1,128,128]{1,2,0:T(8,128)S(1)} custom-call(f32[1,128,128]{2,1,0:T(8,128)S(1)} %fusion.27), custom_call_target="InvertDiagBlocksLowerTriangular" | custom-call | tf_op jit(solution)/shard_map/triangular_solve | solution.py:11
  67.2 6.6 %cholesky.73 = f32[72,72]{1,0:T(8,128)S(1)} custom-call(f32[72,72]{1,0:T(8,128)S(1)} %convolution_subtract_fusion.1), custom_call_target="Cholesky" | custom-call | tf_op jit(solution)/shard_map/cholesky | solution.py:20
  75.9 1.8 %copy.17 = f32[8,128,401]{1,0,2:T(8,128)S(1)} copy(f32[8,128,401]{1,2,0:T(8,128)} %all-to-all-done) | data formatting | bytes 3284992 | tf_op jit(solution)/shard_map/all_to_all | solution.py:114
  78.3 1.5 %fusion.3 = f32[400,200]{1,0:T(8,128)S(1)} fusion(f32[1024,401]{0,1:T(8,128)S(1)} %bitcast.48, f32[1024]{0:T(1024)S(1)} %bitcast.51), kind=kOutput, calls=%fused_computation.4 | convolution fusion | flops 983244800 | bytes 2781696 | tf_op jit(solution)/shard_map/dot_general | solution.py:124
  80.8 7.0 %custom-call.11 = f32[1,72,72]{1,2,0:T(8,128)} custom-call(f32[1,72,72]{2,1,0:T(8,128)} %select_bitcast_fusion), custom_call_target="InvertDiagBlocksLowerTriangular" | custom-call | tf_op jit(solution)/shard_map/triangular_solve | solution.py:11
  87.8 1.0 fusion.44
  89.6 1.5 %collective-permute-start.7 = (f32[300,200]{1,0:T(8,128)}, f32[300,200]{1,0:T(8,128)}, u32[]{:S(2)}, u32[]{:S(2)}) collective-permute-start(f32[300,200]{1,0:T(8,128)} %pad_maximum_fusion), channel_id=1, source_target_pairs={{0,16},{8,24},{16,0},{24,8},{1,17},{9,25},{17,1},{25,9},{2,18},{10... | collective-permute-start | bytes 720008 | tf_op jit(solution)/shard_map/ppermute | solution.py:53
  92.6 6.2 %collective-permute-done.7 = f32[300,200]{1,0:T(8,128)} collective-permute-done((f32[300,200]{1,0:T(8,128)}, f32[300,200]{1,0:T(8,128)}, u32[]{:S(2)}, u32[]{:S(2)}) %collective-permute-start.7) | collective-permute-done | bytes 240032 | tf_op jit(solution)/shard_map/ppermute | solution.py:53
  98.8 0.9 slice_add_fusion.4
  99.7 1.0 slice_add_fusion.2
  100.7 1.6 %collective-permute-start.8 = (f32[250,200]{1,0:T(8,128)S(1)}, f32[250,200]{1,0:T(8,128)S(1)}, u32[]{:S(2)}, u32[]{:S(2)}) collective-permute-start(f32[250,200]{1,0:T(8,128)S(1)} %pad_maximum_fusion.1), channel_id=1, source_target_pairs={{0,8},{8,0},{16,24},{24,16},{1,9},{9,1},{17,25},{25,17},{2,10},{10... | collective-permute-start | bytes 600008 | tf_op jit(solution)/shard_map/ppermute | solution.py:53
  102.6 5.1 %collective-permute-done.8 = f32[250,200]{1,0:T(8,128)S(1)} collective-permute-done((f32[250,200]{1,0:T(8,128)S(1)}, f32[250,200]{1,0:T(8,128)S(1)}, u32[]{:S(2)}, u32[]{:S(2)}) %collective-permute-start.8) | collective-permute-done | bytes 200032 | tf_op jit(solution)/shard_map/ppermute | solution.py:53
  108.1 2.7 %fusion.8 = f32[3,50,1024]{2,1,0:T(8,128)} fusion(f32[3,200,1024]{2,1,0:T(8,128)S(1)} %copy-done, f32[3,1024]{1,0:T(4,128)S(1)} %broadcast_multiply_fusion, s32[]{:T(128)S(6)} %select_n.100, f32[50,200]{1,0:T(8,128)S(1)} %fusion.16, f32[250,200]{1,0:T(8,128)S(1)} %collective-permute-done.8, f32[100,200]{1,0:T(8,128)S(1)} %slice_add_fusion.4, pred[]{:T(512)S(6)} %eq.24), kind=kOutput, calls=%fused_computation.7 | convolution fusion | flops 370052416 | bytes 4005893 | tf_op jit(solution)/shard_map/vnc,mn->vmc/dot_general | solution.py:143
  (53 shorter events, 11.0 us)
Async XLA Ops:
  5.2 1.6 %collective-permute-start = (f32[200,200]{0,1:T(8,128)S(1)}, f32[200,200]{0,1:T(8,128)S(1)}, u32[]{:S(2)}, u32[]{:S(2)}) collective-permute-start(f32[200,200]{0,1:T(8,128)S(1)} %get-tuple-element.33), channel_id=1, source_target_pairs={{0,1},{1,0},{2,3},{3,2},{4,5},{5,4},{6,7},{7,6},{8,9},{9,8},{10,11... | collective-permute-start | bytes 480008 | tf_op jit(solution)/shard_map/ppermute | solution.py:53
  6.9 6.1 %collective-permute-start.1 = (f32[100,200]{0,1:T(8,128)S(1)}, f32[100,200]{0,1:T(8,128)S(1)}, u32[]{:S(2)}, u32[]{:S(2)}) collective-permute-start(f32[100,200]{0,1:T(8,128)S(1)} %slice_select_fusion.1), channel_id=1, source_target_pairs={{0,8},{8,0},{16,24},{24,16},{1,9},{9,1},{17,25},{25,17},{2,10},{10... | collective-permute-start | bytes 240008 | tf_op jit(solution)/shard_map/ppermute | solution.py:53
  13.1 4.7 %collective-permute-start.2 = (f32[100,200]{0,1:T(8,128)S(1)}, f32[100,200]{0,1:T(8,128)S(1)}, u32[]{:S(2)}, u32[]{:S(2)}) collective-permute-start(f32[100,200]{0,1:T(8,128)S(1)} %select_add_fusion.1), channel_id=1, source_target_pairs={{0,16},{8,24},{16,0},{24,8},{1,17},{9,25},{17,1},{25,9},{2,18},{10... | collective-permute-start | bytes 240008 | tf_op jit(solution)/shard_map/ppermute | solution.py:53
  17.8 4.7 %collective-permute-start.3 = (f32[100,200]{0,1:T(8,128)S(1)}, f32[100,200]{0,1:T(8,128)S(1)}, u32[]{:S(2)}, u32[]{:S(2)}) collective-permute-start(f32[100,200]{0,1:T(8,128)S(1)} %add.74), channel_id=1, source_target_pairs={{0,2},{1,3},{2,0},{3,1},{4,6},{5,7},{6,4},{7,5},{8,10},{9,11},{10,... | collective-permute-start | bytes 240008 | tf_op jit(solution)/shard_map/ppermute | solution.py:53
  22.6 7.1 %collective-permute-start.4 = (f32[100,200]{0,1:T(8,128)S(1)}, f32[100,200]{0,1:T(8,128)S(1)}, u32[]{:S(2)}, u32[]{:S(2)}) collective-permute-start(f32[100,200]{0,1:T(8,128)S(1)} %add.75), channel_id=1, source_target_pairs={{0,4},{1,5},{2,6},{3,7},{4,0},{5,1},{6,2},{7,3},{8,12},{9,13},{10,... | collective-permute-start | bytes 240008 | tf_op jit(solution)/shard_map/ppermute | solution.py:53
  31.0 4.9 %copy-start = (f32[3,200,1024]{2,1,0:T(8,128)S(1)}, f32[3,200,1024]{2,1,0:T(8,128)}, u32[]{:S(2)}) copy-start(f32[3,200,1024]{2,1,0:T(8,128)} %param.6) | copy-start | bytes 7372804
  31.0 44.9 %all-to-all-start = ((f32[8,128,401]{1,2,0:T(8,128)}), f32[8,128,401]{1,2,0:T(8,128)}, u32[]{:S(2)}, u32[]{:S(2)}) async-start(f32[8,128,401]{1,2,0:T(8,128)} %broadcast_in_dim.7), calls=%async_computation | async-start | bytes 3342336 | tf_op jit(solution)/shard_map/all_to_all | solution.py:114
  35.9 5.8 %copy-start.1 = (s32[1,8]{1,0:T(1,128)S(1)}, s32[1,8]{1,0:T(1,128)}, u32[]{:S(2)}) copy-start(s32[1,8]{1,0:T(1,128)} %param.11) | copy-start | bytes 100
  35.9 5.8 %copy-start.2 = (s32[1,8]{1,0:T(1,128)S(1)}, s32[1,8]{1,0:T(1,128)}, u32[]{:S(2)}) copy-start(s32[1,8]{1,0:T(1,128)} %param.10) | copy-start | bytes 100
  36.1 5.3 %collective-permute-start.5 = (f32[100,200]{0,1:T(8,128)S(1)}, f32[100,200]{0,1:T(8,128)S(1)}, u32[]{:S(2)}, u32[]{:S(2)}) collective-permute-start(f32[100,200]{0,1:T(8,128)S(1)} %add.76), channel_id=1, source_target_pairs={{0,8},{8,0},{16,24},{24,16},{1,9},{9,1},{17,25},{25,17},{2,10},{10... | collective-permute-start | bytes 240008 | tf_op jit(solution)/shard_map/ppermute | solution.py:53
  41.6 1.5 %collective-permute-start.6 = (f32[200,200]{0,1:T(8,128)S(1)}, f32[200,200]{0,1:T(8,128)S(1)}, u32[]{:S(2)}, u32[]{:S(2)}) collective-permute-start(f32[200,200]{0,1:T(8,128)S(1)} %maximum_select_fusion.1), channel_id=1, source_target_pairs={{0,1},{1,0},{2,3},{3,2},{4,5},{5,4},{6,7},{7,6},{8,9},{9,8},{10,11... | collective-permute-start | bytes 480008 | tf_op jit(solution)/shard_map/ppermute | solution.py:53
  89.6 9.2 %collective-permute-start.7 = (f32[300,200]{1,0:T(8,128)}, f32[300,200]{1,0:T(8,128)}, u32[]{:S(2)}, u32[]{:S(2)}) collective-permute-start(f32[300,200]{1,0:T(8,128)} %pad_maximum_fusion), channel_id=1, source_target_pairs={{0,16},{8,24},{16,0},{24,8},{1,17},{9,25},{17,1},{25,9},{2,18},{10... | collective-permute-start | bytes 720008 | tf_op jit(solution)/shard_map/ppermute | solution.py:53
  100.7 7.0 %collective-permute-start.8 = (f32[250,200]{1,0:T(8,128)S(1)}, f32[250,200]{1,0:T(8,128)S(1)}, u32[]{:S(2)}, u32[]{:S(2)}) collective-permute-start(f32[250,200]{1,0:T(8,128)S(1)} %pad_maximum_fusion.1), channel_id=1, source_target_pairs={{0,8},{8,0},{16,24},{24,16},{1,9},{9,1},{17,25},{25,17},{2,10},{10... | collective-permute-start | bytes 600008 | tf_op jit(solution)/shard_map/ppermute | solution.py:53
